TPU v7x, 128 devices: a whole 4x4x4 slice. The times are simulated.
128 devices in a mesh: grp: 8 (over x, core), mem: 16 (over z, y).
Axes of the slice: x: 4, y: 4, z: 4, core: 2. Of those that a mesh axis runs over, the one named last changes fastest.
Arguments:
- clips: bfloat16 [32768, 1152], P(('grp', 'mem')), may hold values from -6 to 6
- captions: bfloat16 [8192, 1152], P(('grp', 'mem')), may hold values from -6 to 6
- clip_bucket: int32 [32768], P(('grp', 'mem')), may hold values from 0 to 15, as said below
- clip_positive: int32 [32768], P(('grp', 'mem')), may hold values from 0 to 8191, as said below
- caption_bucket: int32 [8192], P(('grp', 'mem')), may hold values from 0 to 15, as said below
- bucket_owner: int32 [16], replicated, may hold values from 0 to 7, as said below
- scale: float32 [1], replicated, may hold values from 0.02 to 0.06
- bias: float32 [1], replicated, may hold values from -4 to -1
Outputs:
- clip_grad: float32 [32768, 1152], P(('grp', 'mem'))
- caption_grad: float32 [8192, 1152], P(('grp', 'mem'))
Inputs may be any that keep to these rules, and one draw needn't show every extreme that they name: `bucket_owner`: each group owns exactly 2 buckets. `caption_bucket`: caption rows g * 1024 to (g + 1) * 1024 - 1 have buckets owned by group g, and every bucket has a caption. `clip_bucket`: within one device's block of 256 clip rows, among the rows whose offsets in the block are equal modulo the size of axis mem, at most 4 have buckets owned by one group; one group receives exactly 4 such rows from every such set of every device. `clip_positive`: each clip's own caption has the clip's bucket.
All inputs are finite; a program needn't handle non-finite values.
Results may differ from a plain program's by a relative error of at most 0.0027.
Values may be sent and summed in bfloat16 or wider, within the bound.
No kernel may reach another device: no remote copies, remote signals or barrier semaphores. Data moves between devices by JAX's collectives and lax.ppermute only.
A program may use at most 128 MiB of HBM per device.

v0:
```python
import jax
import jax.numpy as jnp
from jax import lax
from jax.sharding import PartitionSpec as P


def pair_weights(logits, matched, same):
    sign = jnp.where(matched, 1.0, -1.0).astype(jnp.float32)
    return jnp.where(same, -sign * jax.nn.sigmoid(-sign * logits), 0.0).astype(jnp.bfloat16)


def inner_rows(left, right):
    return lax.dot_general(
        left, right, (((1,), (1,)), ((), ())), preferred_element_type=jnp.float32
    )


def inner_cols(left, right):
    return lax.dot_general(
        left, right, (((0,), (0,)), ((), ())), preferred_element_type=jnp.float32
    )


def shift_pairs(nz, ny, d, along_y):
    pairs = []
    for z in range(nz):
        for y in range(ny):
            if along_y:
                pairs.append((z * ny + y, z * ny + (y + d) % ny))
            else:
                pairs.append((z * ny + y, ((z + d) % nz) * ny + y))
    return pairs


def gather_first(xa, xb, nz, ny):
    parts_a = [xa]
    parts_b = [xb]
    for d in range(1, ny):
        parts_a.append(lax.ppermute(xa, "mem", shift_pairs(nz, ny, d, True)))
        parts_b.append(lax.ppermute(xb, "mem", shift_pairs(nz, ny, d, False)))
    return jnp.stack(parts_a), jnp.stack(parts_b)


def gather_second(inner_a, inner_b, nz, ny):
    parts_a = [inner_a]
    parts_b = [inner_b]
    for d in range(1, nz):
        parts_a.append(lax.ppermute(inner_a, "mem", shift_pairs(nz, ny, d, False)))
        parts_b.append(lax.ppermute(inner_b, "mem", shift_pairs(nz, ny, d, True)))
    return jnp.stack(parts_a), jnp.stack(parts_b)


def reduce_pair(blocks_a, blocks_b, nz, ny):
    low = jnp.bfloat16
    total_a = blocks_a[0]
    total_b = blocks_b[0]
    for d in range(1, nz):
        total_a = total_a + lax.ppermute(blocks_a[d].astype(low), "mem", shift_pairs(nz, ny, -d, False)).astype(jnp.float32)
        total_b = total_b + lax.ppermute(blocks_b[d].astype(low), "mem", shift_pairs(nz, ny, -d, True)).astype(jnp.float32)
    out_a = total_a[0]
    out_b = total_b[0]
    for d in range(1, ny):
        out_a = out_a + lax.ppermute(total_a[d].astype(low), "mem", shift_pairs(nz, ny, -d, True)).astype(jnp.float32)
        out_b = out_b + lax.ppermute(total_b[d].astype(low), "mem", shift_pairs(nz, ny, -d, False)).astype(jnp.float32)
    return out_a, out_b


def inner_body(clips, captions, clip_bucket, clip_positive, caption_bucket, bucket_owner, scale, bias):
    groups = lax.axis_size("grp")
    members = lax.axis_size("mem")
    ny = int(round(members ** 0.5))
    nz = members // ny
    clip_rows, width = clips.shape
    cap_rows = captions.shape[0]
    half = cap_rows // 2
    n_buckets = bucket_owner.shape[0]
    capacity = clip_rows // members * 4
    slots = capacity * groups
    panel = cap_rows * members
    mult = scale[0]
    shift = bias[0]
    group_index = lax.axis_index("grp")
    member = lax.axis_index("mem")
    my_z = member // ny
    my_y = member % ny
    tag = jnp.broadcast_to(caption_bucket.astype(captions.dtype)[:, None], (cap_rows, 128))
    own = jnp.concatenate([captions, tag], axis=1)
    inner_a, inner_b = gather_first(own[:half], own[half:], nz, ny)
    got_a, got_b = gather_second(inner_a, inner_b, nz, ny)
    bucket_hot = clip_bucket[:, None] == jnp.arange(n_buckets, dtype=jnp.int32)[None, :]
    owner = jnp.sum(jnp.where(bucket_hot, bucket_owner[None, :], 0), axis=1)
    onehot = (owner[:, None] == jnp.arange(groups, dtype=jnp.int32)[None, :]).astype(jnp.int32)
    before = jnp.cumsum(onehot, axis=0) - onehot
    rank = jnp.sum(before * onehot, axis=1)
    position = owner * capacity + rank
    meta = jnp.stack(
        [clip_bucket + 1, clip_positive // 128, clip_positive % 128], axis=1
    ).astype(clips.dtype)
    extra = jnp.concatenate([jnp.zeros((clip_rows, 1), clips.dtype), meta,
                             jnp.zeros((clip_rows, 124), clips.dtype)], axis=1)
    send_rows = jnp.zeros((slots, width + 128), clips.dtype).at[position].set(
        jnp.concatenate([clips, extra], axis=1))
    recv_ext = lax.all_to_all(send_rows, "grp", split_axis=0, concat_axis=0, tiled=True)
    recv_rows = recv_ext[:, :width]
    recv_meta = recv_ext[:, width + 1:width + 4].astype(jnp.int32)
    recv_bucket = recv_meta[:, 0] - 1
    recv_positive = jnp.where(recv_bucket >= 0, recv_meta[:, 1] * 128 + recv_meta[:, 2], -1)
    got_a = got_a.reshape(members * half, -1)
    got_b = got_b.reshape(members * half, -1)
    ar = jnp.arange(half, dtype=jnp.int32)
    za = jnp.arange(nz, dtype=jnp.int32)
    ya = jnp.arange(ny, dtype=jnp.int32)
    src_a = ((my_z - za[:, None]) % nz) * ny + (my_y - ya[None, :]) % ny
    src_b = ((my_z - za[None, :]) % nz) * ny + (my_y - ya[:, None]) % ny
    base = group_index * panel
    ids_a = (base + src_a[:, :, None] * cap_rows + ar[None, None, :]).reshape(-1)
    ids_b = (base + src_b[:, :, None] * cap_rows + half + ar[None, None, :]).reshape(-1)
    weights = []
    rows = []
    for got, ids in ((got_a, ids_a), (got_b, ids_b)):
        rows_y = got[:, :width]
        bucket_y = got[:, width].astype(jnp.int32)
        logits = mult * inner_rows(recv_rows, rows_y) + shift
        weights.append(pair_weights(
            logits, recv_positive[:, None] == ids[None, :], recv_bucket[:, None] == bucket_y[None, :]
        ))
        rows.append(rows_y)
    total = (jnp.dot(weights[0], rows[0], preferred_element_type=jnp.float32)
             + jnp.dot(weights[1], rows[1], preferred_element_type=jnp.float32))
    returned = lax.all_to_all(total.astype(jnp.bfloat16), "grp", split_axis=0, concat_axis=0, tiled=True)
    clip_grad = returned[position].astype(jnp.float32)
    weights, recv_rows, total = lax.optimization_barrier((weights, recv_rows, total))
    partial_a = inner_cols(weights[0], recv_rows).reshape(nz, ny, half, width)
    partial_b = inner_cols(weights[1], recv_rows).reshape(ny, nz, half, width)
    grad_a, grad_b = reduce_pair(partial_a, partial_b, nz, ny)
    caption_grad = jnp.concatenate([grad_a, grad_b], axis=0)
    return (clip_grad, caption_grad)


def solution(mesh):
    placed = (
        P(("grp", "mem"), None),
        P(("grp", "mem"), None),
        P(("grp", "mem")),
        P(("grp", "mem")),
        P(("grp", "mem")),
        P(),
        P(),
        P(),
    )
    return jax.shard_map(
        inner_body,
        mesh=mesh,
        in_specs=placed,
        out_specs=(P(("grp", "mem"), None), P(("grp", "mem"), None)),
        check_vma=False,
    )
```

profile of v0, /device:TPU:0, one launch (start us, length us, event | category | flops | bytes accessed | tf_op | source)
XLA Modules:
  0.0 106.3 jit_solution(15978610350735860909)
XLA Ops:
  0.6 0.7 convert_element_type.133
  1.4 1.0 pad_maximum_fusion.5
  2.4 3.4 %collective-permute-start.1 = (bf16[32,1280]{1,0:T(8,128)(2,1)S(1)}, bf16[32,1280]{1,0:T(8,128)(2,1)S(1)}, u32[]{:S(2)}, u32[]{:S(2)}) collective-permute-start(bf16[32,1280]{1,0:T(8,128)(2,1)S(1)} %get-tuple-element.32), channel_id=1, source_target_pairs={{0,2},{1,3},{2,0},{3,1},{4,6},{5,7},{6,4},{7,5},{8,10},{9,11},{10,... | collective-permute-start | bytes 245768 | tf_op jit(solution)/shard_map/ppermute | solution.py:39
  5.7 0.7 collective-permute-start
  6.4 2.6 %collective-permute-start.2 = (bf16[32,1280]{1,0:T(8,128)(2,1)S(1)}, bf16[32,1280]{1,0:T(8,128)(2,1)S(1)}, u32[]{:S(2)}, u32[]{:S(2)}) collective-permute-start(bf16[32,1280]{1,0:T(8,128)(2,1)S(1)} %get-tuple-element.32), channel_id=1, source_target_pairs={{0,3},{1,0},{2,1},{3,2},{4,7},{5,4},{6,5},{7,6},{8,11},{9,8},{10,9... | collective-permute-start | bytes 245768 | tf_op jit(solution)/shard_map/ppermute | solution.py:39
  9.0 3.9 %collective-permute-start.7 = (bf16[32,1280]{1,0:T(8,128)(2,1)S(1)}, bf16[32,1280]{1,0:T(8,128)(2,1)S(1)}, u32[]{:S(2)}, u32[]{:S(2)}) collective-permute-start(bf16[32,1280]{1,0:T(8,128)(2,1)S(1)} %get-tuple-element.30), channel_id=1, source_target_pairs={{0,8},{1,9},{2,10},{3,11},{4,12},{5,13},{6,14},{7,15},{8,0},{9,1},... | collective-permute-start | bytes 245768 | tf_op jit(solution)/shard_map/ppermute | solution.py:40
  12.9 1.0 collective-permute-start.6
  13.9 0.7 add_convert_fusion
  14.6 0.8 select_reduce_fusion
  15.3 0.7 fusion.38
  16.0 0.6 reduce-window.6
  16.6 0.2 slice_reduce_fusion
  17.3 1.2 %concatenate.10 = bf16[256,1280]{1,0:T(8,128)(2,1)S(1)} concatenate(bf16[256,1152]{1,0:T(8,128)(2,1)} %param.8, bf16[256,1]{1,0:T(8,128)(2,1)S(1)} %broadcast_in_dim.40, bf16[256,1]{1,0:T(8,128)(2,1)S(1)} %stack.97, bf16[256,1]{1,0:T(8,128)(2,1)S(1)} %stack.98, bf16[256,1]{1,0:T(8,128)(2,1)S(1)} %stack.99, bf16[256,124]{1,0:T(8,128)(2,1)S(1)} %broadcast_in_dim.41), dimensions={1} | concatenate | bytes 1310720 | tf_op jit(solution)/shard_map/concatenate | solution.py:102
  18.6 2.9 %scatter_custom_fusion = bf16[512,1280]{1,0:T(8,128)(2,1)} fusion(s32[256]{0:T(256)S(1)} %bitcast.120, bf16[256,1280]{1,0:T(8,128)(2,1)S(1)} %concatenate.10, bf16[]{:T(256)} %constant.100.clone.1), kind=kCustom, calls=%fused_computation.30 | custom fusion | bytes 1310722 | tf_op jit(solution)/shard_map/scatter | solution.py:101
  21.5 4.3 %all-to-all-start = ((bf16[8,64,1280]{2,1,0:T(8,128)(2,1)}), bf16[8,64,1280]{2,1,0:T(8,128)(2,1)S(1)}, u32[]{:S(2)}, u32[]{:S(2)}) async-start(bf16[8,64,1280]{2,1,0:T(8,128)(2,1)} %bitcast.5), calls=%async_computation | async-start | bytes 2621440 | tf_op jit(solution)/shard_map/all_to_all | solution.py:103
  27.5 2.2 %collective-permute-start.8 = (bf16[32,1280]{1,0:T(8,128)(2,1)S(1)}, bf16[32,1280]{1,0:T(8,128)(2,1)S(1)}, u32[]{:S(2)}, u32[]{:S(2)}) collective-permute-start(bf16[32,1280]{1,0:T(8,128)(2,1)S(1)} %get-tuple-element.30), channel_id=1, source_target_pairs={{0,12},{1,13},{2,14},{3,15},{4,0},{5,1},{6,2},{7,3},{8,4},{9,5},{1... | collective-permute-start | bytes 245768 | tf_op jit(solution)/shard_map/ppermute | solution.py:40
  29.9 0.9 collective-permute-start.3
  30.8 2.4 %collective-permute-start.5 = (bf16[4,32,1280]{2,1,0:T(8,128)(2,1)S(1)}, bf16[4,32,1280]{2,1,0:T(8,128)(2,1)S(1)}, u32[]{:S(2)}, u32[]{:S(2)}) collective-permute-start(bf16[4,32,1280]{2,1,0:T(8,128)(2,1)S(1)} %get-tuple-element.23), channel_id=1, source_target_pairs={{0,12},{1,13},{2,14},{3,15},{4,0},{5,1},{6,2},{7,3},{8,4},{9,5},{1... | collective-permute-start | bytes 983048 | tf_op jit(solution)/shard_map/ppermute | solution.py:48
  33.2 6.2 %collective-permute-done.8 = bf16[32,1280]{1,0:T(8,128)(2,1)S(1)} collective-permute-done((bf16[32,1280]{1,0:T(8,128)(2,1)S(1)}, bf16[32,1280]{1,0:T(8,128)(2,1)S(1)}, u32[]{:S(2)}, u32[]{:S(2)}) %collective-permute-start.8) | collective-permute-done | bytes 81952 | tf_op jit(solution)/shard_map/ppermute | solution.py:40
  39.6 0.8 collective-permute-start.9
  40.5 1.6 %collective-permute-done.4 = bf16[4,32,1280]{2,1,0:T(8,128)(2,1)S(1)} collective-permute-done((bf16[4,32,1280]{2,1,0:T(8,128)(2,1)S(1)}, bf16[4,32,1280]{2,1,0:T(8,128)(2,1)S(1)}, u32[]{:S(2)}, u32[]{:S(2)}) %collective-permute-start.4) | collective-permute-done | bytes 327712 | tf_op jit(solution)/shard_map/ppermute | solution.py:48
  42.0 0.9 collective-permute-start.11
  42.9 5.1 %collective-permute-done.3 = bf16[4,32,1280]{2,1,0:T(8,128)(2,1)S(1)} collective-permute-done((bf16[4,32,1280]{2,1,0:T(8,128)(2,1)S(1)}, bf16[4,32,1280]{2,1,0:T(8,128)(2,1)S(1)}, u32[]{:S(2)}, u32[]{:S(2)}) %collective-permute-start.3) | collective-permute-done | bytes 327712 | tf_op jit(solution)/shard_map/ppermute | solution.py:48
  48.1 0.2 pad_maximum_fusion
  48.2 1.1 %copy-done.4 = bf16[4,4,32,1280]{3,2,1,0:T(8,128)(2,1)} copy-done((bf16[4,4,32,1280]{3,2,1,0:T(8,128)(2,1)}, bf16[4,4,32,1280]{3,2,1,0:T(8,128)(2,1)S(1)}, u32[]{:S(2)}) %copy-start.4) | copy-done | bytes 1310744
  49.3 0.1 copy.28
  49.4 2.0 %collective-permute-done.9 = bf16[4,32,1280]{2,1,0:T(8,128)(2,1)S(1)} collective-permute-done((bf16[4,32,1280]{2,1,0:T(8,128)(2,1)S(1)}, bf16[4,32,1280]{2,1,0:T(8,128)(2,1)S(1)}, u32[]{:S(2)}, u32[]{:S(2)}) %collective-permute-start.9) | collective-permute-done | bytes 327712 | tf_op jit(solution)/shard_map/ppermute | solution.py:49
  51.5 1.1 collective-permute-done.11
  52.5 0.2 pad_maximum_fusion.1
  52.7 1.0 copy-done
  53.9 1.1 %copy-done.2 = bf16[8,64,1280]{2,1,0:T(8,128)(2,1)} copy-done((bf16[8,64,1280]{2,1,0:T(8,128)(2,1)}, bf16[8,64,1280]{2,1,0:T(8,128)(2,1)S(1)}, u32[]{:S(2)}) %copy-start.2) | copy-done | bytes 1310744
  55.0 0.1 slice_convert_fusion.2
  55.1 1.5 %slice.146 = bf16[512,1152]{1,0:T(8,128)(2,1)S(1)} slice(bf16[512,1280]{1,0:T(8,128)(2,1)} %bitcast.92), slice={[0:512], [0:1152]} | slice | bytes 2359296 | tf_op jit(solution)/shard_map/slice | solution.py:104
  56.6 0.4 fusion.27
  57.0 0.1 copy-done.5
  57.2 1.2 %fusion.17 = bf16[512,512]{1,0:T(8,128)(2,1)S(1)} fusion(bf16[512,1280]{1,0:T(8,128)(2,1)S(1)} %bitcast.96, f32[]{:T(128)} %bitcast.84, f32[]{:T(128)} %bitcast.82, s32[512]{0:T(512)S(1)} %add.260, s32[512]{0:T(512)S(1)} %bitcast.123, s32[512]{0:T(512)S(1)} %get-tuple-element.9, s32[512]{0:T(512)S(1)} %get-tuple-element.8, bf16[512,1280]{1,0:T(8,128)(2,1)S(1)} %bitcast.93), kind=kOutput, calls=%fused_computation.24 | convolution fusion | flops 607387648 | bytes 2891784 | tf_op jit(solution)/shard_map/dot_general | solution.py:13
  58.4 0.8 fusion.20
  59.3 0.5 copy-done.1
  59.7 1.2 %fusion.15 = bf16[512,512]{1,0:T(8,128)(2,1)S(1)} fusion(bf16[512,1280]{1,0:T(8,128)(2,1)S(1)} %bitcast.89, s32[512]{0:T(512)S(1)} %add.272, s32[512]{0:T(512)S(1)} %bitcast.124, f32[]{:T(128)} %bitcast.85, f32[]{:T(128)} %bitcast.83, s32[512]{0:T(512)S(1)} %get-tuple-element.9, s32[512]{0:T(512)S(1)} %get-tuple-element.8, bf16[512,1280]{1,0:T(8,128)(2,1)S(1)} %bitcast.94), kind=kOutput, calls=%fused_computation.22 | convolution fusion | flops 607387648 | bytes 2891784 | tf_op jit(solution)/shard_map/dot_general | solution.py:13
  60.9 1.9 %convolution_add_fusion = bf16[512,1152]{1,0:T(8,128)(2,1)} fusion(f32[512,1152]{1,0:T(8,128)S(1)} %fusion.20, bf16[512,512]{1,0:T(8,128)(2,1)S(1)} %fusion.15, bf16[512,1280]{1,0:T(8,128)(2,1)S(1)} %bitcast.90), kind=kOutput, calls=%fused_computation.2 | convolution fusion | flops 605159424 | bytes 5242880 | tf_op jit(solution)/shard_map/dot_general | solution.py:129
  62.8 4.6 %all-to-all-start.1 = ((bf16[8,64,1152]{2,1,0:T(8,128)(2,1)}), bf16[8,64,1152]{2,1,0:T(8,128)(2,1)S(1)}, u32[]{:S(2)}, u32[]{:S(2)}) async-start(bf16[8,64,1152]{2,1,0:T(8,128)(2,1)} %bitcast.29), calls=%async_computation.1 | async-start | bytes 2359296 | tf_op jit(solution)/shard_map/all_to_all | solution.py:130
  67.4 0.9 fusion.53
  68.5 7.0 %collective-permute-start.12 = (bf16[4,32,1152]{2,1,0:T(8,128)(2,1)S(1)}, bf16[4,32,1152]{2,1,0:T(8,128)(2,1)S(1)}, u32[]{:S(2)}, u32[]{:S(2)}) collective-permute-start(bf16[4,32,1152]{2,1,0:T(8,128)(2,1)S(1)} %bitcast.111), channel_id=1, source_target_pairs={{0,12},{1,13},{2,14},{3,15},{4,0},{5,1},{6,2},{7,3},{8,4},{9,5},{1... | collective-permute-start | bytes 884744 | tf_op jit(solution)/shard_map/ppermute | solution.py:58
  75.5 1.4 %collective-permute-start.13 = (bf16[4,32,1152]{2,1,0:T(8,128)(2,1)S(1)}, bf16[4,32,1152]{2,1,0:T(8,128)(2,1)S(1)}, u32[]{:S(2)}, u32[]{:S(2)}) collective-permute-start(bf16[4,32,1152]{2,1,0:T(8,128)(2,1)S(1)} %bitcast.109), channel_id=1, source_target_pairs={{0,8},{1,9},{2,10},{3,11},{4,12},{5,13},{6,14},{7,15},{8,0},{9,1},... | collective-permute-start | bytes 884744 | tf_op jit(solution)/shard_map/ppermute | solution.py:58
  76.9 0.9 fusion.52
  78.0 3.2 %collective-permute-start.18 = (bf16[4,32,1152]{2,1,0:T(8,128)(2,1)S(1)}, bf16[4,32,1152]{2,1,0:T(8,128)(2,1)S(1)}, u32[]{:S(2)}, u32[]{:S(2)}) collective-permute-start(bf16[4,32,1152]{2,1,0:T(8,128)(2,1)S(1)} %bitcast.108), channel_id=1, source_target_pairs={{0,3},{1,0},{2,1},{3,2},{4,7},{5,4},{6,5},{7,6},{8,11},{9,8},{10,9... | collective-permute-start | bytes 884744 | tf_op jit(solution)/shard_map/ppermute | solution.py:59
  81.2 1.6 %collective-permute-done.14 = bf16[4,32,1152]{2,1,0:T(8,128)(2,1)S(1)} collective-permute-done((bf16[4,32,1152]{2,1,0:T(8,128)(2,1)S(1)}, bf16[4,32,1152]{2,1,0:T(8,128)(2,1)S(1)}, u32[]{:S(2)}, u32[]{:S(2)}) %collective-permute-start.14) | collective-permute-done | bytes 294944 | tf_op jit(solution)/shard_map/ppermute | solution.py:58
  82.8 0.5 collective-permute-start.19
  83.3 5.2 %collective-permute-done.12 = bf16[4,32,1152]{2,1,0:T(8,128)(2,1)S(1)} collective-permute-done((bf16[4,32,1152]{2,1,0:T(8,128)(2,1)S(1)}, bf16[4,32,1152]{2,1,0:T(8,128)(2,1)S(1)}, u32[]{:S(2)}, u32[]{:S(2)}) %collective-permute-start.12) | collective-permute-done | bytes 294944 | tf_op jit(solution)/shard_map/ppermute | solution.py:58
  88.5 1.8 %collective-permute-done.13 = bf16[4,32,1152]{2,1,0:T(8,128)(2,1)S(1)} collective-permute-done((bf16[4,32,1152]{2,1,0:T(8,128)(2,1)S(1)}, bf16[4,32,1152]{2,1,0:T(8,128)(2,1)S(1)}, u32[]{:S(2)}, u32[]{:S(2)}) %collective-permute-start.13) | collective-permute-done | bytes 294944 | tf_op jit(solution)/shard_map/ppermute | solution.py:58
  90.3 0.1 fusion.48
  90.5 0.9 collective-permute-start.15
  91.3 1.2 %collective-permute-start.17 = (bf16[32,1152]{1,0:T(8,128)(2,1)S(1)}, bf16[32,1152]{1,0:T(8,128)(2,1)S(1)}, u32[]{:S(2)}, u32[]{:S(2)}) collective-permute-start(bf16[32,1152]{1,0:T(8,128)(2,1)S(1)} %get-tuple-element.25), channel_id=1, source_target_pairs={{0,1},{1,2},{2,3},{3,0},{4,5},{5,6},{6,7},{7,4},{8,9},{9,10},{10,1... | collective-permute-start | bytes 221192 | tf_op jit(solution)/shard_map/ppermute | solution.py:63
  92.6 1.5 %collective-permute-done.20 = bf16[4,32,1152]{2,1,0:T(8,128)(2,1)S(1)} collective-permute-done((bf16[4,32,1152]{2,1,0:T(8,128)(2,1)S(1)}, bf16[4,32,1152]{2,1,0:T(8,128)(2,1)S(1)}, u32[]{:S(2)}, u32[]{:S(2)}) %collective-permute-start.20) | collective-permute-done | bytes 294944 | tf_op jit(solution)/shard_map/ppermute | solution.py:59
  94.0 0.2 collective-permute-done.18
  94.2 0.1 fusion.49
  94.4 0.8 collective-permute-start.21
  95.2 1.3 %collective-permute-start.23 = (bf16[32,1152]{1,0:T(8,128)(2,1)S(1)}, bf16[32,1152]{1,0:T(8,128)(2,1)S(1)}, u32[]{:S(2)}, u32[]{:S(2)}) collective-permute-start(bf16[32,1152]{1,0:T(8,128)(2,1)S(1)} %get-tuple-element.28), channel_id=1, source_target_pairs={{0,4},{1,5},{2,6},{3,7},{4,8},{5,9},{6,10},{7,11},{8,12},{9,13},{1... | collective-permute-start | bytes 221192 | tf_op jit(solution)/shard_map/ppermute | solution.py:64
  96.5 3.6 %collective-permute-start.22 = (bf16[32,1152]{1,0:T(8,128)(2,1)S(1)}, bf16[32,1152]{1,0:T(8,128)(2,1)S(1)}, u32[]{:S(2)}, u32[]{:S(2)}) collective-permute-start(bf16[32,1152]{1,0:T(8,128)(2,1)S(1)} %get-tuple-element.29), channel_id=1, source_target_pairs={{0,8},{1,9},{2,10},{3,11},{4,12},{5,13},{6,14},{7,15},{8,0},{9,1},... | collective-permute-start | bytes 221192 | tf_op jit(solution)/shard_map/ppermute | solution.py:64
  100.1 0.8 collective-permute-done.23
  100.9 2.2 %collective-permute-done.22 = bf16[32,1152]{1,0:T(8,128)(2,1)S(1)} collective-permute-done((bf16[32,1152]{1,0:T(8,128)(2,1)S(1)}, bf16[32,1152]{1,0:T(8,128)(2,1)S(1)}, u32[]{:S(2)}, u32[]{:S(2)}) %collective-permute-start.22) | collective-permute-done | bytes 73760 | tf_op jit(solution)/shard_map/ppermute | solution.py:64
  103.2 0.7 pad_maximum_fusion.4
  103.9 1.3 %gather_fusion = bf16[256,1152]{1,0:T(8,128)(2,1)S(1)} fusion(bf16[512,1152]{1,0:T(8,128)(2,1)S(1)} %bitcast.87, s32[1024]{0:T(1024)S(1)} %pad_clamp_fusion), kind=kCustom, calls=%fused_computation | custom fusion | bytes 1180672 | tf_op jit(solution)/shard_map/gather | solution.py:131
  105.2 1.1 %convert_element_type.141 = f32[256,1152]{1,0:T(8,128)} convert(bf16[256,1152]{1,0:T(8,128)(2,1)S(1)} %gather_fusion) | non-fusion elementwise | flops 294912 | bytes 1769472 | tf_op jit(solution)/shard_map/convert_element_type | solution.py:131
  (58 shorter events, 1.9 us)
Async XLA Ops:
  2.4 25.2 %collective-permute-start.1 = (bf16[32,1280]{1,0:T(8,128)(2,1)S(1)}, bf16[32,1280]{1,0:T(8,128)(2,1)S(1)}, u32[]{:S(2)}, u32[]{:S(2)}) collective-permute-start(bf16[32,1280]{1,0:T(8,128)(2,1)S(1)} %get-tuple-element.32), channel_id=1, source_target_pairs={{0,2},{1,3},{2,0},{3,1},{4,6},{5,7},{6,4},{7,5},{8,10},{9,11},{10,... | collective-permute-start | bytes 245768 | tf_op jit(solution)/shard_map/ppermute | solution.py:39
  5.7 24.0 %collective-permute-start = (bf16[32,1280]{1,0:T(8,128)(2,1)S(1)}, bf16[32,1280]{1,0:T(8,128)(2,1)S(1)}, u32[]{:S(2)}, u32[]{:S(2)}) collective-permute-start(bf16[32,1280]{1,0:T(8,128)(2,1)S(1)} %get-tuple-element.32), channel_id=1, source_target_pairs={{0,1},{1,2},{2,3},{3,0},{4,5},{5,6},{6,7},{7,4},{8,9},{9,10},{10,1... | collective-permute-start | bytes 245768 | tf_op jit(solution)/shard_map/ppermute | solution.py:39
  6.4 23.3 %collective-permute-start.2 = (bf16[32,1280]{1,0:T(8,128)(2,1)S(1)}, bf16[32,1280]{1,0:T(8,128)(2,1)S(1)}, u32[]{:S(2)}, u32[]{:S(2)}) collective-permute-start(bf16[32,1280]{1,0:T(8,128)(2,1)S(1)} %get-tuple-element.32), channel_id=1, source_target_pairs={{0,3},{1,0},{2,1},{3,2},{4,7},{5,4},{6,5},{7,6},{8,11},{9,8},{10,9... | collective-permute-start | bytes 245768 | tf_op jit(solution)/shard_map/ppermute | solution.py:39
  9.0 21.8 %collective-permute-start.7 = (bf16[32,1280]{1,0:T(8,128)(2,1)S(1)}, bf16[32,1280]{1,0:T(8,128)(2,1)S(1)}, u32[]{:S(2)}, u32[]{:S(2)}) collective-permute-start(bf16[32,1280]{1,0:T(8,128)(2,1)S(1)} %get-tuple-element.30), channel_id=1, source_target_pairs={{0,8},{1,9},{2,10},{3,11},{4,12},{5,13},{6,14},{7,15},{8,0},{9,1},... | collective-permute-start | bytes 245768 | tf_op jit(solution)/shard_map/ppermute | solution.py:40
  12.9 20.4 %collective-permute-start.6 = (bf16[32,1280]{1,0:T(8,128)(2,1)S(1)}, bf16[32,1280]{1,0:T(8,128)(2,1)S(1)}, u32[]{:S(2)}, u32[]{:S(2)}) collective-permute-start(bf16[32,1280]{1,0:T(8,128)(2,1)S(1)} %get-tuple-element.30), channel_id=1, source_target_pairs={{0,4},{1,5},{2,6},{3,7},{4,8},{5,9},{6,10},{7,11},{8,12},{9,13},{1... | collective-permute-start | bytes 245768 | tf_op jit(solution)/shard_map/ppermute | solution.py:40
  21.5 32.4 %all-to-all-start = ((bf16[8,64,1280]{2,1,0:T(8,128)(2,1)}), bf16[8,64,1280]{2,1,0:T(8,128)(2,1)S(1)}, u32[]{:S(2)}, u32[]{:S(2)}) async-start(bf16[8,64,1280]{2,1,0:T(8,128)(2,1)} %bitcast.5), calls=%async_computation | async-start | bytes 2621440 | tf_op jit(solution)/shard_map/all_to_all | solution.py:103
  27.5 11.9 %collective-permute-start.8 = (bf16[32,1280]{1,0:T(8,128)(2,1)S(1)}, bf16[32,1280]{1,0:T(8,128)(2,1)S(1)}, u32[]{:S(2)}, u32[]{:S(2)}) collective-permute-start(bf16[32,1280]{1,0:T(8,128)(2,1)S(1)} %get-tuple-element.30), channel_id=1, source_target_pairs={{0,12},{1,13},{2,14},{3,15},{4,0},{5,1},{6,2},{7,3},{8,4},{9,5},{1... | collective-permute-start | bytes 245768 | tf_op jit(solution)/shard_map/ppermute | solution.py:40
  29.8 12.2 %collective-permute-start.4 = (bf16[4,32,1280]{2,1,0:T(8,128)(2,1)S(1)}, bf16[4,32,1280]{2,1,0:T(8,128)(2,1)S(1)}, u32[]{:S(2)}, u32[]{:S(2)}) collective-permute-start(bf16[4,32,1280]{2,1,0:T(8,128)(2,1)S(1)} %get-tuple-element.23), channel_id=1, source_target_pairs={{0,8},{1,9},{2,10},{3,11},{4,12},{5,13},{6,14},{7,15},{8,0},{9,1},... | collective-permute-start | bytes 983048 | tf_op jit(solution)/shard_map/ppermute | solution.py:48
  29.9 18.1 %collective-permute-start.3 = (bf16[4,32,1280]{2,1,0:T(8,128)(2,1)S(1)}, bf16[4,32,1280]{2,1,0:T(8,128)(2,1)S(1)}, u32[]{:S(2)}, u32[]{:S(2)}) collective-permute-start(bf16[4,32,1280]{2,1,0:T(8,128)(2,1)S(1)} %get-tuple-element.23), channel_id=1, source_target_pairs={{0,4},{1,5},{2,6},{3,7},{4,8},{5,9},{6,10},{7,11},{8,12},{9,13},{1... | collective-permute-start | bytes 983048 | tf_op jit(solution)/shard_map/ppermute | solution.py:48
  30.8 17.3 %collective-permute-start.5 = (bf16[4,32,1280]{2,1,0:T(8,128)(2,1)S(1)}, bf16[4,32,1280]{2,1,0:T(8,128)(2,1)S(1)}, u32[]{:S(2)}, u32[]{:S(2)}) collective-permute-start(bf16[4,32,1280]{2,1,0:T(8,128)(2,1)S(1)} %get-tuple-element.23), channel_id=1, source_target_pairs={{0,12},{1,13},{2,14},{3,15},{4,0},{5,1},{6,2},{7,3},{8,4},{9,5},{1... | collective-permute-start | bytes 983048 | tf_op jit(solution)/shard_map/ppermute | solution.py:48
  39.5 9.9 %collective-permute-start.10 = (bf16[4,32,1280]{2,1,0:T(8,128)(2,1)S(1)}, bf16[4,32,1280]{2,1,0:T(8,128)(2,1)S(1)}, u32[]{:S(2)}, u32[]{:S(2)}) collective-permute-start(bf16[4,32,1280]{2,1,0:T(8,128)(2,1)S(1)} %get-tuple-element.21), channel_id=1, source_target_pairs={{0,2},{1,3},{2,0},{3,1},{4,6},{5,7},{6,4},{7,5},{8,10},{9,11},{10,... | collective-permute-start | bytes 983048 | tf_op jit(solution)/shard_map/ppermute | solution.py:49
  39.6 11.9 %collective-permute-start.9 = (bf16[4,32,1280]{2,1,0:T(8,128)(2,1)S(1)}, bf16[4,32,1280]{2,1,0:T(8,128)(2,1)S(1)}, u32[]{:S(2)}, u32[]{:S(2)}) collective-permute-start(bf16[4,32,1280]{2,1,0:T(8,128)(2,1)S(1)} %get-tuple-element.21), channel_id=1, source_target_pairs={{0,1},{1,2},{2,3},{3,0},{4,5},{5,6},{6,7},{7,4},{8,9},{9,10},{10,1... | collective-permute-start | bytes 983048 | tf_op jit(solution)/shard_map/ppermute | solution.py:49
  42.0 10.5 %collective-permute-start.11 = (bf16[4,32,1280]{2,1,0:T(8,128)(2,1)S(1)}, bf16[4,32,1280]{2,1,0:T(8,128)(2,1)S(1)}, u32[]{:S(2)}, u32[]{:S(2)}) collective-permute-start(bf16[4,32,1280]{2,1,0:T(8,128)(2,1)S(1)} %get-tuple-element.21), channel_id=1, source_target_pairs={{0,3},{1,0},{2,1},{3,2},{4,7},{5,4},{6,5},{7,6},{8,11},{9,8},{10,9... | collective-permute-start | bytes 983048 | tf_op jit(solution)/shard_map/ppermute | solution.py:49
  48.2 1.1 %copy-start.4 = (bf16[4,4,32,1280]{3,2,1,0:T(8,128)(2,1)}, bf16[4,4,32,1280]{3,2,1,0:T(8,128)(2,1)S(1)}, u32[]{:S(2)}) copy-start(bf16[4,4,32,1280]{3,2,1,0:T(8,128)(2,1)S(1)} %pad_maximum_fusion) | copy-start | bytes 3932164
  52.7 1.1 copy-start
  53.9 1.1 %copy-start.2 = (bf16[8,64,1280]{2,1,0:T(8,128)(2,1)}, bf16[8,64,1280]{2,1,0:T(8,128)(2,1)S(1)}, u32[]{:S(2)}) copy-start(bf16[8,64,1280]{2,1,0:T(8,128)(2,1)S(1)} %all-to-all-done) | copy-start | bytes 3932164
  55.1 1.9 %copy-start.3 = (bf16[8,64,1280]{2,1,0:T(8,128)(2,1)S(1)}, bf16[8,64,1280]{2,1,0:T(8,128)(2,1)}, u32[]{:S(2)}) copy-start(bf16[8,64,1280]{2,1,0:T(8,128)(2,1)} %copy-done.2) | copy-start | bytes 3932164
  55.1 2.1 %copy-start.5 = (bf16[4,4,32,1280]{3,2,1,0:T(8,128)(2,1)S(1)}, bf16[4,4,32,1280]{3,2,1,0:T(8,128)(2,1)}, u32[]{:S(2)}) copy-start(bf16[4,4,32,1280]{3,2,1,0:T(8,128)(2,1)} %copy-done.4) | copy-start | bytes 3932164
  58.4 1.3 %copy-start.1 = (bf16[4,4,32,1280]{3,2,1,0:T(8,128)(2,1)S(1)}, bf16[4,4,32,1280]{3,2,1,0:T(8,128)(2,1)}, u32[]{:S(2)}) copy-start(bf16[4,4,32,1280]{3,2,1,0:T(8,128)(2,1)} %copy-done) | copy-start | bytes 3932164
  62.8 41.1 %all-to-all-start.1 = ((bf16[8,64,1152]{2,1,0:T(8,128)(2,1)}), bf16[8,64,1152]{2,1,0:T(8,128)(2,1)S(1)}, u32[]{:S(2)}, u32[]{:S(2)}) async-start(bf16[8,64,1152]{2,1,0:T(8,128)(2,1)} %bitcast.29), calls=%async_computation.1 | async-start | bytes 2359296 | tf_op jit(solution)/shard_map/all_to_all | solution.py:130
  68.4 14.4 %collective-permute-start.14 = (bf16[4,32,1152]{2,1,0:T(8,128)(2,1)S(1)}, bf16[4,32,1152]{2,1,0:T(8,128)(2,1)S(1)}, u32[]{:S(2)}, u32[]{:S(2)}) collective-permute-start(bf16[4,32,1152]{2,1,0:T(8,128)(2,1)S(1)} %bitcast.112), channel_id=1, source_target_pairs={{0,4},{1,5},{2,6},{3,7},{4,8},{5,9},{6,10},{7,11},{8,12},{9,13},{1... | collective-permute-start | bytes 884744 | tf_op jit(solution)/shard_map/ppermute | solution.py:58
  68.5 20.0 %collective-permute-start.12 = (bf16[4,32,1152]{2,1,0:T(8,128)(2,1)S(1)}, bf16[4,32,1152]{2,1,0:T(8,128)(2,1)S(1)}, u32[]{:S(2)}, u32[]{:S(2)}) collective-permute-start(bf16[4,32,1152]{2,1,0:T(8,128)(2,1)S(1)} %bitcast.111), channel_id=1, source_target_pairs={{0,12},{1,13},{2,14},{3,15},{4,0},{5,1},{6,2},{7,3},{8,4},{9,5},{1... | collective-permute-start | bytes 884744 | tf_op jit(solution)/shard_map/ppermute | solution.py:58
  75.5 14.8 %collective-permute-start.13 = (bf16[4,32,1152]{2,1,0:T(8,128)(2,1)S(1)}, bf16[4,32,1152]{2,1,0:T(8,128)(2,1)S(1)}, u32[]{:S(2)}, u32[]{:S(2)}) collective-permute-start(bf16[4,32,1152]{2,1,0:T(8,128)(2,1)S(1)} %bitcast.109), channel_id=1, source_target_pairs={{0,8},{1,9},{2,10},{3,11},{4,12},{5,13},{6,14},{7,15},{8,0},{9,1},... | collective-permute-start | bytes 884744 | tf_op jit(solution)/shard_map/ppermute | solution.py:58
  77.9 16.2 %collective-permute-start.20 = (bf16[4,32,1152]{2,1,0:T(8,128)(2,1)S(1)}, bf16[4,32,1152]{2,1,0:T(8,128)(2,1)S(1)}, u32[]{:S(2)}, u32[]{:S(2)}) collective-permute-start(bf16[4,32,1152]{2,1,0:T(8,128)(2,1)S(1)} %bitcast.110), channel_id=1, source_target_pairs={{0,1},{1,2},{2,3},{3,0},{4,5},{5,6},{6,7},{7,4},{8,9},{9,10},{10,1... | collective-permute-start | bytes 884744 | tf_op jit(solution)/shard_map/ppermute | solution.py:59
  78.0 16.3 %collective-permute-start.18 = (bf16[4,32,1152]{2,1,0:T(8,128)(2,1)S(1)}, bf16[4,32,1152]{2,1,0:T(8,128)(2,1)S(1)}, u32[]{:S(2)}, u32[]{:S(2)}) collective-permute-start(bf16[4,32,1152]{2,1,0:T(8,128)(2,1)S(1)} %bitcast.108), channel_id=1, source_target_pairs={{0,3},{1,0},{2,1},{3,2},{4,7},{5,4},{6,5},{7,6},{8,11},{9,8},{10,9... | collective-permute-start | bytes 884744 | tf_op jit(solution)/shard_map/ppermute | solution.py:59
  82.8 11.4 %collective-permute-start.19 = (bf16[4,32,1152]{2,1,0:T(8,128)(2,1)S(1)}, bf16[4,32,1152]{2,1,0:T(8,128)(2,1)S(1)}, u32[]{:S(2)}, u32[]{:S(2)}) collective-permute-start(bf16[4,32,1152]{2,1,0:T(8,128)(2,1)S(1)} %bitcast.107), channel_id=1, source_target_pairs={{0,2},{1,3},{2,0},{3,1},{4,6},{5,7},{6,4},{7,5},{8,10},{9,11},{10,... | collective-permute-start | bytes 884744 | tf_op jit(solution)/shard_map/ppermute | solution.py:59
  90.5 6.0 %collective-permute-start.15 = (bf16[32,1152]{1,0:T(8,128)(2,1)S(1)}, bf16[32,1152]{1,0:T(8,128)(2,1)S(1)}, u32[]{:S(2)}, u32[]{:S(2)}) collective-permute-start(bf16[32,1152]{1,0:T(8,128)(2,1)S(1)} %get-tuple-element.24), channel_id=1, source_target_pairs={{0,3},{1,0},{2,1},{3,2},{4,7},{5,4},{6,5},{7,6},{8,11},{9,8},{10,9... | collective-permute-start | bytes 221192 | tf_op jit(solution)/shard_map/ppermute | solution.py:63
  91.3 8.7 %collective-permute-start.17 = (bf16[32,1152]{1,0:T(8,128)(2,1)S(1)}, bf16[32,1152]{1,0:T(8,128)(2,1)S(1)}, u32[]{:S(2)}, u32[]{:S(2)}) collective-permute-start(bf16[32,1152]{1,0:T(8,128)(2,1)S(1)} %get-tuple-element.25), channel_id=1, source_target_pairs={{0,1},{1,2},{2,3},{3,0},{4,5},{5,6},{6,7},{7,4},{8,9},{9,10},{10,1... | collective-permute-start | bytes 221192 | tf_op jit(solution)/shard_map/ppermute | solution.py:63
  94.0 6.0 %collective-permute-start.16 = (bf16[32,1152]{1,0:T(8,128)(2,1)S(1)}, bf16[32,1152]{1,0:T(8,128)(2,1)S(1)}, u32[]{:S(2)}, u32[]{:S(2)}) collective-permute-start(bf16[32,1152]{1,0:T(8,128)(2,1)S(1)} %get-tuple-element.26), channel_id=1, source_target_pairs={{0,2},{1,3},{2,0},{3,1},{4,6},{5,7},{6,4},{7,5},{8,10},{9,11},{10,... | collective-permute-start | bytes 221192 | tf_op jit(solution)/shard_map/ppermute | solution.py:63
  94.4 5.7 %collective-permute-start.21 = (bf16[32,1152]{1,0:T(8,128)(2,1)S(1)}, bf16[32,1152]{1,0:T(8,128)(2,1)S(1)}, u32[]{:S(2)}, u32[]{:S(2)}) collective-permute-start(bf16[32,1152]{1,0:T(8,128)(2,1)S(1)} %get-tuple-element.27), channel_id=1, source_target_pairs={{0,12},{1,13},{2,14},{3,15},{4,0},{5,1},{6,2},{7,3},{8,4},{9,5},{1... | collective-permute-start | bytes 221192 | tf_op jit(solution)/shard_map/ppermute | solution.py:64
  95.2 5.8 %collective-permute-start.23 = (bf16[32,1152]{1,0:T(8,128)(2,1)S(1)}, bf16[32,1152]{1,0:T(8,128)(2,1)S(1)}, u32[]{:S(2)}, u32[]{:S(2)}) collective-permute-start(bf16[32,1152]{1,0:T(8,128)(2,1)S(1)} %get-tuple-element.28), channel_id=1, source_target_pairs={{0,4},{1,5},{2,6},{3,7},{4,8},{5,9},{6,10},{7,11},{8,12},{9,13},{1... | collective-permute-start | bytes 221192 | tf_op jit(solution)/shard_map/ppermute | solution.py:64
  96.5 6.7 %collective-permute-start.22 = (bf16[32,1152]{1,0:T(8,128)(2,1)S(1)}, bf16[32,1152]{1,0:T(8,128)(2,1)S(1)}, u32[]{:S(2)}, u32[]{:S(2)}) collective-permute-start(bf16[32,1152]{1,0:T(8,128)(2,1)S(1)} %get-tuple-element.29), channel_id=1, source_target_pairs={{0,8},{1,9},{2,10},{3,11},{4,12},{5,13},{6,14},{7,15},{8,0},{9,1},... | collective-permute-start | bytes 221192 | tf_op jit(solution)/shard_map/ppermute | solution.py:64
where the time goes:
time: 107 us; the launch traced here: 106 us
  starting transfers between devices  47.9 us (45%)
  waiting for transfers between devices  29.3 us (27%)
  local copies, waits for them, and re-layouts  12 us (11%)
  other arithmetic  7.9 us (7%)
  matrix products  6.89 us (6%)
  between operations  2.25 us (2%)
    ppermute x3, waiting for transfers between devices, reduce_pair(): lax.ppermute(blocks_a[d].astype(low), 'mem', shift_pairs(nz, ny, -d, False))  8.58 us
    ppermute x3, starting transfers between devices, reduce_pair(): lax.ppermute(blocks_a[d].astype(low), 'mem', shift_pairs(nz, ny, -d, False))  8.47 us
    ppermute x3, starting transfers between devices, gather_first(): parts_b.append(lax.ppermute(xb, 'mem', shift_pairs(nz, ny, d, False)))  7.12 us
    ppermute x3, waiting for transfers between devices, gather_second(): parts_a.append(lax.ppermute(inner_a, 'mem', shift_pairs(nz, ny, d, False)))  6.7 us
    ppermute x3, starting transfers between devices, gather_first(): parts_a.append(lax.ppermute(xa, 'mem', shift_pairs(nz, ny, d, True)))  6.62 us
    ppermute x3, waiting for transfers between devices, gather_first(): parts_b.append(lax.ppermute(xb, 'mem', shift_pairs(nz, ny, d, False)))  6.23 us
    ppermute x3, starting transfers between devices, reduce_pair(): lax.ppermute(total_b[d].astype(low), 'mem', shift_pairs(nz, ny, -d, False))  5.68 us
    all_to_all x1, starting transfers between devices, inner_body(): lax.all_to_all(total.astype(jnp.bfloat16), 'grp', split_axis=0, concat_ax...  4.61 us
  transfers between devices with their start and end apart: 26, of which 12 were waited for; matrix products, arithmetic and copies ran while one was open for 11% of the time, Pallas kernels for 0%

commit v1 on v0

--- a/solution.py
+++ b/solution.py
@@ -32,22 +32,18 @@
     return pairs
 
 
-def gather_first(xa, xb, nz, ny):
-    parts_a = [xa]
+def gather_first(xb, nz, ny):
     parts_b = [xb]
-    for d in range(1, ny):
-        parts_a.append(lax.ppermute(xa, "mem", shift_pairs(nz, ny, d, True)))
+    for d in range(1, nz):
         parts_b.append(lax.ppermute(xb, "mem", shift_pairs(nz, ny, d, False)))
-    return jnp.stack(parts_a), jnp.stack(parts_b)
+    return jnp.stack(parts_b)
 
 
-def gather_second(inner_a, inner_b, nz, ny):
-    parts_a = [inner_a]
+def gather_second(inner_b, nz, ny):
     parts_b = [inner_b]
-    for d in range(1, nz):
-        parts_a.append(lax.ppermute(inner_a, "mem", shift_pairs(nz, ny, d, False)))
+    for d in range(1, ny):
         parts_b.append(lax.ppermute(inner_b, "mem", shift_pairs(nz, ny, d, True)))
-    return jnp.stack(parts_a), jnp.stack(parts_b)
+    return jnp.stack(parts_b)
 
 
 def reduce_pair(blocks_a, blocks_b, nz, ny):
@@ -85,8 +81,8 @@
     my_y = member % ny
     tag = jnp.broadcast_to(caption_bucket.astype(captions.dtype)[:, None], (cap_rows, 128))
     own = jnp.concatenate([captions, tag], axis=1)
-    inner_a, inner_b = gather_first(own[:half], own[half:], nz, ny)
-    got_a, got_b = gather_second(inner_a, inner_b, nz, ny)
+    got_a = lax.all_gather(own[:half], "mem", axis=0, tiled=True)
+    got_b = gather_second(gather_first(own[half:], nz, ny), nz, ny)
     bucket_hot = clip_bucket[:, None] == jnp.arange(n_buckets, dtype=jnp.int32)[None, :]
     owner = jnp.sum(jnp.where(bucket_hot, bucket_owner[None, :], 0), axis=1)
     onehot = (owner[:, None] == jnp.arange(groups, dtype=jnp.int32)[None, :]).astype(jnp.int32)
@@ -98,8 +94,11 @@
     ).astype(clips.dtype)
     extra = jnp.concatenate([jnp.zeros((clip_rows, 1), clips.dtype), meta,
                              jnp.zeros((clip_rows, 124), clips.dtype)], axis=1)
-    send_rows = jnp.zeros((slots, width + 128), clips.dtype).at[position].set(
-        jnp.concatenate([clips, extra], axis=1))
+    placer = (position[:, None] == jnp.arange(slots, dtype=jnp.int32)[None, :]).astype(clips.dtype)
+    send_rows = lax.dot_general(
+        placer, jnp.concatenate([clips, extra], axis=1), (((0,), (0,)), ((), ())),
+        preferred_element_type=jnp.float32,
+    ).astype(clips.dtype)
     recv_ext = lax.all_to_all(send_rows, "grp", split_axis=0, concat_axis=0, tiled=True)
     recv_rows = recv_ext[:, :width]
     recv_meta = recv_ext[:, width + 1:width + 4].astype(jnp.int32)
@@ -113,7 +112,7 @@
     src_a = ((my_z - za[:, None]) % nz) * ny + (my_y - ya[None, :]) % ny
     src_b = ((my_z - za[None, :]) % nz) * ny + (my_y - ya[:, None]) % ny
     base = group_index * panel
-    ids_a = (base + src_a[:, :, None] * cap_rows + ar[None, None, :]).reshape(-1)
+    ids_a = (base + jnp.arange(members, dtype=jnp.int32)[:, None] * cap_rows + ar[None, :]).reshape(-1)
     ids_b = (base + src_b[:, :, None] * cap_rows + half + ar[None, None, :]).reshape(-1)
     weights = []
     rows = []
@@ -128,9 +127,11 @@
     total = (jnp.dot(weights[0], rows[0], preferred_element_type=jnp.float32)
              + jnp.dot(weights[1], rows[1], preferred_element_type=jnp.float32))
     returned = lax.all_to_all(total.astype(jnp.bfloat16), "grp", split_axis=0, concat_axis=0, tiled=True)
-    clip_grad = returned[position].astype(jnp.float32)
+    clip_grad = jnp.dot(placer, returned, preferred_element_type=jnp.float32)
     weights, recv_rows, total = lax.optimization_barrier((weights, recv_rows, total))
-    partial_a = inner_cols(weights[0], recv_rows).reshape(nz, ny, half, width)
+    partial_a = jnp.take(
+        inner_cols(weights[0], recv_rows).reshape(members, half, width), src_a.reshape(-1), axis=0
+    ).reshape(nz, ny, half, width)
     partial_b = inner_cols(weights[1], recv_rows).reshape(ny, nz, half, width)
     grad_a, grad_b = reduce_pair(partial_a, partial_b, nz, ny)
     caption_grad = jnp.concatenate([grad_a, grad_b], axis=0)

time: 107 us -> 124 us (1.16)
  between operations: 2.25 us -> 15.6 us
  starting transfers between devices: 47.9 us -> 38.4 us
  matrix products: 6.89 us -> 14.5 us
  waiting for transfers between devices: 29.3 us -> 34.8 us
  other arithmetic: 7.9 us -> 12.4 us
  local copies, waits for them, and re-layouts: 12 us -> 7.7 us
    ppermute x3, waiting for transfers between devices: 3.09 us -> 17.1 us  [gather_second(): parts_b.append(lax.ppermute(inner_b, 'mem', shift_pairs(nz, ny, d, True)))]
    ppermute x6 -> x0, starting transfers between devices: 10 us -> none  [the longest x3 6.62 us: gather_first(): parts_a.append(lax.ppermute(xa, 'mem', shift_pairs(nz, ny, d, True)))]
    all_gather x0 -> x1, waiting for transfers between devices: none -> 8.16 us  [inner_body(): got_a = lax.all_gather(own[:half], 'mem', axis=0, tiled=True)]
    ppermute x6 -> x0, waiting for transfers between devices: 6.71 us -> none  [the longest x3 6.7 us: gather_second(): parts_a.append(lax.ppermute(inner_a, 'mem', shift_pairs(nz, ny, d, False)))]
    ppermute x3, waiting for transfers between devices: 6.23 us -> 0.01 us  [gather_first(): parts_b.append(lax.ppermute(xb, 'mem', shift_pairs(nz, ny, d, False)))]
    dot_general x0 -> x2, matrix products: none -> 4.61 us  [the longest x1 2.83 us: inner_body(): clip_grad = jnp.dot(placer, returned, preferred_element_type=jnp.float32)]
    unnamed x14 -> x9, local copies, waits for them, and re-layouts: 4.05 us -> 0.12 us
    ppermute x3, starting transfers between devices: 5.68 us -> 2.14 us  [reduce_pair(): lax.ppermute(total_b[d].astype(low), 'mem', shift_pairs(nz, ny, -d, False))]
  transfers between devices with their start and end apart: 26 -> 21, of which waited for: 12 -> 9; matrix products, arithmetic and copies ran while one was open for 11% -> 18% of each run, Pallas kernels for 0% -> 0%
where the time goes in v1:
time: 124 us; the launch traced here: 123 us
  starting transfers between devices  38.4 us (31%)
  waiting for transfers between devices  34.8 us (28%)
  between operations  15.6 us (13%)
  matrix products  14.5 us (12%)
  other arithmetic  12.4 us (10%)
  local copies, waits for them, and re-layouts  7.7 us (6%)
    ppermute x3, waiting for transfers between devices, gather_second(): parts_b.append(lax.ppermute(inner_b, 'mem', shift_pairs(nz, ny, d, True)))  17.1 us
    ppermute x3, starting transfers between devices, reduce_pair(): lax.ppermute(blocks_a[d].astype(low), 'mem', shift_pairs(nz, ny, -d, False))  8.67 us
    all_gather x1, waiting for transfers between devices, inner_body(): got_a = lax.all_gather(own[:half], 'mem', axis=0, tiled=True)  8.16 us
    ppermute x3, waiting for transfers between devices, reduce_pair(): lax.ppermute(blocks_a[d].astype(low), 'mem', shift_pairs(nz, ny, -d, False))  6.19 us
    another operation x7, other arithmetic  5.5 us
    dot_general x2, matrix products, inner_rows(): lax.dot_general(left, right, (((1,), (1,)), ((), ())), preferred_element_...  5.44 us
    ppermute x3, starting transfers between devices, gather_first(): parts_b.append(lax.ppermute(xb, 'mem', shift_pairs(nz, ny, d, False)))  5.41 us
    ppermute x3, starting transfers between devices, reduce_pair(): lax.ppermute(blocks_b[d].astype(low), 'mem', shift_pairs(nz, ny, -d, True))  4.93 us
  transfers between devices with their start and end apart: 21, of which 9 were waited for; matrix products, arithmetic and copies ran while one was open for 18% of the time, Pallas kernels for 0%

profile of v1, /device:TPU:0, one launch (start us, length us, event | category | flops | bytes accessed | tf_op | source)
XLA Modules:
  0.0 123.3 jit_solution(12876602995221154734)
XLA Ops:
  7.2 0.7 convert_element_type.126
  7.9 1.6 %pad_maximum_fusion.3 = (bf16[32,1280]{1,0:T(8,128)(2,1)S(1)}, bf16[32,1280]{1,0:T(8,128)(2,1)}) fusion(bf16[64,128]{1,0:T(8,128)(2,1)S(1)} %broadcast_in_dim.76, bf16[64,1152]{1,0:T(8,128)(2,1)} %param.9), kind=kLoop, calls=%fused_computation.60 | loop fusion | flops 327680 | bytes 327680 | tf_op jit(solution)/shard_map/concatenate | solution.py:83
  9.5 4.1 %collective-permute-start.2 = (bf16[32,1280]{1,0:T(8,128)(2,1)S(1)}, bf16[32,1280]{1,0:T(8,128)(2,1)S(1)}, u32[]{:S(2)}, u32[]{:S(2)}) collective-permute-start(bf16[32,1280]{1,0:T(8,128)(2,1)S(1)} %get-tuple-element.30), channel_id=1, source_target_pairs={{0,12},{1,13},{2,14},{3,15},{4,0},{5,1},{6,2},{7,3},{8,4},{9,5},{1... | collective-permute-start | bytes 245768 | tf_op jit(solution)/shard_map/ppermute | solution.py:38
  13.7 1.3 %collective-permute-start = (bf16[32,1280]{1,0:T(8,128)(2,1)S(1)}, bf16[32,1280]{1,0:T(8,128)(2,1)S(1)}, u32[]{:S(2)}, u32[]{:S(2)}) collective-permute-start(bf16[32,1280]{1,0:T(8,128)(2,1)S(1)} %get-tuple-element.30), channel_id=1, source_target_pairs={{0,4},{1,5},{2,6},{3,7},{4,8},{5,9},{6,10},{7,11},{8,12},{9,13},{1... | collective-permute-start | bytes 245768 | tf_op jit(solution)/shard_map/ppermute | solution.py:38
  15.0 0.7 add_convert_fusion
  15.6 0.1 stack.57
  15.7 0.7 fusion.41
  16.4 0.1 stack.58
  16.5 0.1 stack.59
  16.6 0.8 select_reduce_fusion
  17.4 0.6 reduce-window.6
  18.0 0.2 slice_reduce_fusion
  18.3 0.1 fusion.39
  18.4 1.2 concatenate.10
  19.7 1.8 %convolution_convert_fusion = bf16[512,1280]{1,0:T(8,128)(2,1)} fusion(bf16[256,1280]{1,0:T(8,128)(2,1)S(1)} %concatenate.10, s32[256]{0:T(256)S(1)} %multiply_add_fusion), kind=kOutput, calls=%fused_computation.2 | convolution fusion | flops 336330752 | bytes 1967104 | tf_op jit(solution)/shard_map/dot_general | solution.py:98
  21.4 4.3 %all-to-all-start = ((bf16[8,64,1280]{2,1,0:T(8,128)(2,1)}), bf16[8,64,1280]{2,1,0:T(8,128)(2,1)}, u32[]{:S(2)}, u32[]{:S(2)}) async-start(bf16[8,64,1280]{2,1,0:T(8,128)(2,1)} %bitcast.3), calls=%async_computation | async-start | bytes 2621440 | tf_op jit(solution)/shard_map/all_to_all | solution.py:102
  25.9 0.1 add.289
  26.1 0.1 add.287
  27.4 0.1 add.264
  27.5 0.1 add.280
  27.7 3.1 %collective-permute-start.5 = (bf16[4,32,1280]{2,1,0:T(8,128)(2,1)S(1)}, bf16[4,32,1280]{2,1,0:T(8,128)(2,1)S(1)}, u32[]{:S(2)}, u32[]{:S(2)}) collective-permute-start(bf16[4,32,1280]{2,1,0:T(8,128)(2,1)S(1)} %get-tuple-element.23), channel_id=1, source_target_pairs={{0,3},{1,0},{2,1},{3,2},{4,7},{5,4},{6,5},{7,6},{8,11},{9,8},{10,9... | collective-permute-start | bytes 983048 | tf_op jit(solution)/shard_map/ppermute | solution.py:45
  30.8 0.6 collective-permute-start.4
  31.4 1.0 collective-permute-start.3
  32.4 13.6 %collective-permute-done.5 = bf16[4,32,1280]{2,1,0:T(8,128)(2,1)S(1)} collective-permute-done((bf16[4,32,1280]{2,1,0:T(8,128)(2,1)S(1)}, bf16[4,32,1280]{2,1,0:T(8,128)(2,1)S(1)}, u32[]{:S(2)}, u32[]{:S(2)}) %collective-permute-start.5) | collective-permute-done | bytes 327712 | tf_op jit(solution)/shard_map/ppermute | solution.py:45
  46.0 3.5 %collective-permute-done.3 = bf16[4,32,1280]{2,1,0:T(8,128)(2,1)S(1)} collective-permute-done((bf16[4,32,1280]{2,1,0:T(8,128)(2,1)S(1)}, bf16[4,32,1280]{2,1,0:T(8,128)(2,1)S(1)}, u32[]{:S(2)}, u32[]{:S(2)}) %collective-permute-start.3) | collective-permute-done | bytes 327712 | tf_op jit(solution)/shard_map/ppermute | solution.py:45
  49.5 0.2 pad_maximum_fusion
  49.7 0.1 copy.24
  49.8 1.4 %slice.146 = bf16[512,1152]{1,0:T(8,128)(2,1)S(1)} slice(bf16[512,1280]{1,0:T(8,128)(2,1)} %bitcast.4), slice={[0:512], [0:1152]} | slice | bytes 2359296 | tf_op jit(solution)/shard_map/slice | solution.py:103
  51.2 1.0 slice_convert_fusion.1
  52.2 0.4 fusion.30
  52.6 2.5 %fusion.15 = bf16[512,512]{1,0:T(8,128)(2,1)S(1)} fusion(bf16[512,1280]{1,0:T(8,128)(2,1)S(1)} %bitcast.75, s32[512]{0:T(512)S(1)} %add.280, s32[512]{0:T(512)S(1)} %bitcast.87, f32[]{:T(128)} %bitcast.72, f32[]{:T(128)} %bitcast.70, s32[512]{0:T(512)S(1)} %get-tuple-element.9, s32[512]{0:T(512)S(1)} %get-tuple-element.8, bf16[512,1280]{1,0:T(8,128)(2,1)} %bitcast.4), kind=kOutput, calls=%fused_computation.21 | convolution fusion | flops 607387648 | bytes 2892800 | tf_op jit(solution)/shard_map/dot_general | solution.py:13
  55.1 8.2 %all-gather.2.cloned.1.call-done = bf16[512,1280]{1,0:T(8,128)(2,1)} async-done(((bf16[32,1280]{1,0:T(8,128)(2,1)}), bf16[512,1280]{1,0:T(8,128)(2,1)}) %all-gather.2.cloned.1.call-update) | async-done | bytes 1310736 | tf_op jit(solution)/shard_map/all_gather | solution.py:84
  63.2 1.1 convert_reduce_fusion
  64.3 2.9 %fusion.17 = bf16[512,512]{1,0:T(8,128)(2,1)S(1)} fusion(bf16[512,1280]{1,0:T(8,128)(2,1)} %all-gather.2.cloned.1.call-done, f32[]{:T(128)} %bitcast.71, f32[]{:T(128)} %bitcast.69, s32[512]{0:T(512)S(1)} %add.264, s32[512]{0:T(512)S(1)} %convert_reduce_fusion, s32[512]{0:T(512)S(1)} %get-tuple-element.9, s32[512]{0:T(512)S(1)} %get-tuple-element.8, ...), kind=kOutput, calls=%fused_computation.23 | convolution fusion | flops 607387648 | bytes 2892800 | tf_op jit(solution)/shard_map/dot_general | solution.py:13
  67.3 0.8 fusion.20
  68.1 1.9 %convolution_add_fusion = bf16[512,1152]{1,0:T(8,128)(2,1)} fusion(f32[512,1152]{1,0:T(8,128)S(1)} %fusion.20, bf16[512,512]{1,0:T(8,128)(2,1)S(1)} %fusion.15, bf16[512,1280]{1,0:T(8,128)(2,1)S(1)} %bitcast.76), kind=kOutput, calls=%fused_computation.1 | convolution fusion | flops 605159424 | bytes 5242880 | tf_op jit(solution)/shard_map/dot_general | solution.py:128
  70.0 4.3 %all-to-all-start.1 = ((bf16[8,64,1152]{2,1,0:T(8,128)(2,1)}), bf16[8,64,1152]{2,1,0:T(8,128)(2,1)}, u32[]{:S(2)}, u32[]{:S(2)}) async-start(bf16[8,64,1152]{2,1,0:T(8,128)(2,1)} %bitcast.77), calls=%async_computation.1 | async-start | bytes 2359296 | tf_op jit(solution)/shard_map/all_to_all | solution.py:129
  74.3 0.9 fusion.56
  75.2 0.9 fusion.55
  76.1 1.0 collective-permute-start.14
  77.1 2.7 %collective-permute-start.13 = (bf16[4,32,1152]{2,1,0:T(8,128)(2,1)}, bf16[4,32,1152]{2,1,0:T(8,128)(2,1)}, u32[]{:S(2)}, u32[]{:S(2)}) collective-permute-start(bf16[4,32,1152]{2,1,0:T(8,128)(2,1)} %bitcast.27), channel_id=1, source_target_pairs={{0,2},{1,3},{2,0},{3,1},{4,6},{5,7},{6,4},{7,5},{8,10},{9,11},{10,... | collective-permute-start | bytes 884744 | tf_op jit(solution)/shard_map/ppermute | solution.py:55
  79.8 0.9 slice.158
  80.6 1.3 %collective-permute-start.12 = (bf16[4,32,1152]{2,1,0:T(8,128)(2,1)}, bf16[4,32,1152]{2,1,0:T(8,128)(2,1)}, u32[]{:S(2)}, u32[]{:S(2)}) collective-permute-start(bf16[4,32,1152]{2,1,0:T(8,128)(2,1)} %bitcast.26), channel_id=1, source_target_pairs={{0,3},{1,0},{2,1},{3,2},{4,7},{5,4},{6,5},{7,6},{8,11},{9,8},{10,9... | collective-permute-start | bytes 884744 | tf_op jit(solution)/shard_map/ppermute | solution.py:55
  81.9 0.9 fusion.57
  82.8 2.1 %gather_fusion = f32[16,32,1152]{2,1,0:T(8,128)} fusion(f32[16,32,1152]{2,1,0:T(8,128)S(1)} %bitcast.73, s32[1024]{0:T(1024)S(1)} %pad_clamp_fusion), kind=kCustom, calls=%fused_computation | custom fusion | bytes 4718656 | tf_op jit(solution)/shard_map/jit(_take)/gather | solution.py:132
  84.9 2.1 %fusion.52 = (bf16[16,32,1152]{2,1,0:T(8,128)(2,1)S(1)}, f32[16,32,1152]{2,1,0:T(8,128)S(1)}) fusion(f32[16,32,1152]{2,1,0:T(8,128)} %gather_fusion, pred[16]{0:T(512)(128)(4,1)S(1)} %compare_and_fusion), kind=kLoop, calls=%fused_computation.110 | loop fusion | flops 1179648 | bytes 5898256 | tf_op jit(solution)/shard_map/convert.13
  87.0 0.1 fusion.54
  87.1 0.4 collective-permute-start.8
  87.5 2.7 %collective-permute-start.7 = (bf16[4,32,1152]{2,1,0:T(8,128)(2,1)S(1)}, bf16[4,32,1152]{2,1,0:T(8,128)(2,1)S(1)}, u32[]{:S(2)}, u32[]{:S(2)}) collective-permute-start(bf16[4,32,1152]{2,1,0:T(8,128)(2,1)S(1)} %get-tuple-element.18), channel_id=1, source_target_pairs={{0,8},{1,9},{2,10},{3,11},{4,12},{5,13},{6,14},{7,15},{8,0},{9,1},... | collective-permute-start | bytes 884744 | tf_op jit(solution)/shard_map/ppermute | solution.py:54
  90.2 5.6 %collective-permute-start.6 = (bf16[4,32,1152]{2,1,0:T(8,128)(2,1)S(1)}, bf16[4,32,1152]{2,1,0:T(8,128)(2,1)S(1)}, u32[]{:S(2)}, u32[]{:S(2)}) collective-permute-start(bf16[4,32,1152]{2,1,0:T(8,128)(2,1)S(1)} %get-tuple-element.16), channel_id=1, source_target_pairs={{0,12},{1,13},{2,14},{3,15},{4,0},{5,1},{6,2},{7,3},{8,4},{9,5},{1... | collective-permute-start | bytes 884744 | tf_op jit(solution)/shard_map/ppermute | solution.py:54
  95.8 1.3 %fusion.53 = (bf16[4,32,1152]{2,1,0:T(8,128)(2,1)S(1)}, f32[4,32,1152]{2,1,0:T(8,128)S(1)}) fusion(bf16[4,32,1152]{2,1,0:T(8,128)(2,1)} %collective-permute-done.14, bf16[4,32,1152]{2,1,0:T(8,128)(2,1)} %collective-permute-done.13, f32[4,32,1152]{2,1,0:T(8,128)S(1)} %bitcast.78, bf16[4,32,1152]{2,1,0:T(8,128)(2,1)} %collective-permute-done.12), kind=kLoop, calls=%fused_computation.111 | loop fusion | flops 1032192 | bytes 2359296 | tf_op jit(solution)/shard_map/convert.4
  97.2 2.1 %collective-permute-start.16 = (bf16[32,1152]{1,0:T(8,128)(2,1)S(1)}, bf16[32,1152]{1,0:T(8,128)(2,1)S(1)}, u32[]{:S(2)}, u32[]{:S(2)}) collective-permute-start(bf16[32,1152]{1,0:T(8,128)(2,1)S(1)} %get-tuple-element.29), channel_id=1, source_target_pairs={{0,8},{1,9},{2,10},{3,11},{4,12},{5,13},{6,14},{7,15},{8,0},{9,1},... | collective-permute-start | bytes 221192 | tf_op jit(solution)/shard_map/ppermute | solution.py:60
  99.2 3.1 %collective-permute-done.8 = bf16[4,32,1152]{2,1,0:T(8,128)(2,1)S(1)} collective-permute-done((bf16[4,32,1152]{2,1,0:T(8,128)(2,1)S(1)}, bf16[4,32,1152]{2,1,0:T(8,128)(2,1)S(1)}, u32[]{:S(2)}, u32[]{:S(2)}) %collective-permute-start.8) | collective-permute-done | bytes 294944 | tf_op jit(solution)/shard_map/ppermute | solution.py:54
  102.3 2.1 %collective-permute-done.7 = bf16[4,32,1152]{2,1,0:T(8,128)(2,1)S(1)} collective-permute-done((bf16[4,32,1152]{2,1,0:T(8,128)(2,1)S(1)}, bf16[4,32,1152]{2,1,0:T(8,128)(2,1)S(1)}, u32[]{:S(2)}, u32[]{:S(2)}) %collective-permute-start.7) | collective-permute-done | bytes 294944 | tf_op jit(solution)/shard_map/ppermute | solution.py:54
  104.4 1.0 collective-permute-done.6
  105.4 0.1 fusion.50
  105.6 0.9 collective-permute-start.11
  106.5 0.8 collective-permute-start.10
  107.3 2.3 %collective-permute-start.9 = (bf16[32,1152]{1,0:T(8,128)(2,1)S(1)}, bf16[32,1152]{1,0:T(8,128)(2,1)S(1)}, u32[]{:S(2)}, u32[]{:S(2)}) collective-permute-start(bf16[32,1152]{1,0:T(8,128)(2,1)S(1)} %get-tuple-element.24), channel_id=1, source_target_pairs={{0,3},{1,0},{2,1},{3,2},{4,7},{5,4},{6,5},{7,6},{8,11},{9,8},{10,9... | collective-permute-start | bytes 221192 | tf_op jit(solution)/shard_map/ppermute | solution.py:59
  109.6 1.6 %collective-permute-done.11 = bf16[32,1152]{1,0:T(8,128)(2,1)S(1)} collective-permute-done((bf16[32,1152]{1,0:T(8,128)(2,1)S(1)}, bf16[32,1152]{1,0:T(8,128)(2,1)S(1)}, u32[]{:S(2)}, u32[]{:S(2)}) %collective-permute-start.11) | collective-permute-done | bytes 73760 | tf_op jit(solution)/shard_map/ppermute | solution.py:59
  111.2 1.1 collective-permute-done.10
  112.3 0.6 collective-permute-done.9
  112.9 0.7 pad_maximum_fusion.2
  113.7 2.8 %fusion.25 = f32[256,1152]{1,0:T(8,128)} fusion(bf16[512,1152]{1,0:T(8,128)(2,1)} %bitcast.18, s32[256]{0:T(256)S(1)} %multiply_add_fusion), kind=kOutput, calls=%fused_computation.35 | convolution fusion | flops 302120960 | bytes 2360320 | tf_op jit(solution)/shard_map/dot_general | solution.py:130
  (46 shorter events, 0.8 us)
Async XLA Ops:
  7.2 56.1 %all-gather.2.cloned.1.call-start = ((), (), s32[]{:S(2)}) async-start(), calls=%async_computation.2 | async-start | bytes 1392640 | tf_op jit(solution)/shard_map/all_gather | solution.py:84
  9.5 18.1 %collective-permute-start.2 = (bf16[32,1280]{1,0:T(8,128)(2,1)S(1)}, bf16[32,1280]{1,0:T(8,128)(2,1)S(1)}, u32[]{:S(2)}, u32[]{:S(2)}) collective-permute-start(bf16[32,1280]{1,0:T(8,128)(2,1)S(1)} %get-tuple-element.30), channel_id=1, source_target_pairs={{0,12},{1,13},{2,14},{3,15},{4,0},{5,1},{6,2},{7,3},{8,4},{9,5},{1... | collective-permute-start | bytes 245768 | tf_op jit(solution)/shard_map/ppermute | solution.py:38
  13.7 13.9 %collective-permute-start.1 = (bf16[32,1280]{1,0:T(8,128)(2,1)S(1)}, bf16[32,1280]{1,0:T(8,128)(2,1)S(1)}, u32[]{:S(2)}, u32[]{:S(2)}) collective-permute-start(bf16[32,1280]{1,0:T(8,128)(2,1)S(1)} %get-tuple-element.30), channel_id=1, source_target_pairs={{0,8},{1,9},{2,10},{3,11},{4,12},{5,13},{6,14},{7,15},{8,0},{9,1},... | collective-permute-start | bytes 245768 | tf_op jit(solution)/shard_map/ppermute | solution.py:38
  13.7 13.9 %collective-permute-start = (bf16[32,1280]{1,0:T(8,128)(2,1)S(1)}, bf16[32,1280]{1,0:T(8,128)(2,1)S(1)}, u32[]{:S(2)}, u32[]{:S(2)}) collective-permute-start(bf16[32,1280]{1,0:T(8,128)(2,1)S(1)} %get-tuple-element.30), channel_id=1, source_target_pairs={{0,4},{1,5},{2,6},{3,7},{4,8},{5,9},{6,10},{7,11},{8,12},{9,13},{1... | collective-permute-start | bytes 245768 | tf_op jit(solution)/shard_map/ppermute | solution.py:38
  21.4 28.4 %all-to-all-start = ((bf16[8,64,1280]{2,1,0:T(8,128)(2,1)}), bf16[8,64,1280]{2,1,0:T(8,128)(2,1)}, u32[]{:S(2)}, u32[]{:S(2)}) async-start(bf16[8,64,1280]{2,1,0:T(8,128)(2,1)} %bitcast.3), calls=%async_computation | async-start | bytes 2621440 | tf_op jit(solution)/shard_map/all_to_all | solution.py:102
  27.7 18.4 %collective-permute-start.5 = (bf16[4,32,1280]{2,1,0:T(8,128)(2,1)S(1)}, bf16[4,32,1280]{2,1,0:T(8,128)(2,1)S(1)}, u32[]{:S(2)}, u32[]{:S(2)}) collective-permute-start(bf16[4,32,1280]{2,1,0:T(8,128)(2,1)S(1)} %get-tuple-element.23), channel_id=1, source_target_pairs={{0,3},{1,0},{2,1},{3,2},{4,7},{5,4},{6,5},{7,6},{8,11},{9,8},{10,9... | collective-permute-start | bytes 983048 | tf_op jit(solution)/shard_map/ppermute | solution.py:45
  30.8 15.3 %collective-permute-start.4 = (bf16[4,32,1280]{2,1,0:T(8,128)(2,1)S(1)}, bf16[4,32,1280]{2,1,0:T(8,128)(2,1)S(1)}, u32[]{:S(2)}, u32[]{:S(2)}) collective-permute-start(bf16[4,32,1280]{2,1,0:T(8,128)(2,1)S(1)} %get-tuple-element.23), channel_id=1, source_target_pairs={{0,2},{1,3},{2,0},{3,1},{4,6},{5,7},{6,4},{7,5},{8,10},{9,11},{10,... | collective-permute-start | bytes 983048 | tf_op jit(solution)/shard_map/ppermute | solution.py:45
  31.4 18.1 %collective-permute-start.3 = (bf16[4,32,1280]{2,1,0:T(8,128)(2,1)S(1)}, bf16[4,32,1280]{2,1,0:T(8,128)(2,1)S(1)}, u32[]{:S(2)}, u32[]{:S(2)}) collective-permute-start(bf16[4,32,1280]{2,1,0:T(8,128)(2,1)S(1)} %get-tuple-element.23), channel_id=1, source_target_pairs={{0,1},{1,2},{2,3},{3,0},{4,5},{5,6},{6,7},{7,4},{8,9},{9,10},{10,1... | collective-permute-start | bytes 983048 | tf_op jit(solution)/shard_map/ppermute | solution.py:45
  64.3 3.0 %copy-start.3 = (bf16[512,1280]{1,0:T(8,128)(2,1)S(1)}, bf16[512,1280]{1,0:T(8,128)(2,1)}, u32[]{:S(2)}) copy-start(bf16[512,1280]{1,0:T(8,128)(2,1)} %all-gather.2.cloned.1.call-done) | copy-start | bytes 3932164
  67.3 0.9 copy-start
  70.0 43.6 %all-to-all-start.1 = ((bf16[8,64,1152]{2,1,0:T(8,128)(2,1)}), bf16[8,64,1152]{2,1,0:T(8,128)(2,1)}, u32[]{:S(2)}, u32[]{:S(2)}) async-start(bf16[8,64,1152]{2,1,0:T(8,128)(2,1)} %bitcast.77), calls=%async_computation.1 | async-start | bytes 2359296 | tf_op jit(solution)/shard_map/all_to_all | solution.py:129
  75.2 6.7 %copy-start.1 = (bf16[512,512]{1,0:T(8,128)(2,1)S(1)}, bf16[512,512]{1,0:T(8,128)(2,1)}, u32[]{:S(2)}) copy-start(bf16[512,512]{1,0:T(8,128)(2,1)} %copy-done) | copy-start | bytes 1572868
  76.1 14.1 %collective-permute-start.14 = (bf16[4,32,1152]{2,1,0:T(8,128)(2,1)}, bf16[4,32,1152]{2,1,0:T(8,128)(2,1)}, u32[]{:S(2)}, u32[]{:S(2)}) collective-permute-start(bf16[4,32,1152]{2,1,0:T(8,128)(2,1)} %bitcast.28), channel_id=1, source_target_pairs={{0,1},{1,2},{2,3},{3,0},{4,5},{5,6},{6,7},{7,4},{8,9},{9,10},{10,1... | collective-permute-start | bytes 884744 | tf_op jit(solution)/shard_map/ppermute | solution.py:55
  77.1 18.7 %collective-permute-start.13 = (bf16[4,32,1152]{2,1,0:T(8,128)(2,1)}, bf16[4,32,1152]{2,1,0:T(8,128)(2,1)}, u32[]{:S(2)}, u32[]{:S(2)}) collective-permute-start(bf16[4,32,1152]{2,1,0:T(8,128)(2,1)} %bitcast.27), channel_id=1, source_target_pairs={{0,2},{1,3},{2,0},{3,1},{4,6},{5,7},{6,4},{7,5},{8,10},{9,11},{10,... | collective-permute-start | bytes 884744 | tf_op jit(solution)/shard_map/ppermute | solution.py:55
  80.6 15.2 %collective-permute-start.12 = (bf16[4,32,1152]{2,1,0:T(8,128)(2,1)}, bf16[4,32,1152]{2,1,0:T(8,128)(2,1)}, u32[]{:S(2)}, u32[]{:S(2)}) collective-permute-start(bf16[4,32,1152]{2,1,0:T(8,128)(2,1)} %bitcast.26), channel_id=1, source_target_pairs={{0,3},{1,0},{2,1},{3,2},{4,7},{5,4},{6,5},{7,6},{8,11},{9,8},{10,9... | collective-permute-start | bytes 884744 | tf_op jit(solution)/shard_map/ppermute | solution.py:55
  87.0 8.8 %copy-start.2 = (f32[128,1152]{1,0:T(8,128)S(1)}, f32[128,1152]{1,0:T(8,128)}, u32[]{:S(2)}) copy-start(f32[128,1152]{1,0:T(8,128)} %slice.158) | copy-start | bytes 1769476
  87.1 15.2 %collective-permute-start.8 = (bf16[4,32,1152]{2,1,0:T(8,128)(2,1)S(1)}, bf16[4,32,1152]{2,1,0:T(8,128)(2,1)S(1)}, u32[]{:S(2)}, u32[]{:S(2)}) collective-permute-start(bf16[4,32,1152]{2,1,0:T(8,128)(2,1)S(1)} %get-tuple-element.17), channel_id=1, source_target_pairs={{0,4},{1,5},{2,6},{3,7},{4,8},{5,9},{6,10},{7,11},{8,12},{9,13},{1... | collective-permute-start | bytes 884744 | tf_op jit(solution)/shard_map/ppermute | solution.py:54
  87.5 16.9 %collective-permute-start.7 = (bf16[4,32,1152]{2,1,0:T(8,128)(2,1)S(1)}, bf16[4,32,1152]{2,1,0:T(8,128)(2,1)S(1)}, u32[]{:S(2)}, u32[]{:S(2)}) collective-permute-start(bf16[4,32,1152]{2,1,0:T(8,128)(2,1)S(1)} %get-tuple-element.18), channel_id=1, source_target_pairs={{0,8},{1,9},{2,10},{3,11},{4,12},{5,13},{6,14},{7,15},{8,0},{9,1},... | collective-permute-start | bytes 884744 | tf_op jit(solution)/shard_map/ppermute | solution.py:54
  90.2 15.2 %collective-permute-start.6 = (bf16[4,32,1152]{2,1,0:T(8,128)(2,1)S(1)}, bf16[4,32,1152]{2,1,0:T(8,128)(2,1)S(1)}, u32[]{:S(2)}, u32[]{:S(2)}) collective-permute-start(bf16[4,32,1152]{2,1,0:T(8,128)(2,1)S(1)} %get-tuple-element.16), channel_id=1, source_target_pairs={{0,12},{1,13},{2,14},{3,15},{4,0},{5,1},{6,2},{7,3},{8,4},{9,5},{1... | collective-permute-start | bytes 884744 | tf_op jit(solution)/shard_map/ppermute | solution.py:54
  97.1 10.2 %collective-permute-start.17 = (bf16[32,1152]{1,0:T(8,128)(2,1)S(1)}, bf16[32,1152]{1,0:T(8,128)(2,1)S(1)}, u32[]{:S(2)}, u32[]{:S(2)}) collective-permute-start(bf16[32,1152]{1,0:T(8,128)(2,1)S(1)} %get-tuple-element.28), channel_id=1, source_target_pairs={{0,4},{1,5},{2,6},{3,7},{4,8},{5,9},{6,10},{7,11},{8,12},{9,13},{1... | collective-permute-start | bytes 221192 | tf_op jit(solution)/shard_map/ppermute | solution.py:60
  97.2 12.4 %collective-permute-start.16 = (bf16[32,1152]{1,0:T(8,128)(2,1)S(1)}, bf16[32,1152]{1,0:T(8,128)(2,1)S(1)}, u32[]{:S(2)}, u32[]{:S(2)}) collective-permute-start(bf16[32,1152]{1,0:T(8,128)(2,1)S(1)} %get-tuple-element.29), channel_id=1, source_target_pairs={{0,8},{1,9},{2,10},{3,11},{4,12},{5,13},{6,14},{7,15},{8,0},{9,1},... | collective-permute-start | bytes 221192 | tf_op jit(solution)/shard_map/ppermute | solution.py:60
  102.3 7.3 %collective-permute-start.15 = (bf16[32,1152]{1,0:T(8,128)(2,1)S(1)}, bf16[32,1152]{1,0:T(8,128)(2,1)S(1)}, u32[]{:S(2)}, u32[]{:S(2)}) collective-permute-start(bf16[32,1152]{1,0:T(8,128)(2,1)S(1)} %get-tuple-element.27), channel_id=1, source_target_pairs={{0,12},{1,13},{2,14},{3,15},{4,0},{5,1},{6,2},{7,3},{8,4},{9,5},{1... | collective-permute-start | bytes 221192 | tf_op jit(solution)/shard_map/ppermute | solution.py:60
  105.6 5.6 %collective-permute-start.11 = (bf16[32,1152]{1,0:T(8,128)(2,1)S(1)}, bf16[32,1152]{1,0:T(8,128)(2,1)S(1)}, u32[]{:S(2)}, u32[]{:S(2)}) collective-permute-start(bf16[32,1152]{1,0:T(8,128)(2,1)S(1)} %get-tuple-element.25), channel_id=1, source_target_pairs={{0,1},{1,2},{2,3},{3,0},{4,5},{5,6},{6,7},{7,4},{8,9},{9,10},{10,1... | collective-permute-start | bytes 221192 | tf_op jit(solution)/shard_map/ppermute | solution.py:59
  106.5 5.9 %collective-permute-start.10 = (bf16[32,1152]{1,0:T(8,128)(2,1)S(1)}, bf16[32,1152]{1,0:T(8,128)(2,1)S(1)}, u32[]{:S(2)}, u32[]{:S(2)}) collective-permute-start(bf16[32,1152]{1,0:T(8,128)(2,1)S(1)} %get-tuple-element.26), channel_id=1, source_target_pairs={{0,2},{1,3},{2,0},{3,1},{4,6},{5,7},{6,4},{7,5},{8,10},{9,11},{10,... | collective-permute-start | bytes 221192 | tf_op jit(solution)/shard_map/ppermute | solution.py:59
  107.3 5.6 %collective-permute-start.9 = (bf16[32,1152]{1,0:T(8,128)(2,1)S(1)}, bf16[32,1152]{1,0:T(8,128)(2,1)S(1)}, u32[]{:S(2)}, u32[]{:S(2)}) collective-permute-start(bf16[32,1152]{1,0:T(8,128)(2,1)S(1)} %get-tuple-element.24), channel_id=1, source_target_pairs={{0,3},{1,0},{2,1},{3,2},{4,7},{5,4},{6,5},{7,6},{8,11},{9,8},{10,9... | collective-permute-start | bytes 221192 | tf_op jit(solution)/shard_map/ppermute | solution.py:59
Sparse Core Ops, SparseCore 0:
  15.1 48.1 all-gather.1

commit v2 on v0

--- a/solution.py
+++ b/solution.py
@@ -98,8 +98,11 @@
     ).astype(clips.dtype)
     extra = jnp.concatenate([jnp.zeros((clip_rows, 1), clips.dtype), meta,
                              jnp.zeros((clip_rows, 124), clips.dtype)], axis=1)
-    send_rows = jnp.zeros((slots, width + 128), clips.dtype).at[position].set(
-        jnp.concatenate([clips, extra], axis=1))
+    placer = (position[:, None] == jnp.arange(slots, dtype=jnp.int32)[None, :]).astype(clips.dtype)
+    send_rows = lax.dot_general(
+        placer, jnp.concatenate([clips, extra], axis=1), (((0,), (0,)), ((), ())),
+        preferred_element_type=jnp.float32,
+    ).astype(clips.dtype)
     recv_ext = lax.all_to_all(send_rows, "grp", split_axis=0, concat_axis=0, tiled=True)
     recv_rows = recv_ext[:, :width]
     recv_meta = recv_ext[:, width + 1:width + 4].astype(jnp.int32)
@@ -125,13 +128,13 @@
             logits, recv_positive[:, None] == ids[None, :], recv_bucket[:, None] == bucket_y[None, :]
         ))
         rows.append(rows_y)
-    total = (jnp.dot(weights[0], rows[0], preferred_element_type=jnp.float32)
-             + jnp.dot(weights[1], rows[1], preferred_element_type=jnp.float32))
-    returned = lax.all_to_all(total.astype(jnp.bfloat16), "grp", split_axis=0, concat_axis=0, tiled=True)
-    clip_grad = returned[position].astype(jnp.float32)
-    weights, recv_rows, total = lax.optimization_barrier((weights, recv_rows, total))
     partial_a = inner_cols(weights[0], recv_rows).reshape(nz, ny, half, width)
     partial_b = inner_cols(weights[1], recv_rows).reshape(ny, nz, half, width)
+    weight_b, partial_b = lax.optimization_barrier((weights[1], partial_b))
+    total = (jnp.dot(weights[0], rows[0], preferred_element_type=jnp.float32)
+             + jnp.dot(weight_b, rows[1], preferred_element_type=jnp.float32))
+    returned = lax.all_to_all(total.astype(jnp.bfloat16), "grp", split_axis=0, concat_axis=0, tiled=True)
+    clip_grad = jnp.dot(placer, returned, preferred_element_type=jnp.float32)
     grad_a, grad_b = reduce_pair(partial_a, partial_b, nz, ny)
     caption_grad = jnp.concatenate([grad_a, grad_b], axis=0)
     return (clip_grad, caption_grad)

time: 107 us -> 106 us (level)
  matrix products: 6.89 us -> 14.3 us
  local copies, waits for them, and re-layouts: 12 us -> 5.06 us
  starting transfers between devices: 47.9 us -> 41.3 us
  other arithmetic: 7.9 us -> 13.8 us
  waiting for transfers between devices: 29.3 us -> 28.2 us
    ppermute x3, waiting for transfers between devices: 8.58 us -> 0.01 us  [reduce_pair(): lax.ppermute(blocks_a[d].astype(low), 'mem', shift_pairs(nz, ny, -d, False))]
    ppermute x3, starting transfers between devices: 8.47 us -> 2.03 us  [reduce_pair(): lax.ppermute(blocks_a[d].astype(low), 'mem', shift_pairs(nz, ny, -d, False))]
    ppermute x3, waiting for transfers between devices: 6.23 us -> 0.01 us  [gather_first(): parts_b.append(lax.ppermute(xb, 'mem', shift_pairs(nz, ny, d, False)))]
    ppermute x3, waiting for transfers between devices: 6.7 us -> 11.4 us  [gather_second(): parts_a.append(lax.ppermute(inner_a, 'mem', shift_pairs(nz, ny, d, False)))]
    ppermute x3, waiting for transfers between devices: 1.65 us -> 6.09 us  [reduce_pair(): lax.ppermute(blocks_b[d].astype(low), 'mem', shift_pairs(nz, ny, -d, True))]
    unnamed x14 -> x8, local copies, waits for them, and re-layouts: 4.05 us -> 0.23 us
    another operation x4, other arithmetic: 0.44 us -> 4.03 us  [gather_second(): return (jnp.stack(parts_a), jnp.stack(parts_b))]
    ppermute x3, waiting for transfers between devices: 3.09 us -> 6.52 us  [gather_second(): parts_b.append(lax.ppermute(inner_b, 'mem', shift_pairs(nz, ny, d, True)))]
  transfers between devices with their start and end apart: 26 -> 26, of which waited for: 12 -> 7; matrix products, arithmetic and copies ran while one was open for 11% -> 22% of each run, Pallas kernels for 0% -> 0%
where the time goes in v2:
time: 106 us; the launch traced here: 105 us
  starting transfers between devices  41.3 us (39%)
  waiting for transfers between devices  28.2 us (27%)
  matrix products  14.3 us (13%)
  other arithmetic  13.8 us (13%)
  local copies, waits for them, and re-layouts  5.06 us (5%)
  between operations  2.18 us (2%)
    ppermute x3, waiting for transfers between devices, gather_second(): parts_a.append(lax.ppermute(inner_a, 'mem', shift_pairs(nz, ny, d, False)))  11.4 us
    ppermute x3, starting transfers between devices, gather_first(): parts_b.append(lax.ppermute(xb, 'mem', shift_pairs(nz, ny, d, False)))  6.52 us
    ppermute x3, waiting for transfers between devices, gather_second(): parts_b.append(lax.ppermute(inner_b, 'mem', shift_pairs(nz, ny, d, True)))  6.52 us
    ppermute x3, waiting for transfers between devices, reduce_pair(): lax.ppermute(blocks_b[d].astype(low), 'mem', shift_pairs(nz, ny, -d, True))  6.09 us
    ppermute x3, starting transfers between devices, gather_first(): parts_a.append(lax.ppermute(xa, 'mem', shift_pairs(nz, ny, d, True)))  6.01 us
    ppermute x3, starting transfers between devices, reduce_pair(): lax.ppermute(total_b[d].astype(low), 'mem', shift_pairs(nz, ny, -d, False))  5.62 us
    ppermute x3, starting transfers between devices, reduce_pair(): lax.ppermute(total_a[d].astype(low), 'mem', shift_pairs(nz, ny, -d, True))  4.98 us
    another operation x7, other arithmetic  4.76 us
  transfers between devices with their start and end apart: 26, of which 7 were waited for; matrix products, arithmetic and copies ran while one was open for 22% of the time, Pallas kernels for 0%

profile of v2, /device:TPU:0, one launch (start us, length us, event | category | flops | bytes accessed | tf_op | source)
XLA Modules:
  0.0 104.9 jit_solution(6896924931119732253)
XLA Ops:
  0.6 0.7 convert_element_type.135
  1.4 1.0 pad_maximum_fusion.5
  2.4 1.8 %collective-permute-start = (bf16[32,1280]{1,0:T(8,128)(2,1)S(1)}, bf16[32,1280]{1,0:T(8,128)(2,1)S(1)}, u32[]{:S(2)}, u32[]{:S(2)}) collective-permute-start(bf16[32,1280]{1,0:T(8,128)(2,1)S(1)} %get-tuple-element.30), channel_id=1, source_target_pairs={{0,1},{1,2},{2,3},{3,0},{4,5},{5,6},{6,7},{7,4},{8,9},{9,10},{10,1... | collective-permute-start | bytes 245768 | tf_op jit(solution)/shard_map/ppermute | solution.py:39
  4.1 2.9 %collective-permute-start.1 = (bf16[32,1280]{1,0:T(8,128)(2,1)S(1)}, bf16[32,1280]{1,0:T(8,128)(2,1)S(1)}, u32[]{:S(2)}, u32[]{:S(2)}) collective-permute-start(bf16[32,1280]{1,0:T(8,128)(2,1)S(1)} %get-tuple-element.30), channel_id=1, source_target_pairs={{0,2},{1,3},{2,0},{3,1},{4,6},{5,7},{6,4},{7,5},{8,10},{9,11},{10,... | collective-permute-start | bytes 245768 | tf_op jit(solution)/shard_map/ppermute | solution.py:39
  7.0 1.3 %collective-permute-start.2 = (bf16[32,1280]{1,0:T(8,128)(2,1)S(1)}, bf16[32,1280]{1,0:T(8,128)(2,1)S(1)}, u32[]{:S(2)}, u32[]{:S(2)}) collective-permute-start(bf16[32,1280]{1,0:T(8,128)(2,1)S(1)} %get-tuple-element.30), channel_id=1, source_target_pairs={{0,3},{1,0},{2,1},{3,2},{4,7},{5,4},{6,5},{7,6},{8,11},{9,8},{10,9... | collective-permute-start | bytes 245768 | tf_op jit(solution)/shard_map/ppermute | solution.py:39
  8.4 1.9 %collective-permute-start.6 = (bf16[32,1280]{1,0:T(8,128)(2,1)S(1)}, bf16[32,1280]{1,0:T(8,128)(2,1)S(1)}, u32[]{:S(2)}, u32[]{:S(2)}) collective-permute-start(bf16[32,1280]{1,0:T(8,128)(2,1)S(1)} %get-tuple-element.28), channel_id=1, source_target_pairs={{0,4},{1,5},{2,6},{3,7},{4,8},{5,9},{6,10},{7,11},{8,12},{9,13},{1... | collective-permute-start | bytes 245768 | tf_op jit(solution)/shard_map/ppermute | solution.py:40
  10.3 3.6 %collective-permute-start.7 = (bf16[32,1280]{1,0:T(8,128)(2,1)S(1)}, bf16[32,1280]{1,0:T(8,128)(2,1)S(1)}, u32[]{:S(2)}, u32[]{:S(2)}) collective-permute-start(bf16[32,1280]{1,0:T(8,128)(2,1)S(1)} %get-tuple-element.28), channel_id=1, source_target_pairs={{0,8},{1,9},{2,10},{3,11},{4,12},{5,13},{6,14},{7,15},{8,0},{9,1},... | collective-permute-start | bytes 245768 | tf_op jit(solution)/shard_map/ppermute | solution.py:40
  13.9 0.7 add_convert_fusion
  14.5 0.8 select_reduce_fusion
  15.3 0.6 reduce-window.6
  15.9 0.2 slice_reduce_fusion
  16.3 0.7 fusion.48
  17.0 0.1 stack.98
  17.1 0.1 stack.99
  17.2 0.1 stack.97
  17.3 1.2 %concatenate.10 = bf16[256,1280]{1,0:T(8,128)(2,1)S(1)} concatenate(bf16[256,1152]{1,0:T(8,128)(2,1)} %param.8, bf16[256,1]{1,0:T(8,128)(2,1)S(1)} %broadcast_in_dim.34, bf16[256,1]{1,0:T(8,128)(2,1)S(1)} %stack.97, bf16[256,1]{1,0:T(8,128)(2,1)S(1)} %stack.98, bf16[256,1]{1,0:T(8,128)(2,1)S(1)} %stack.99, bf16[256,124]{1,0:T(8,128)(2,1)S(1)} %broadcast_in_dim.35), dimensions={1} | concatenate | bytes 1310720 | tf_op jit(solution)/shard_map/concatenate | solution.py:103
  18.5 1.8 %convolution_convert_fusion = bf16[512,1280]{1,0:T(8,128)(2,1)} fusion(bf16[256,1280]{1,0:T(8,128)(2,1)S(1)} %concatenate.10, s32[256]{0:T(256)S(1)} %multiply_add_fusion.1), kind=kOutput, calls=%fused_computation.2 | convolution fusion | flops 336330752 | bytes 1967104 | tf_op jit(solution)/shard_map/dot_general | solution.py:102
  20.3 4.3 %all-to-all-start = ((bf16[8,64,1280]{2,1,0:T(8,128)(2,1)}), bf16[8,64,1280]{2,1,0:T(8,128)(2,1)S(1)}, u32[]{:S(2)}, u32[]{:S(2)}) async-start(bf16[8,64,1280]{2,1,0:T(8,128)(2,1)} %bitcast.3), calls=%async_computation | async-start | bytes 2621440 | tf_op jit(solution)/shard_map/all_to_all | solution.py:106
  24.8 1.0 collective-permute-start.8
  25.8 0.8 fusion.55
  26.6 1.0 collective-permute-start.3
  27.6 0.5 collective-permute-start.4
  28.1 2.2 %collective-permute-start.5 = (bf16[4,32,1280]{2,1,0:T(8,128)(2,1)}, bf16[4,32,1280]{2,1,0:T(8,128)(2,1)S(1)}, u32[]{:S(2)}, u32[]{:S(2)}) collective-permute-start(bf16[4,32,1280]{2,1,0:T(8,128)(2,1)} %get-tuple-element.21), channel_id=1, source_target_pairs={{0,12},{1,13},{2,14},{3,15},{4,0},{5,1},{6,2},{7,3},{8,4},{9,5},{1... | collective-permute-start | bytes 983048 | tf_op jit(solution)/shard_map/ppermute | solution.py:48
  31.8 0.8 fusion.54
  32.6 0.7 collective-permute-start.9
  33.3 0.8 collective-permute-start.10
  34.1 10.8 %collective-permute-done.3 = bf16[4,32,1280]{2,1,0:T(8,128)(2,1)S(1)} collective-permute-done((bf16[4,32,1280]{2,1,0:T(8,128)(2,1)}, bf16[4,32,1280]{2,1,0:T(8,128)(2,1)S(1)}, u32[]{:S(2)}, u32[]{:S(2)}) %collective-permute-start.3) | collective-permute-done | bytes 327712 | tf_op jit(solution)/shard_map/ppermute | solution.py:48
  44.9 0.6 collective-permute-done.5
  45.5 1.2 %pad_maximum_fusion = bf16[4,4,32,1280]{3,2,1,0:T(8,128)(2,1)} fusion(bf16[1,4,32,1280]{3,2,1,0:T(8,128)(2,1)S(1)} %bitcast.108, bf16[1,4,32,1280]{3,2,1,0:T(8,128)(2,1)S(1)} %bitcast.107, bf16[1,4,32,1280]{3,2,1,0:T(8,128)(2,1)S(1)} %bitcast.106, bf16[1,4,32,1280]{3,2,1,0:T(8,128)(2,1)S(1)} %get-tuple-element.20), kind=kLoop, calls=%fused_computation.19 | loop fusion | flops 1966080 | bytes 2621440 | tf_op jit(solution)/shard_map/stack | solution.py:50
  46.7 0.9 slice_convert_fusion.1
  47.7 0.1 copy.28
  47.8 2.6 %collective-permute-done.9 = bf16[4,32,1280]{2,1,0:T(8,128)(2,1)S(1)} collective-permute-done((bf16[4,32,1280]{2,1,0:T(8,128)(2,1)}, bf16[4,32,1280]{2,1,0:T(8,128)(2,1)S(1)}, u32[]{:S(2)}, u32[]{:S(2)}) %collective-permute-start.9) | collective-permute-done | bytes 327712 | tf_op jit(solution)/shard_map/ppermute | solution.py:49
  50.4 3.9 %collective-permute-done.11 = bf16[4,32,1280]{2,1,0:T(8,128)(2,1)} collective-permute-done((bf16[4,32,1280]{2,1,0:T(8,128)(2,1)}, bf16[4,32,1280]{2,1,0:T(8,128)(2,1)}, u32[]{:S(2)}, u32[]{:S(2)}) %collective-permute-start.11) | collective-permute-done | bytes 327712 | tf_op jit(solution)/shard_map/ppermute | solution.py:49
  54.3 1.2 %pad_maximum_fusion.1 = bf16[4,4,32,1280]{3,2,1,0:T(8,128)(2,1)S(1)} fusion(bf16[1,4,32,1280]{3,2,1,0:T(8,128)(2,1)} %bitcast.24, bf16[1,4,32,1280]{3,2,1,0:T(8,128)(2,1)} %bitcast.23, bf16[1,4,32,1280]{3,2,1,0:T(8,128)(2,1)S(1)} %bitcast.109, bf16[1,4,32,1280]{3,2,1,0:T(8,128)(2,1)S(1)} %get-tuple-element.18), kind=kLoop, calls=%fused_computation.20 | loop fusion | flops 1966080 | bytes 2621440 | tf_op jit(solution)/shard_map/stack | solution.py:50
  55.6 0.1 copy.29
  55.7 0.1 slice_convert_fusion.2
  55.8 0.4 fusion.37
  56.2 2.7 %fusion.18 = bf16[512,512]{1,0:T(8,128)(2,1)S(1)} fusion(bf16[512,1280]{1,0:T(8,128)(2,1)} %bitcast.13, bf16[512,1280]{1,0:T(8,128)(2,1)S(1)} %bitcast.97, f32[]{:T(128)} %bitcast.92, f32[]{:T(128)} %bitcast.90, s32[512]{0:T(512)S(1)} %add.241, s32[512]{0:T(512)S(1)} %bitcast.119, s32[512]{0:T(512)S(1)} %get-tuple-element.7, s32[512]{0:T(512)S(1)} %get-tuple-element.6), kind=kOutput, calls=%fused_computation.24 | convolution fusion | flops 607387648 | bytes 2892800 | tf_op jit(solution)/shard_map/dot_general | solution.py:13
  58.9 0.9 fusion.60
  59.8 2.1 %fusion.21 = f32[512,1152]{1,0:T(8,128)S(1)} fusion(bf16[512,512]{1,0:T(8,128)(2,1)S(1)} %fusion.18, bf16[512,1280]{1,0:T(8,128)(2,1)} %bitcast.13), kind=kOutput, calls=%fused_computation.27 | convolution fusion | flops 603979776 | bytes 4063232 | tf_op jit(solution)/shard_map/dot_general | solution.py:134
  61.9 1.0 fusion.59
  62.9 2.0 %collective-permute-start.14 = (bf16[4,32,1152]{2,1,0:T(8,128)(2,1)}, bf16[4,32,1152]{2,1,0:T(8,128)(2,1)}, u32[]{:S(2)}, u32[]{:S(2)}) collective-permute-start(bf16[4,32,1152]{2,1,0:T(8,128)(2,1)} %bitcast.33), channel_id=1, source_target_pairs={{0,4},{1,5},{2,6},{3,7},{4,8},{5,9},{6,10},{7,11},{8,12},{9,13},{1... | collective-permute-start | bytes 884744 | tf_op jit(solution)/shard_map/ppermute | solution.py:58
  64.9 0.9 slice.144
  65.8 1.2 %fusion.16 = bf16[512,512]{1,0:T(8,128)(2,1)S(1)} fusion(bf16[512,1280]{1,0:T(8,128)(2,1)S(1)} %bitcast.102, bf16[512,1280]{1,0:T(8,128)(2,1)S(1)} %bitcast.99, s32[512]{0:T(512)S(1)} %add.253, s32[512]{0:T(512)S(1)} %bitcast.118, f32[]{:T(128)} %bitcast.93, f32[]{:T(128)} %bitcast.91, s32[512]{0:T(512)S(1)} %get-tuple-element.7, s32[512]{0:T(512)S(1)} %get-tuple-element.6), kind=kOutput, calls=%fused_computation.22 | convolution fusion | flops 607387648 | bytes 2891784 | tf_op jit(solution)/shard_map/dot_general | solution.py:13
  67.0 2.2 %fusion.26 = f32[512,1152]{1,0:T(8,128)S(1)} fusion(bf16[512,512]{1,0:T(8,128)(2,1)S(1)} %fusion.16, bf16[512,1280]{1,0:T(8,128)(2,1)} %bitcast.100), kind=kOutput, calls=%fused_computation.32 | convolution fusion | flops 603979776 | bytes 4063232 | tf_op jit(solution)/shard_map/dot_general | solution.py:19
  69.2 0.1 convert.39
  69.3 1.0 slice_bitcast_fusion.2
  70.3 1.5 %collective-permute-start.18 = (bf16[4,32,1152]{2,1,0:T(8,128)(2,1)}, bf16[4,32,1152]{2,1,0:T(8,128)(2,1)}, u32[]{:S(2)}, u32[]{:S(2)}) collective-permute-start(bf16[4,32,1152]{2,1,0:T(8,128)(2,1)} %get-tuple-element.15), channel_id=1, source_target_pairs={{0,3},{1,0},{2,1},{3,2},{4,7},{5,4},{6,5},{7,6},{8,11},{9,8},{10,9... | collective-permute-start | bytes 884744 | tf_op jit(solution)/shard_map/ppermute | solution.py:59
  71.8 1.1 %collective-permute-start.19 = (bf16[4,32,1152]{2,1,0:T(8,128)(2,1)}, bf16[4,32,1152]{2,1,0:T(8,128)(2,1)}, u32[]{:S(2)}, u32[]{:S(2)}) collective-permute-start(bf16[4,32,1152]{2,1,0:T(8,128)(2,1)} %get-tuple-element.17), channel_id=1, source_target_pairs={{0,2},{1,3},{2,0},{3,1},{4,6},{5,7},{6,4},{7,5},{8,10},{9,11},{10,... | collective-permute-start | bytes 884744 | tf_op jit(solution)/shard_map/ppermute | solution.py:59
  72.9 1.9 %fusion = bf16[512,1152]{1,0:T(8,128)(2,1)} fusion(f32[512,1152]{1,0:T(8,128)S(1)} %fusion.21, bf16[512,512]{1,0:T(8,128)(2,1)S(1)} %fusion.16, bf16[512,1280]{1,0:T(8,128)(2,1)S(1)} %bitcast.103), kind=kOutput, calls=%fused_computation.1 | convolution fusion | flops 605159424 | bytes 5242880 | tf_op jit(solution)/shard_map/dot_general | solution.py:135
  74.8 4.0 %all-to-all-start.1 = ((bf16[8,64,1152]{2,1,0:T(8,128)(2,1)}), bf16[8,64,1152]{2,1,0:T(8,128)(2,1)S(1)}, u32[]{:S(2)}, u32[]{:S(2)}) async-start(bf16[8,64,1152]{2,1,0:T(8,128)(2,1)} %bitcast.28), calls=%async_computation.1 | async-start | bytes 2359296 | tf_op jit(solution)/shard_map/all_to_all | solution.py:136
  78.9 1.4 %fusion.56 = (bf16[4,32,1152]{2,1,0:T(8,128)(2,1)S(1)}, f32[4,32,1152]{2,1,0:T(8,128)S(1)}) fusion(bf16[4,32,1152]{2,1,0:T(8,128)(2,1)} %collective-permute-done.14, bf16[4,32,1152]{2,1,0:T(8,128)(2,1)} %collective-permute-done.13, f32[4,32,1152]{2,1,0:T(8,128)} %bitcast.105, bf16[4,32,1152]{2,1,0:T(8,128)(2,1)} %collective-permute-done.12), kind=kLoop, calls=%fused_computation.113 | loop fusion | flops 1032192 | bytes 2359296 | tf_op jit(solution)/shard_map/convert.10
  80.4 3.3 %collective-permute-start.15 = (bf16[32,1152]{1,0:T(8,128)(2,1)S(1)}, bf16[32,1152]{1,0:T(8,128)(2,1)S(1)}, u32[]{:S(2)}, u32[]{:S(2)}) collective-permute-start(bf16[32,1152]{1,0:T(8,128)(2,1)S(1)} %get-tuple-element.22), channel_id=1, source_target_pairs={{0,3},{1,0},{2,1},{3,2},{4,7},{5,4},{6,5},{7,6},{8,11},{9,8},{10,9... | collective-permute-start | bytes 221192 | tf_op jit(solution)/shard_map/ppermute | solution.py:63
  83.7 1.2 %collective-permute-start.16 = (bf16[32,1152]{1,0:T(8,128)(2,1)S(1)}, bf16[32,1152]{1,0:T(8,128)(2,1)S(1)}, u32[]{:S(2)}, u32[]{:S(2)}) collective-permute-start(bf16[32,1152]{1,0:T(8,128)(2,1)S(1)} %get-tuple-element.24), channel_id=1, source_target_pairs={{0,2},{1,3},{2,0},{3,1},{4,6},{5,7},{6,4},{7,5},{8,10},{9,11},{10,... | collective-permute-start | bytes 221192 | tf_op jit(solution)/shard_map/ppermute | solution.py:63
  84.9 0.5 collective-permute-start.17
  85.4 6.1 %collective-permute-done.20 = bf16[4,32,1152]{2,1,0:T(8,128)(2,1)S(1)} collective-permute-done((bf16[4,32,1152]{2,1,0:T(8,128)(2,1)}, bf16[4,32,1152]{2,1,0:T(8,128)(2,1)S(1)}, u32[]{:S(2)}, u32[]{:S(2)}) %collective-permute-start.20) | collective-permute-done | bytes 294944 | tf_op jit(solution)/shard_map/ppermute | solution.py:59
  91.5 1.2 %fusion.57 = (bf16[4,32,1152]{2,1,0:T(8,128)(2,1)S(1)}, f32[4,32,1152]{2,1,0:T(8,128)S(1)}) fusion(bf16[4,32,1152]{2,1,0:T(8,128)(2,1)S(1)} %collective-permute-done.20, bf16[4,32,1152]{2,1,0:T(8,128)(2,1)} %collective-permute-done.19, bf16[4,32,1152]{2,1,0:T(8,128)(2,1)} %collective-permute-done.18, f32[4,4,32,1152]{3,2,1,0:T(8,128)S(1)} %bitcast.95), kind=kLoop, calls=%fused_computation.114 | loop fusion | flops 1032192 | bytes 2359296 | tf_op jit(solution)/shard_map/convert.4
  92.7 2.7 %collective-permute-start.21 = (bf16[32,1152]{1,0:T(8,128)(2,1)S(1)}, bf16[32,1152]{1,0:T(8,128)(2,1)S(1)}, u32[]{:S(2)}, u32[]{:S(2)}) collective-permute-start(bf16[32,1152]{1,0:T(8,128)(2,1)S(1)} %get-tuple-element.25), channel_id=1, source_target_pairs={{0,12},{1,13},{2,14},{3,15},{4,0},{5,1},{6,2},{7,3},{8,4},{9,5},{1... | collective-permute-start | bytes 221192 | tf_op jit(solution)/shard_map/ppermute | solution.py:64
  95.4 1.6 %collective-permute-start.22 = (bf16[32,1152]{1,0:T(8,128)(2,1)S(1)}, bf16[32,1152]{1,0:T(8,128)(2,1)S(1)}, u32[]{:S(2)}, u32[]{:S(2)}) collective-permute-start(bf16[32,1152]{1,0:T(8,128)(2,1)S(1)} %get-tuple-element.27), channel_id=1, source_target_pairs={{0,8},{1,9},{2,10},{3,11},{4,12},{5,13},{6,14},{7,15},{8,0},{9,1},... | collective-permute-start | bytes 221192 | tf_op jit(solution)/shard_map/ppermute | solution.py:64
  97.0 1.3 %collective-permute-start.23 = (bf16[32,1152]{1,0:T(8,128)(2,1)S(1)}, bf16[32,1152]{1,0:T(8,128)(2,1)S(1)}, u32[]{:S(2)}, u32[]{:S(2)}) collective-permute-start(bf16[32,1152]{1,0:T(8,128)(2,1)S(1)} %get-tuple-element.26), channel_id=1, source_target_pairs={{0,4},{1,5},{2,6},{3,7},{4,8},{5,9},{6,10},{7,11},{8,12},{9,13},{1... | collective-permute-start | bytes 221192 | tf_op jit(solution)/shard_map/ppermute | solution.py:64
  98.4 2.9 %collective-permute-done.22 = bf16[32,1152]{1,0:T(8,128)(2,1)S(1)} collective-permute-done((bf16[32,1152]{1,0:T(8,128)(2,1)S(1)}, bf16[32,1152]{1,0:T(8,128)(2,1)S(1)}, u32[]{:S(2)}, u32[]{:S(2)}) %collective-permute-start.22) | collective-permute-done | bytes 73760 | tf_op jit(solution)/shard_map/ppermute | solution.py:64
  101.3 1.3 %collective-permute-done.23 = bf16[32,1152]{1,0:T(8,128)(2,1)S(1)} collective-permute-done((bf16[32,1152]{1,0:T(8,128)(2,1)S(1)}, bf16[32,1152]{1,0:T(8,128)(2,1)S(1)}, u32[]{:S(2)}, u32[]{:S(2)}) %collective-permute-start.23) | collective-permute-done | bytes 73760 | tf_op jit(solution)/shard_map/ppermute | solution.py:64
  102.6 0.7 pad_maximum_fusion.4
  103.3 1.6 %fusion.32 = f32[256,1152]{1,0:T(8,128)} fusion(bf16[512,1152]{1,0:T(8,128)(2,1)S(1)} %bitcast.104, s32[256]{0:T(256)S(1)} %multiply_add_fusion.1), kind=kOutput, calls=%fused_computation.41 | convolution fusion | flops 302120960 | bytes 2360320 | tf_op jit(solution)/shard_map/dot_general | solution.py:137
  (48 shorter events, 0.9 us)
Async XLA Ops:
  2.4 22.4 %collective-permute-start = (bf16[32,1280]{1,0:T(8,128)(2,1)S(1)}, bf16[32,1280]{1,0:T(8,128)(2,1)S(1)}, u32[]{:S(2)}, u32[]{:S(2)}) collective-permute-start(bf16[32,1280]{1,0:T(8,128)(2,1)S(1)} %get-tuple-element.30), channel_id=1, source_target_pairs={{0,1},{1,2},{2,3},{3,0},{4,5},{5,6},{6,7},{7,4},{8,9},{9,10},{10,1... | collective-permute-start | bytes 245768 | tf_op jit(solution)/shard_map/ppermute | solution.py:39
  4.1 21.7 %collective-permute-start.1 = (bf16[32,1280]{1,0:T(8,128)(2,1)S(1)}, bf16[32,1280]{1,0:T(8,128)(2,1)S(1)}, u32[]{:S(2)}, u32[]{:S(2)}) collective-permute-start(bf16[32,1280]{1,0:T(8,128)(2,1)S(1)} %get-tuple-element.30), channel_id=1, source_target_pairs={{0,2},{1,3},{2,0},{3,1},{4,6},{5,7},{6,4},{7,5},{8,10},{9,11},{10,... | collective-permute-start | bytes 245768 | tf_op jit(solution)/shard_map/ppermute | solution.py:39
  7.0 18.8 %collective-permute-start.2 = (bf16[32,1280]{1,0:T(8,128)(2,1)S(1)}, bf16[32,1280]{1,0:T(8,128)(2,1)S(1)}, u32[]{:S(2)}, u32[]{:S(2)}) collective-permute-start(bf16[32,1280]{1,0:T(8,128)(2,1)S(1)} %get-tuple-element.30), channel_id=1, source_target_pairs={{0,3},{1,0},{2,1},{3,2},{4,7},{5,4},{6,5},{7,6},{8,11},{9,8},{10,9... | collective-permute-start | bytes 245768 | tf_op jit(solution)/shard_map/ppermute | solution.py:39
  8.4 19.7 %collective-permute-start.6 = (bf16[32,1280]{1,0:T(8,128)(2,1)S(1)}, bf16[32,1280]{1,0:T(8,128)(2,1)S(1)}, u32[]{:S(2)}, u32[]{:S(2)}) collective-permute-start(bf16[32,1280]{1,0:T(8,128)(2,1)S(1)} %get-tuple-element.28), channel_id=1, source_target_pairs={{0,4},{1,5},{2,6},{3,7},{4,8},{5,9},{6,10},{7,11},{8,12},{9,13},{1... | collective-permute-start | bytes 245768 | tf_op jit(solution)/shard_map/ppermute | solution.py:40
  10.3 21.6 %collective-permute-start.7 = (bf16[32,1280]{1,0:T(8,128)(2,1)S(1)}, bf16[32,1280]{1,0:T(8,128)(2,1)S(1)}, u32[]{:S(2)}, u32[]{:S(2)}) collective-permute-start(bf16[32,1280]{1,0:T(8,128)(2,1)S(1)} %get-tuple-element.28), channel_id=1, source_target_pairs={{0,8},{1,9},{2,10},{3,11},{4,12},{5,13},{6,14},{7,15},{8,0},{9,1},... | collective-permute-start | bytes 245768 | tf_op jit(solution)/shard_map/ppermute | solution.py:40
  20.3 35.4 %all-to-all-start = ((bf16[8,64,1280]{2,1,0:T(8,128)(2,1)}), bf16[8,64,1280]{2,1,0:T(8,128)(2,1)S(1)}, u32[]{:S(2)}, u32[]{:S(2)}) async-start(bf16[8,64,1280]{2,1,0:T(8,128)(2,1)} %bitcast.3), calls=%async_computation | async-start | bytes 2621440 | tf_op jit(solution)/shard_map/all_to_all | solution.py:106
  24.8 7.1 %collective-permute-start.8 = (bf16[32,1280]{1,0:T(8,128)(2,1)S(1)}, bf16[32,1280]{1,0:T(8,128)(2,1)S(1)}, u32[]{:S(2)}, u32[]{:S(2)}) collective-permute-start(bf16[32,1280]{1,0:T(8,128)(2,1)S(1)} %get-tuple-element.28), channel_id=1, source_target_pairs={{0,12},{1,13},{2,14},{3,15},{4,0},{5,1},{6,2},{7,3},{8,4},{9,5},{1... | collective-permute-start | bytes 245768 | tf_op jit(solution)/shard_map/ppermute | solution.py:40
  26.6 18.3 %collective-permute-start.3 = (bf16[4,32,1280]{2,1,0:T(8,128)(2,1)}, bf16[4,32,1280]{2,1,0:T(8,128)(2,1)S(1)}, u32[]{:S(2)}, u32[]{:S(2)}) collective-permute-start(bf16[4,32,1280]{2,1,0:T(8,128)(2,1)} %get-tuple-element.21), channel_id=1, source_target_pairs={{0,4},{1,5},{2,6},{3,7},{4,8},{5,9},{6,10},{7,11},{8,12},{9,13},{1... | collective-permute-start | bytes 983048 | tf_op jit(solution)/shard_map/ppermute | solution.py:48
  27.6 17.3 %collective-permute-start.4 = (bf16[4,32,1280]{2,1,0:T(8,128)(2,1)}, bf16[4,32,1280]{2,1,0:T(8,128)(2,1)S(1)}, u32[]{:S(2)}, u32[]{:S(2)}) collective-permute-start(bf16[4,32,1280]{2,1,0:T(8,128)(2,1)} %get-tuple-element.21), channel_id=1, source_target_pairs={{0,8},{1,9},{2,10},{3,11},{4,12},{5,13},{6,14},{7,15},{8,0},{9,1},... | collective-permute-start | bytes 983048 | tf_op jit(solution)/shard_map/ppermute | solution.py:48
  28.1 17.4 %collective-permute-start.5 = (bf16[4,32,1280]{2,1,0:T(8,128)(2,1)}, bf16[4,32,1280]{2,1,0:T(8,128)(2,1)S(1)}, u32[]{:S(2)}, u32[]{:S(2)}) collective-permute-start(bf16[4,32,1280]{2,1,0:T(8,128)(2,1)} %get-tuple-element.21), channel_id=1, source_target_pairs={{0,12},{1,13},{2,14},{3,15},{4,0},{5,1},{6,2},{7,3},{8,4},{9,5},{1... | collective-permute-start | bytes 983048 | tf_op jit(solution)/shard_map/ppermute | solution.py:48
  32.6 17.7 %collective-permute-start.9 = (bf16[4,32,1280]{2,1,0:T(8,128)(2,1)}, bf16[4,32,1280]{2,1,0:T(8,128)(2,1)S(1)}, u32[]{:S(2)}, u32[]{:S(2)}) collective-permute-start(bf16[4,32,1280]{2,1,0:T(8,128)(2,1)} %get-tuple-element.19), channel_id=1, source_target_pairs={{0,1},{1,2},{2,3},{3,0},{4,5},{5,6},{6,7},{7,4},{8,9},{9,10},{10,1... | collective-permute-start | bytes 983048 | tf_op jit(solution)/shard_map/ppermute | solution.py:49
  33.3 17.0 %collective-permute-start.10 = (bf16[4,32,1280]{2,1,0:T(8,128)(2,1)}, bf16[4,32,1280]{2,1,0:T(8,128)(2,1)}, u32[]{:S(2)}, u32[]{:S(2)}) collective-permute-start(bf16[4,32,1280]{2,1,0:T(8,128)(2,1)} %get-tuple-element.19), channel_id=1, source_target_pairs={{0,2},{1,3},{2,0},{3,1},{4,6},{5,7},{6,4},{7,5},{8,10},{9,11},{10,... | collective-permute-start | bytes 983048 | tf_op jit(solution)/shard_map/ppermute | solution.py:49
  44.9 9.4 %collective-permute-start.11 = (bf16[4,32,1280]{2,1,0:T(8,128)(2,1)}, bf16[4,32,1280]{2,1,0:T(8,128)(2,1)}, u32[]{:S(2)}, u32[]{:S(2)}) collective-permute-start(bf16[4,32,1280]{2,1,0:T(8,128)(2,1)} %get-tuple-element.19), channel_id=1, source_target_pairs={{0,3},{1,0},{2,1},{3,2},{4,7},{5,4},{6,5},{7,6},{8,11},{9,8},{10,9... | collective-permute-start | bytes 983048 | tf_op jit(solution)/shard_map/ppermute | solution.py:49
  55.5 10.3 %copy-start.1 = (bf16[4,4,32,1280]{3,2,1,0:T(8,128)(2,1)}, bf16[4,4,32,1280]{3,2,1,0:T(8,128)(2,1)S(1)}, u32[]{:S(2)}) copy-start(bf16[4,4,32,1280]{3,2,1,0:T(8,128)(2,1)S(1)} %pad_maximum_fusion.1) | copy-start | bytes 3932164
  55.7 10.1 %copy-start = (bf16[8,64,1280]{2,1,0:T(8,128)(2,1)}, bf16[8,64,1280]{2,1,0:T(8,128)(2,1)S(1)}, u32[]{:S(2)}) copy-start(bf16[8,64,1280]{2,1,0:T(8,128)(2,1)S(1)} %all-to-all-done) | copy-start | bytes 3932164
  62.9 15.9 %collective-permute-start.12 = (bf16[4,32,1152]{2,1,0:T(8,128)(2,1)}, bf16[4,32,1152]{2,1,0:T(8,128)(2,1)}, u32[]{:S(2)}, u32[]{:S(2)}) collective-permute-start(bf16[4,32,1152]{2,1,0:T(8,128)(2,1)} %bitcast.31), channel_id=1, source_target_pairs={{0,12},{1,13},{2,14},{3,15},{4,0},{5,1},{6,2},{7,3},{8,4},{9,5},{1... | collective-permute-start | bytes 884744 | tf_op jit(solution)/shard_map/ppermute | solution.py:58
  62.9 16.0 %collective-permute-start.13 = (bf16[4,32,1152]{2,1,0:T(8,128)(2,1)}, bf16[4,32,1152]{2,1,0:T(8,128)(2,1)}, u32[]{:S(2)}, u32[]{:S(2)}) collective-permute-start(bf16[4,32,1152]{2,1,0:T(8,128)(2,1)} %bitcast.32), channel_id=1, source_target_pairs={{0,8},{1,9},{2,10},{3,11},{4,12},{5,13},{6,14},{7,15},{8,0},{9,1},... | collective-permute-start | bytes 884744 | tf_op jit(solution)/shard_map/ppermute | solution.py:58
  62.9 16.0 %collective-permute-start.14 = (bf16[4,32,1152]{2,1,0:T(8,128)(2,1)}, bf16[4,32,1152]{2,1,0:T(8,128)(2,1)}, u32[]{:S(2)}, u32[]{:S(2)}) collective-permute-start(bf16[4,32,1152]{2,1,0:T(8,128)(2,1)} %bitcast.33), channel_id=1, source_target_pairs={{0,4},{1,5},{2,6},{3,7},{4,8},{5,9},{6,10},{7,11},{8,12},{9,13},{1... | collective-permute-start | bytes 884744 | tf_op jit(solution)/shard_map/ppermute | solution.py:58
  69.3 3.6 %copy-start.2 = (bf16[4,4,32,1280]{3,2,1,0:T(8,128)(2,1)S(1)}, bf16[4,4,32,1280]{3,2,1,0:T(8,128)(2,1)}, u32[]{:S(2)}) copy-start(bf16[4,4,32,1280]{3,2,1,0:T(8,128)(2,1)} %copy-done.1) | copy-start | bytes 3932164
  70.3 14.6 %collective-permute-start.18 = (bf16[4,32,1152]{2,1,0:T(8,128)(2,1)}, bf16[4,32,1152]{2,1,0:T(8,128)(2,1)}, u32[]{:S(2)}, u32[]{:S(2)}) collective-permute-start(bf16[4,32,1152]{2,1,0:T(8,128)(2,1)} %get-tuple-element.15), channel_id=1, source_target_pairs={{0,3},{1,0},{2,1},{3,2},{4,7},{5,4},{6,5},{7,6},{8,11},{9,8},{10,9... | collective-permute-start | bytes 884744 | tf_op jit(solution)/shard_map/ppermute | solution.py:59
  71.8 13.6 %collective-permute-start.19 = (bf16[4,32,1152]{2,1,0:T(8,128)(2,1)}, bf16[4,32,1152]{2,1,0:T(8,128)(2,1)}, u32[]{:S(2)}, u32[]{:S(2)}) collective-permute-start(bf16[4,32,1152]{2,1,0:T(8,128)(2,1)} %get-tuple-element.17), channel_id=1, source_target_pairs={{0,2},{1,3},{2,0},{3,1},{4,6},{5,7},{6,4},{7,5},{8,10},{9,11},{10,... | collective-permute-start | bytes 884744 | tf_op jit(solution)/shard_map/ppermute | solution.py:59
  74.8 28.5 %all-to-all-start.1 = ((bf16[8,64,1152]{2,1,0:T(8,128)(2,1)}), bf16[8,64,1152]{2,1,0:T(8,128)(2,1)S(1)}, u32[]{:S(2)}, u32[]{:S(2)}) async-start(bf16[8,64,1152]{2,1,0:T(8,128)(2,1)} %bitcast.28), calls=%async_computation.1 | async-start | bytes 2359296 | tf_op jit(solution)/shard_map/all_to_all | solution.py:136
  78.8 12.7 %collective-permute-start.20 = (bf16[4,32,1152]{2,1,0:T(8,128)(2,1)}, bf16[4,32,1152]{2,1,0:T(8,128)(2,1)S(1)}, u32[]{:S(2)}, u32[]{:S(2)}) collective-permute-start(bf16[4,32,1152]{2,1,0:T(8,128)(2,1)} %get-tuple-element.16), channel_id=1, source_target_pairs={{0,1},{1,2},{2,3},{3,0},{4,5},{5,6},{6,7},{7,4},{8,9},{9,10},{10,1... | collective-permute-start | bytes 884744 | tf_op jit(solution)/shard_map/ppermute | solution.py:59
  80.4 16.6 %collective-permute-start.15 = (bf16[32,1152]{1,0:T(8,128)(2,1)S(1)}, bf16[32,1152]{1,0:T(8,128)(2,1)S(1)}, u32[]{:S(2)}, u32[]{:S(2)}) collective-permute-start(bf16[32,1152]{1,0:T(8,128)(2,1)S(1)} %get-tuple-element.22), channel_id=1, source_target_pairs={{0,3},{1,0},{2,1},{3,2},{4,7},{5,4},{6,5},{7,6},{8,11},{9,8},{10,9... | collective-permute-start | bytes 221192 | tf_op jit(solution)/shard_map/ppermute | solution.py:63
  83.7 14.6 %collective-permute-start.16 = (bf16[32,1152]{1,0:T(8,128)(2,1)S(1)}, bf16[32,1152]{1,0:T(8,128)(2,1)S(1)}, u32[]{:S(2)}, u32[]{:S(2)}) collective-permute-start(bf16[32,1152]{1,0:T(8,128)(2,1)S(1)} %get-tuple-element.24), channel_id=1, source_target_pairs={{0,2},{1,3},{2,0},{3,1},{4,6},{5,7},{6,4},{7,5},{8,10},{9,11},{10,... | collective-permute-start | bytes 221192 | tf_op jit(solution)/shard_map/ppermute | solution.py:63
  84.9 13.5 %collective-permute-start.17 = (bf16[32,1152]{1,0:T(8,128)(2,1)S(1)}, bf16[32,1152]{1,0:T(8,128)(2,1)S(1)}, u32[]{:S(2)}, u32[]{:S(2)}) collective-permute-start(bf16[32,1152]{1,0:T(8,128)(2,1)S(1)} %get-tuple-element.23), channel_id=1, source_target_pairs={{0,1},{1,2},{2,3},{3,0},{4,5},{5,6},{6,7},{7,4},{8,9},{9,10},{10,1... | collective-permute-start | bytes 221192 | tf_op jit(solution)/shard_map/ppermute | solution.py:63
  92.7 5.7 %collective-permute-start.21 = (bf16[32,1152]{1,0:T(8,128)(2,1)S(1)}, bf16[32,1152]{1,0:T(8,128)(2,1)S(1)}, u32[]{:S(2)}, u32[]{:S(2)}) collective-permute-start(bf16[32,1152]{1,0:T(8,128)(2,1)S(1)} %get-tuple-element.25), channel_id=1, source_target_pairs={{0,12},{1,13},{2,14},{3,15},{4,0},{5,1},{6,2},{7,3},{8,4},{9,5},{1... | collective-permute-start | bytes 221192 | tf_op jit(solution)/shard_map/ppermute | solution.py:64
  95.4 5.9 %collective-permute-start.22 = (bf16[32,1152]{1,0:T(8,128)(2,1)S(1)}, bf16[32,1152]{1,0:T(8,128)(2,1)S(1)}, u32[]{:S(2)}, u32[]{:S(2)}) collective-permute-start(bf16[32,1152]{1,0:T(8,128)(2,1)S(1)} %get-tuple-element.27), channel_id=1, source_target_pairs={{0,8},{1,9},{2,10},{3,11},{4,12},{5,13},{6,14},{7,15},{8,0},{9,1},... | collective-permute-start | bytes 221192 | tf_op jit(solution)/shard_map/ppermute | solution.py:64
  97.0 5.6 %collective-permute-start.23 = (bf16[32,1152]{1,0:T(8,128)(2,1)S(1)}, bf16[32,1152]{1,0:T(8,128)(2,1)S(1)}, u32[]{:S(2)}, u32[]{:S(2)}) collective-permute-start(bf16[32,1152]{1,0:T(8,128)(2,1)S(1)} %get-tuple-element.26), channel_id=1, source_target_pairs={{0,4},{1,5},{2,6},{3,7},{4,8},{5,9},{6,10},{7,11},{8,12},{9,13},{1... | collective-permute-start | bytes 221192 | tf_op jit(solution)/shard_map/ppermute | solution.py:64

commit v3 on v2

--- a/solution.py
+++ b/solution.py
@@ -128,13 +128,13 @@
             logits, recv_positive[:, None] == ids[None, :], recv_bucket[:, None] == bucket_y[None, :]
         ))
         rows.append(rows_y)
-    partial_a = inner_cols(weights[0], recv_rows).reshape(nz, ny, half, width)
-    partial_b = inner_cols(weights[1], recv_rows).reshape(ny, nz, half, width)
-    weight_b, partial_b = lax.optimization_barrier((weights[1], partial_b))
     total = (jnp.dot(weights[0], rows[0], preferred_element_type=jnp.float32)
-             + jnp.dot(weight_b, rows[1], preferred_element_type=jnp.float32))
+             + jnp.dot(weights[1], rows[1], preferred_element_type=jnp.float32))
     returned = lax.all_to_all(total.astype(jnp.bfloat16), "grp", split_axis=0, concat_axis=0, tiled=True)
     clip_grad = jnp.dot(placer, returned, preferred_element_type=jnp.float32)
+    partial_a = inner_cols(weights[0], recv_rows).reshape(nz, ny, half, width)
+    weight_b, rows_b, total = lax.optimization_barrier((weights[1], recv_rows, total))
+    partial_b = inner_cols(weight_b, rows_b).reshape(ny, nz, half, width)
     grad_a, grad_b = reduce_pair(partial_a, partial_b, nz, ny)
     caption_grad = jnp.concatenate([grad_a, grad_b], axis=0)
     return (clip_grad, caption_grad)

time: 106 us -> 102 us (0.962)
  waiting for transfers between devices: 28.2 us -> 31.7 us
  matrix products: 14.3 us -> 11.5 us
  other arithmetic: 13.8 us -> 11.5 us
  starting transfers between devices: 41.3 us -> 39 us
    ppermute x3, starting transfers between devices: 4.98 us -> 2.61 us  [reduce_pair(): lax.ppermute(total_a[d].astype(low), 'mem', shift_pairs(nz, ny, -d, True))]
    ppermute x3, waiting for transfers between devices: 0.01 us -> 1.88 us  [reduce_pair(): lax.ppermute(blocks_a[d].astype(low), 'mem', shift_pairs(nz, ny, -d, False))]
    unnamed x8 -> x6, local copies, waits for them, and re-layouts: 0.23 us -> 1.71 us
    dot_general x1, matrix products: 2.13 us -> 0.84 us  [inner_body(): jnp.dot(weights[0], rows[0], preferred_element_type=jnp.float32)]
    dot_general x2, matrix products: 3.02 us -> 1.74 us  [inner_cols(): lax.dot_general(left, right, (((0,), (0,)), ((), ())), preferred_element_...]
    slice x1 -> x4, local copies, waits for them, and re-layouts: 0.21 us -> 1.27 us  [the longest x1 0.93 us: reduce_pair(): blocks_b[d].astype(low)]
    another operation x7 -> x6, other arithmetic: 4.76 us -> 4.35 us
  transfers between devices with their start and end apart: 26 -> 26, of which waited for: 7 -> 9; matrix products, arithmetic and copies ran while one was open for 22% -> 18% of each run, Pallas kernels for 0% -> 0%
where the time goes in v3:
time: 102 us
  starting transfers between devices  39 us (38%)
  waiting for transfers between devices  31.7 us (31%)
  other arithmetic  11.5 us (11%)
  matrix products  11.5 us (11%)
  local copies, waits for them, and re-layouts  5.79 us (6%)
  between operations  2.18 us (2%)
    ppermute x3, waiting for transfers between devices, gather_second(): parts_a.append(lax.ppermute(inner_a, 'mem', shift_pairs(nz, ny, d, False)))  11.4 us
    ppermute x3, waiting for transfers between devices, gather_second(): parts_b.append(lax.ppermute(inner_b, 'mem', shift_pairs(nz, ny, d, True)))  7.41 us
    ppermute x3, waiting for transfers between devices, reduce_pair(): lax.ppermute(blocks_b[d].astype(low), 'mem', shift_pairs(nz, ny, -d, True))  6.87 us
    ppermute x3, starting transfers between devices, gather_first(): parts_b.append(lax.ppermute(xb, 'mem', shift_pairs(nz, ny, d, False)))  6.52 us
    ppermute x3, starting transfers between devices, gather_first(): parts_a.append(lax.ppermute(xa, 'mem', shift_pairs(nz, ny, d, True)))  6.01 us
    ppermute x3, starting transfers between devices, reduce_pair(): lax.ppermute(total_b[d].astype(low), 'mem', shift_pairs(nz, ny, -d, False))  5.62 us
    another operation x6, other arithmetic  4.35 us
    all_to_all x1, starting transfers between devices, inner_body(): lax.all_to_all(send_rows, 'grp', split_axis=0, concat_axis=0, tiled=True)  4.3 us
  transfers between devices with their start and end apart: 26, of which 9 were waited for; matrix products, arithmetic and copies ran while one was open for 18% of the time, Pallas kernels for 0%

profile of v3, /device:TPU:0, one launch (start us, length us, event | category | flops | bytes accessed | tf_op | source)
XLA Modules:
  0.0 101.7 jit_solution(4283236769155346311)
XLA Ops:
  0.6 0.7 convert_element_type.135
  1.4 1.0 pad_maximum_fusion.5
  2.4 1.8 %collective-permute-start = (bf16[32,1280]{1,0:T(8,128)(2,1)S(1)}, bf16[32,1280]{1,0:T(8,128)(2,1)S(1)}, u32[]{:S(2)}, u32[]{:S(2)}) collective-permute-start(bf16[32,1280]{1,0:T(8,128)(2,1)S(1)} %get-tuple-element.30), channel_id=1, source_target_pairs={{0,1},{1,2},{2,3},{3,0},{4,5},{5,6},{6,7},{7,4},{8,9},{9,10},{10,1... | collective-permute-start | bytes 245768 | tf_op jit(solution)/shard_map/ppermute | solution.py:39
  4.1 2.9 %collective-permute-start.1 = (bf16[32,1280]{1,0:T(8,128)(2,1)S(1)}, bf16[32,1280]{1,0:T(8,128)(2,1)S(1)}, u32[]{:S(2)}, u32[]{:S(2)}) collective-permute-start(bf16[32,1280]{1,0:T(8,128)(2,1)S(1)} %get-tuple-element.30), channel_id=1, source_target_pairs={{0,2},{1,3},{2,0},{3,1},{4,6},{5,7},{6,4},{7,5},{8,10},{9,11},{10,... | collective-permute-start | bytes 245768 | tf_op jit(solution)/shard_map/ppermute | solution.py:39
  7.0 1.3 %collective-permute-start.2 = (bf16[32,1280]{1,0:T(8,128)(2,1)S(1)}, bf16[32,1280]{1,0:T(8,128)(2,1)S(1)}, u32[]{:S(2)}, u32[]{:S(2)}) collective-permute-start(bf16[32,1280]{1,0:T(8,128)(2,1)S(1)} %get-tuple-element.30), channel_id=1, source_target_pairs={{0,3},{1,0},{2,1},{3,2},{4,7},{5,4},{6,5},{7,6},{8,11},{9,8},{10,9... | collective-permute-start | bytes 245768 | tf_op jit(solution)/shard_map/ppermute | solution.py:39
  8.4 1.9 %collective-permute-start.6 = (bf16[32,1280]{1,0:T(8,128)(2,1)S(1)}, bf16[32,1280]{1,0:T(8,128)(2,1)S(1)}, u32[]{:S(2)}, u32[]{:S(2)}) collective-permute-start(bf16[32,1280]{1,0:T(8,128)(2,1)S(1)} %get-tuple-element.28), channel_id=1, source_target_pairs={{0,4},{1,5},{2,6},{3,7},{4,8},{5,9},{6,10},{7,11},{8,12},{9,13},{1... | collective-permute-start | bytes 245768 | tf_op jit(solution)/shard_map/ppermute | solution.py:40
  10.3 3.6 %collective-permute-start.7 = (bf16[32,1280]{1,0:T(8,128)(2,1)S(1)}, bf16[32,1280]{1,0:T(8,128)(2,1)S(1)}, u32[]{:S(2)}, u32[]{:S(2)}) collective-permute-start(bf16[32,1280]{1,0:T(8,128)(2,1)S(1)} %get-tuple-element.28), channel_id=1, source_target_pairs={{0,8},{1,9},{2,10},{3,11},{4,12},{5,13},{6,14},{7,15},{8,0},{9,1},... | collective-permute-start | bytes 245768 | tf_op jit(solution)/shard_map/ppermute | solution.py:40
  13.9 0.7 add_convert_fusion
  14.5 0.8 select_reduce_fusion
  15.3 0.6 reduce-window.6
  15.9 0.2 slice_reduce_fusion
  16.3 0.7 fusion.39
  17.0 0.1 stack.98
  17.1 0.1 stack.99
  17.2 0.1 stack.97
  17.3 1.2 %concatenate.10 = bf16[256,1280]{1,0:T(8,128)(2,1)S(1)} concatenate(bf16[256,1152]{1,0:T(8,128)(2,1)} %param.8, bf16[256,1]{1,0:T(8,128)(2,1)S(1)} %broadcast_in_dim.34, bf16[256,1]{1,0:T(8,128)(2,1)S(1)} %stack.97, bf16[256,1]{1,0:T(8,128)(2,1)S(1)} %stack.98, bf16[256,1]{1,0:T(8,128)(2,1)S(1)} %stack.99, bf16[256,124]{1,0:T(8,128)(2,1)S(1)} %broadcast_in_dim.35), dimensions={1} | concatenate | bytes 1310720 | tf_op jit(solution)/shard_map/concatenate | solution.py:103
  18.6 1.8 %convolution_convert_fusion = bf16[512,1280]{1,0:T(8,128)(2,1)} fusion(bf16[256,1280]{1,0:T(8,128)(2,1)S(1)} %concatenate.10, s32[256]{0:T(256)S(1)} %multiply_add_fusion.1), kind=kOutput, calls=%fused_computation.1 | convolution fusion | flops 336330752 | bytes 1967104 | tf_op jit(solution)/shard_map/dot_general | solution.py:102
  20.3 4.3 %all-to-all-start = ((bf16[8,64,1280]{2,1,0:T(8,128)(2,1)}), bf16[8,64,1280]{2,1,0:T(8,128)(2,1)S(1)}, u32[]{:S(2)}, u32[]{:S(2)}) async-start(bf16[8,64,1280]{2,1,0:T(8,128)(2,1)} %bitcast.3), calls=%async_computation | async-start | bytes 2621440 | tf_op jit(solution)/shard_map/all_to_all | solution.py:106
  24.8 1.0 %collective-permute-start.8 = (bf16[32,1280]{1,0:T(8,128)(2,1)S(1)}, bf16[32,1280]{1,0:T(8,128)(2,1)S(1)}, u32[]{:S(2)}, u32[]{:S(2)}) collective-permute-start(bf16[32,1280]{1,0:T(8,128)(2,1)S(1)} %get-tuple-element.28), channel_id=1, source_target_pairs={{0,12},{1,13},{2,14},{3,15},{4,0},{5,1},{6,2},{7,3},{8,4},{9,5},{1... | collective-permute-start | bytes 245768 | tf_op jit(solution)/shard_map/ppermute | solution.py:40
  25.8 0.8 fusion.46
  26.6 1.0 collective-permute-start.3
  27.6 0.5 collective-permute-start.4
  28.1 2.2 %collective-permute-start.5 = (bf16[4,32,1280]{2,1,0:T(8,128)(2,1)}, bf16[4,32,1280]{2,1,0:T(8,128)(2,1)S(1)}, u32[]{:S(2)}, u32[]{:S(2)}) collective-permute-start(bf16[4,32,1280]{2,1,0:T(8,128)(2,1)} %get-tuple-element.21), channel_id=1, source_target_pairs={{0,12},{1,13},{2,14},{3,15},{4,0},{5,1},{6,2},{7,3},{8,4},{9,5},{1... | collective-permute-start | bytes 983048 | tf_op jit(solution)/shard_map/ppermute | solution.py:48
  31.8 0.8 fusion.45
  32.7 0.7 collective-permute-start.9
  33.3 0.8 collective-permute-start.10
  34.1 10.8 %collective-permute-done.3 = bf16[4,32,1280]{2,1,0:T(8,128)(2,1)S(1)} collective-permute-done((bf16[4,32,1280]{2,1,0:T(8,128)(2,1)}, bf16[4,32,1280]{2,1,0:T(8,128)(2,1)S(1)}, u32[]{:S(2)}, u32[]{:S(2)}) %collective-permute-start.3) | collective-permute-done | bytes 327712 | tf_op jit(solution)/shard_map/ppermute | solution.py:48
  44.9 0.6 collective-permute-done.5
  45.5 0.2 pad_maximum_fusion
  45.7 1.1 %copy-done = bf16[4,4,32,1280]{3,2,1,0:T(8,128)(2,1)} copy-done((bf16[4,4,32,1280]{3,2,1,0:T(8,128)(2,1)}, bf16[4,4,32,1280]{3,2,1,0:T(8,128)(2,1)S(1)}, u32[]{:S(2)}) %copy-start) | copy-done | bytes 1310744
  46.8 0.1 copy.28
  46.9 3.5 %collective-permute-done.9 = bf16[4,32,1280]{2,1,0:T(8,128)(2,1)S(1)} collective-permute-done((bf16[4,32,1280]{2,1,0:T(8,128)(2,1)}, bf16[4,32,1280]{2,1,0:T(8,128)(2,1)S(1)}, u32[]{:S(2)}, u32[]{:S(2)}) %collective-permute-start.9) | collective-permute-done | bytes 327712 | tf_op jit(solution)/shard_map/ppermute | solution.py:49
  50.4 3.9 %collective-permute-done.11 = bf16[4,32,1280]{2,1,0:T(8,128)(2,1)} collective-permute-done((bf16[4,32,1280]{2,1,0:T(8,128)(2,1)}, bf16[4,32,1280]{2,1,0:T(8,128)(2,1)}, u32[]{:S(2)}, u32[]{:S(2)}) %collective-permute-start.11) | collective-permute-done | bytes 327712 | tf_op jit(solution)/shard_map/ppermute | solution.py:49
  54.3 1.2 %pad_maximum_fusion.1 = bf16[4,4,32,1280]{3,2,1,0:T(8,128)(2,1)S(1)} fusion(bf16[1,4,32,1280]{3,2,1,0:T(8,128)(2,1)} %bitcast.24, bf16[1,4,32,1280]{3,2,1,0:T(8,128)(2,1)} %bitcast.23, bf16[1,4,32,1280]{3,2,1,0:T(8,128)(2,1)S(1)} %bitcast.102, bf16[1,4,32,1280]{3,2,1,0:T(8,128)(2,1)S(1)} %get-tuple-element.18), kind=kLoop, calls=%fused_computation.19 | loop fusion | flops 1966080 | bytes 2621440 | tf_op jit(solution)/shard_map/stack | solution.py:50
  55.6 0.1 copy.29
  55.7 0.1 slice_convert_fusion.2
  55.8 0.4 fusion.28
  56.2 2.5 %fusion.17 = bf16[512,512]{1,0:T(8,128)(2,1)S(1)} fusion(bf16[512,1280]{1,0:T(8,128)(2,1)} %bitcast.94, f32[]{:T(128)} %bitcast.83, f32[]{:T(128)} %bitcast.81, s32[512]{0:T(512)S(1)} %add.241, s32[512]{0:T(512)S(1)} %bitcast.112, s32[512]{0:T(512)S(1)} %get-tuple-element.7, s32[512]{0:T(512)S(1)} %get-tuple-element.6, bf16[512,1280]{1,0:T(8,128)(2,1)S(1)} %bitcast.86), kind=kOutput, calls=%fused_computation.23 | convolution fusion | flops 607387648 | bytes 2892800 | tf_op jit(solution)/shard_map/dot_general | solution.py:13
  58.7 0.9 fusion.56
  59.6 0.4 copy-done.1
  60.0 0.8 fusion.20
  60.9 1.0 fusion.53
  61.9 2.0 %collective-permute-start.14 = (bf16[4,32,1152]{2,1,0:T(8,128)(2,1)}, bf16[4,32,1152]{2,1,0:T(8,128)(2,1)}, u32[]{:S(2)}, u32[]{:S(2)}) collective-permute-start(bf16[4,32,1152]{2,1,0:T(8,128)(2,1)} %bitcast.32), channel_id=1, source_target_pairs={{0,4},{1,5},{2,6},{3,7},{4,8},{5,9},{6,10},{7,11},{8,12},{9,13},{1... | collective-permute-start | bytes 884744 | tf_op jit(solution)/shard_map/ppermute | solution.py:58
  64.0 1.2 %fusion.15 = bf16[512,512]{1,0:T(8,128)(2,1)S(1)} fusion(bf16[512,1280]{1,0:T(8,128)(2,1)S(1)} %bitcast.91, s32[512]{0:T(512)S(1)} %add.253, s32[512]{0:T(512)S(1)} %bitcast.111, f32[]{:T(128)} %bitcast.84, f32[]{:T(128)} %bitcast.82, s32[512]{0:T(512)S(1)} %get-tuple-element.7, s32[512]{0:T(512)S(1)} %get-tuple-element.6, bf16[512,1280]{1,0:T(8,128)(2,1)S(1)} %bitcast.89), kind=kOutput, calls=%fused_computation.21 | convolution fusion | flops 607387648 | bytes 2891784 | tf_op jit(solution)/shard_map/dot_general | solution.py:13
  65.2 1.9 %convolution_add_fusion = bf16[512,1152]{1,0:T(8,128)(2,1)} fusion(f32[512,1152]{1,0:T(8,128)S(1)} %fusion.20, bf16[512,512]{1,0:T(8,128)(2,1)S(1)} %fusion.15, bf16[512,1280]{1,0:T(8,128)(2,1)S(1)} %bitcast.92), kind=kOutput, calls=%fused_computation | convolution fusion | flops 605159424 | bytes 5242880 | tf_op jit(solution)/shard_map/dot_general | solution.py:132
  67.1 0.9 fusion.55
  67.9 0.9 fusion.54
  68.9 1.5 %collective-permute-start.18 = (bf16[4,32,1152]{2,1,0:T(8,128)(2,1)}, bf16[4,32,1152]{2,1,0:T(8,128)(2,1)}, u32[]{:S(2)}, u32[]{:S(2)}) collective-permute-start(bf16[4,32,1152]{2,1,0:T(8,128)(2,1)} %bitcast.38), channel_id=1, source_target_pairs={{0,3},{1,0},{2,1},{3,2},{4,7},{5,4},{6,5},{7,6},{8,11},{9,8},{10,9... | collective-permute-start | bytes 884744 | tf_op jit(solution)/shard_map/ppermute | solution.py:59
  70.4 1.1 %collective-permute-start.19 = (bf16[4,32,1152]{2,1,0:T(8,128)(2,1)}, bf16[4,32,1152]{2,1,0:T(8,128)(2,1)}, u32[]{:S(2)}, u32[]{:S(2)}) collective-permute-start(bf16[4,32,1152]{2,1,0:T(8,128)(2,1)} %bitcast.39), channel_id=1, source_target_pairs={{0,2},{1,3},{2,0},{3,1},{4,6},{5,7},{6,4},{7,5},{8,10},{9,11},{10,... | collective-permute-start | bytes 884744 | tf_op jit(solution)/shard_map/ppermute | solution.py:59
  71.6 4.0 %all-to-all-start.1 = ((bf16[8,64,1152]{2,1,0:T(8,128)(2,1)}), bf16[8,64,1152]{2,1,0:T(8,128)(2,1)S(1)}, u32[]{:S(2)}, u32[]{:S(2)}) async-start(bf16[8,64,1152]{2,1,0:T(8,128)(2,1)} %bitcast.27), calls=%async_computation.1 | async-start | bytes 2359296 | tf_op jit(solution)/shard_map/all_to_all | solution.py:133
  75.7 1.9 %collective-permute-done.14 = bf16[4,32,1152]{2,1,0:T(8,128)(2,1)} collective-permute-done((bf16[4,32,1152]{2,1,0:T(8,128)(2,1)}, bf16[4,32,1152]{2,1,0:T(8,128)(2,1)}, u32[]{:S(2)}, u32[]{:S(2)}) %collective-permute-start.14) | collective-permute-done | bytes 294944 | tf_op jit(solution)/shard_map/ppermute | solution.py:58
  77.6 1.2 %fusion.51 = (bf16[4,32,1152]{2,1,0:T(8,128)(2,1)S(1)}, f32[4,32,1152]{2,1,0:T(8,128)S(1)}) fusion(bf16[4,32,1152]{2,1,0:T(8,128)(2,1)} %collective-permute-done.14, bf16[4,32,1152]{2,1,0:T(8,128)(2,1)} %collective-permute-done.13, f32[4,32,1152]{2,1,0:T(8,128)S(1)} %bitcast.98, bf16[4,32,1152]{2,1,0:T(8,128)(2,1)S(1)} %collective-permute-done.12), kind=kLoop, calls=%fused_computation.105 | loop fusion | flops 1032192 | bytes 2359296 | tf_op jit(solution)/shard_map/convert.10
  78.8 1.8 %collective-permute-start.15 = (bf16[32,1152]{1,0:T(8,128)(2,1)S(1)}, bf16[32,1152]{1,0:T(8,128)(2,1)S(1)}, u32[]{:S(2)}, u32[]{:S(2)}) collective-permute-start(bf16[32,1152]{1,0:T(8,128)(2,1)S(1)} %get-tuple-element.22), channel_id=1, source_target_pairs={{0,3},{1,0},{2,1},{3,2},{4,7},{5,4},{6,5},{7,6},{8,11},{9,8},{10,9... | collective-permute-start | bytes 221192 | tf_op jit(solution)/shard_map/ppermute | solution.py:63
  80.6 0.8 collective-permute-start.16
  81.4 0.9 collective-permute-done.18
  82.3 6.0 %collective-permute-done.20 = bf16[4,32,1152]{2,1,0:T(8,128)(2,1)S(1)} collective-permute-done((bf16[4,32,1152]{2,1,0:T(8,128)(2,1)}, bf16[4,32,1152]{2,1,0:T(8,128)(2,1)S(1)}, u32[]{:S(2)}, u32[]{:S(2)}) %collective-permute-start.20) | collective-permute-done | bytes 294944 | tf_op jit(solution)/shard_map/ppermute | solution.py:59
  88.3 1.2 %fusion.52 = (bf16[4,32,1152]{2,1,0:T(8,128)(2,1)S(1)}, f32[4,32,1152]{2,1,0:T(8,128)S(1)}) fusion(bf16[4,32,1152]{2,1,0:T(8,128)(2,1)S(1)} %collective-permute-done.20, bf16[4,32,1152]{2,1,0:T(8,128)(2,1)} %collective-permute-done.19, f32[4,32,1152]{2,1,0:T(8,128)S(1)} %bitcast.97, bf16[4,32,1152]{2,1,0:T(8,128)(2,1)} %collective-permute-done.18), kind=kLoop, calls=%fused_computation.106 | loop fusion | flops 1032192 | bytes 2359296 | tf_op jit(solution)/shard_map/convert.4
  89.5 2.7 %collective-permute-start.21 = (bf16[32,1152]{1,0:T(8,128)(2,1)S(1)}, bf16[32,1152]{1,0:T(8,128)(2,1)S(1)}, u32[]{:S(2)}, u32[]{:S(2)}) collective-permute-start(bf16[32,1152]{1,0:T(8,128)(2,1)S(1)} %get-tuple-element.25), channel_id=1, source_target_pairs={{0,12},{1,13},{2,14},{3,15},{4,0},{5,1},{6,2},{7,3},{8,4},{9,5},{1... | collective-permute-start | bytes 221192 | tf_op jit(solution)/shard_map/ppermute | solution.py:64
  92.2 1.6 %collective-permute-start.22 = (bf16[32,1152]{1,0:T(8,128)(2,1)S(1)}, bf16[32,1152]{1,0:T(8,128)(2,1)S(1)}, u32[]{:S(2)}, u32[]{:S(2)}) collective-permute-start(bf16[32,1152]{1,0:T(8,128)(2,1)S(1)} %get-tuple-element.27), channel_id=1, source_target_pairs={{0,8},{1,9},{2,10},{3,11},{4,12},{5,13},{6,14},{7,15},{8,0},{9,1},... | collective-permute-start | bytes 221192 | tf_op jit(solution)/shard_map/ppermute | solution.py:64
  93.8 1.3 %collective-permute-start.23 = (bf16[32,1152]{1,0:T(8,128)(2,1)S(1)}, bf16[32,1152]{1,0:T(8,128)(2,1)S(1)}, u32[]{:S(2)}, u32[]{:S(2)}) collective-permute-start(bf16[32,1152]{1,0:T(8,128)(2,1)S(1)} %get-tuple-element.26), channel_id=1, source_target_pairs={{0,4},{1,5},{2,6},{3,7},{4,8},{5,9},{6,10},{7,11},{8,12},{9,13},{1... | collective-permute-start | bytes 221192 | tf_op jit(solution)/shard_map/ppermute | solution.py:64
  95.2 2.9 %collective-permute-done.22 = bf16[32,1152]{1,0:T(8,128)(2,1)S(1)} collective-permute-done((bf16[32,1152]{1,0:T(8,128)(2,1)S(1)}, bf16[32,1152]{1,0:T(8,128)(2,1)S(1)}, u32[]{:S(2)}, u32[]{:S(2)}) %collective-permute-start.22) | collective-permute-done | bytes 73760 | tf_op jit(solution)/shard_map/ppermute | solution.py:64
  98.1 1.3 %collective-permute-done.23 = bf16[32,1152]{1,0:T(8,128)(2,1)S(1)} collective-permute-done((bf16[32,1152]{1,0:T(8,128)(2,1)S(1)}, bf16[32,1152]{1,0:T(8,128)(2,1)S(1)}, u32[]{:S(2)}, u32[]{:S(2)}) %collective-permute-start.23) | collective-permute-done | bytes 73760 | tf_op jit(solution)/shard_map/ppermute | solution.py:64
  99.4 0.7 pad_maximum_fusion.4
  100.1 1.6 %fusion.23 = f32[256,1152]{1,0:T(8,128)} fusion(bf16[512,1152]{1,0:T(8,128)(2,1)S(1)} %bitcast.96, s32[256]{0:T(256)S(1)} %multiply_add_fusion.1), kind=kOutput, calls=%fused_computation.32 | convolution fusion | flops 302120960 | bytes 2360320 | tf_op jit(solution)/shard_map/dot_general | solution.py:134
  (47 shorter events, 1.1 us)
Async XLA Ops:
  2.4 22.4 %collective-permute-start = (bf16[32,1280]{1,0:T(8,128)(2,1)S(1)}, bf16[32,1280]{1,0:T(8,128)(2,1)S(1)}, u32[]{:S(2)}, u32[]{:S(2)}) collective-permute-start(bf16[32,1280]{1,0:T(8,128)(2,1)S(1)} %get-tuple-element.30), channel_id=1, source_target_pairs={{0,1},{1,2},{2,3},{3,0},{4,5},{5,6},{6,7},{7,4},{8,9},{9,10},{10,1... | collective-permute-start | bytes 245768 | tf_op jit(solution)/shard_map/ppermute | solution.py:39
  4.1 21.7 %collective-permute-start.1 = (bf16[32,1280]{1,0:T(8,128)(2,1)S(1)}, bf16[32,1280]{1,0:T(8,128)(2,1)S(1)}, u32[]{:S(2)}, u32[]{:S(2)}) collective-permute-start(bf16[32,1280]{1,0:T(8,128)(2,1)S(1)} %get-tuple-element.30), channel_id=1, source_target_pairs={{0,2},{1,3},{2,0},{3,1},{4,6},{5,7},{6,4},{7,5},{8,10},{9,11},{10,... | collective-permute-start | bytes 245768 | tf_op jit(solution)/shard_map/ppermute | solution.py:39
  7.0 18.8 %collective-permute-start.2 = (bf16[32,1280]{1,0:T(8,128)(2,1)S(1)}, bf16[32,1280]{1,0:T(8,128)(2,1)S(1)}, u32[]{:S(2)}, u32[]{:S(2)}) collective-permute-start(bf16[32,1280]{1,0:T(8,128)(2,1)S(1)} %get-tuple-element.30), channel_id=1, source_target_pairs={{0,3},{1,0},{2,1},{3,2},{4,7},{5,4},{6,5},{7,6},{8,11},{9,8},{10,9... | collective-permute-start | bytes 245768 | tf_op jit(solution)/shard_map/ppermute | solution.py:39
  8.4 19.7 %collective-permute-start.6 = (bf16[32,1280]{1,0:T(8,128)(2,1)S(1)}, bf16[32,1280]{1,0:T(8,128)(2,1)S(1)}, u32[]{:S(2)}, u32[]{:S(2)}) collective-permute-start(bf16[32,1280]{1,0:T(8,128)(2,1)S(1)} %get-tuple-element.28), channel_id=1, source_target_pairs={{0,4},{1,5},{2,6},{3,7},{4,8},{5,9},{6,10},{7,11},{8,12},{9,13},{1... | collective-permute-start | bytes 245768 | tf_op jit(solution)/shard_map/ppermute | solution.py:40
  10.3 21.6 %collective-permute-start.7 = (bf16[32,1280]{1,0:T(8,128)(2,1)S(1)}, bf16[32,1280]{1,0:T(8,128)(2,1)S(1)}, u32[]{:S(2)}, u32[]{:S(2)}) collective-permute-start(bf16[32,1280]{1,0:T(8,128)(2,1)S(1)} %get-tuple-element.28), channel_id=1, source_target_pairs={{0,8},{1,9},{2,10},{3,11},{4,12},{5,13},{6,14},{7,15},{8,0},{9,1},... | collective-permute-start | bytes 245768 | tf_op jit(solution)/shard_map/ppermute | solution.py:40
  20.3 35.4 %all-to-all-start = ((bf16[8,64,1280]{2,1,0:T(8,128)(2,1)}), bf16[8,64,1280]{2,1,0:T(8,128)(2,1)S(1)}, u32[]{:S(2)}, u32[]{:S(2)}) async-start(bf16[8,64,1280]{2,1,0:T(8,128)(2,1)} %bitcast.3), calls=%async_computation | async-start | bytes 2621440 | tf_op jit(solution)/shard_map/all_to_all | solution.py:106
  24.8 7.1 %collective-permute-start.8 = (bf16[32,1280]{1,0:T(8,128)(2,1)S(1)}, bf16[32,1280]{1,0:T(8,128)(2,1)S(1)}, u32[]{:S(2)}, u32[]{:S(2)}) collective-permute-start(bf16[32,1280]{1,0:T(8,128)(2,1)S(1)} %get-tuple-element.28), channel_id=1, source_target_pairs={{0,12},{1,13},{2,14},{3,15},{4,0},{5,1},{6,2},{7,3},{8,4},{9,5},{1... | collective-permute-start | bytes 245768 | tf_op jit(solution)/shard_map/ppermute | solution.py:40
  26.6 18.3 %collective-permute-start.3 = (bf16[4,32,1280]{2,1,0:T(8,128)(2,1)}, bf16[4,32,1280]{2,1,0:T(8,128)(2,1)S(1)}, u32[]{:S(2)}, u32[]{:S(2)}) collective-permute-start(bf16[4,32,1280]{2,1,0:T(8,128)(2,1)} %get-tuple-element.21), channel_id=1, source_target_pairs={{0,4},{1,5},{2,6},{3,7},{4,8},{5,9},{6,10},{7,11},{8,12},{9,13},{1... | collective-permute-start | bytes 983048 | tf_op jit(solution)/shard_map/ppermute | solution.py:48
  27.6 17.3 %collective-permute-start.4 = (bf16[4,32,1280]{2,1,0:T(8,128)(2,1)}, bf16[4,32,1280]{2,1,0:T(8,128)(2,1)S(1)}, u32[]{:S(2)}, u32[]{:S(2)}) collective-permute-start(bf16[4,32,1280]{2,1,0:T(8,128)(2,1)} %get-tuple-element.21), channel_id=1, source_target_pairs={{0,8},{1,9},{2,10},{3,11},{4,12},{5,13},{6,14},{7,15},{8,0},{9,1},... | collective-permute-start | bytes 983048 | tf_op jit(solution)/shard_map/ppermute | solution.py:48
  28.1 17.4 %collective-permute-start.5 = (bf16[4,32,1280]{2,1,0:T(8,128)(2,1)}, bf16[4,32,1280]{2,1,0:T(8,128)(2,1)S(1)}, u32[]{:S(2)}, u32[]{:S(2)}) collective-permute-start(bf16[4,32,1280]{2,1,0:T(8,128)(2,1)} %get-tuple-element.21), channel_id=1, source_target_pairs={{0,12},{1,13},{2,14},{3,15},{4,0},{5,1},{6,2},{7,3},{8,4},{9,5},{1... | collective-permute-start | bytes 983048 | tf_op jit(solution)/shard_map/ppermute | solution.py:48
  32.7 17.7 %collective-permute-start.9 = (bf16[4,32,1280]{2,1,0:T(8,128)(2,1)}, bf16[4,32,1280]{2,1,0:T(8,128)(2,1)S(1)}, u32[]{:S(2)}, u32[]{:S(2)}) collective-permute-start(bf16[4,32,1280]{2,1,0:T(8,128)(2,1)} %get-tuple-element.19), channel_id=1, source_target_pairs={{0,1},{1,2},{2,3},{3,0},{4,5},{5,6},{6,7},{7,4},{8,9},{9,10},{10,1... | collective-permute-start | bytes 983048 | tf_op jit(solution)/shard_map/ppermute | solution.py:49
  33.3 17.1 %collective-permute-start.10 = (bf16[4,32,1280]{2,1,0:T(8,128)(2,1)}, bf16[4,32,1280]{2,1,0:T(8,128)(2,1)}, u32[]{:S(2)}, u32[]{:S(2)}) collective-permute-start(bf16[4,32,1280]{2,1,0:T(8,128)(2,1)} %get-tuple-element.19), channel_id=1, source_target_pairs={{0,2},{1,3},{2,0},{3,1},{4,6},{5,7},{6,4},{7,5},{8,10},{9,11},{10,... | collective-permute-start | bytes 983048 | tf_op jit(solution)/shard_map/ppermute | solution.py:49
  44.9 9.4 %collective-permute-start.11 = (bf16[4,32,1280]{2,1,0:T(8,128)(2,1)}, bf16[4,32,1280]{2,1,0:T(8,128)(2,1)}, u32[]{:S(2)}, u32[]{:S(2)}) collective-permute-start(bf16[4,32,1280]{2,1,0:T(8,128)(2,1)} %get-tuple-element.19), channel_id=1, source_target_pairs={{0,3},{1,0},{2,1},{3,2},{4,7},{5,4},{6,5},{7,6},{8,11},{9,8},{10,9... | collective-permute-start | bytes 983048 | tf_op jit(solution)/shard_map/ppermute | solution.py:49
  45.7 1.1 %copy-start = (bf16[4,4,32,1280]{3,2,1,0:T(8,128)(2,1)}, bf16[4,4,32,1280]{3,2,1,0:T(8,128)(2,1)S(1)}, u32[]{:S(2)}) copy-start(bf16[4,4,32,1280]{3,2,1,0:T(8,128)(2,1)S(1)} %pad_maximum_fusion) | copy-start | bytes 3932164
  58.7 1.3 %copy-start.1 = (bf16[4,4,32,1280]{3,2,1,0:T(8,128)(2,1)S(1)}, bf16[4,4,32,1280]{3,2,1,0:T(8,128)(2,1)}, u32[]{:S(2)}) copy-start(bf16[4,4,32,1280]{3,2,1,0:T(8,128)(2,1)} %copy-done) | copy-start | bytes 3932164
  61.9 13.7 %collective-permute-start.12 = (bf16[4,32,1152]{2,1,0:T(8,128)(2,1)}, bf16[4,32,1152]{2,1,0:T(8,128)(2,1)S(1)}, u32[]{:S(2)}, u32[]{:S(2)}) collective-permute-start(bf16[4,32,1152]{2,1,0:T(8,128)(2,1)} %bitcast.30), channel_id=1, source_target_pairs={{0,12},{1,13},{2,14},{3,15},{4,0},{5,1},{6,2},{7,3},{8,4},{9,5},{1... | collective-permute-start | bytes 884744 | tf_op jit(solution)/shard_map/ppermute | solution.py:58
  61.9 13.8 %collective-permute-start.13 = (bf16[4,32,1152]{2,1,0:T(8,128)(2,1)}, bf16[4,32,1152]{2,1,0:T(8,128)(2,1)}, u32[]{:S(2)}, u32[]{:S(2)}) collective-permute-start(bf16[4,32,1152]{2,1,0:T(8,128)(2,1)} %bitcast.31), channel_id=1, source_target_pairs={{0,8},{1,9},{2,10},{3,11},{4,12},{5,13},{6,14},{7,15},{8,0},{9,1},... | collective-permute-start | bytes 884744 | tf_op jit(solution)/shard_map/ppermute | solution.py:58
  61.9 15.7 %collective-permute-start.14 = (bf16[4,32,1152]{2,1,0:T(8,128)(2,1)}, bf16[4,32,1152]{2,1,0:T(8,128)(2,1)}, u32[]{:S(2)}, u32[]{:S(2)}) collective-permute-start(bf16[4,32,1152]{2,1,0:T(8,128)(2,1)} %bitcast.32), channel_id=1, source_target_pairs={{0,4},{1,5},{2,6},{3,7},{4,8},{5,9},{6,10},{7,11},{8,12},{9,13},{1... | collective-permute-start | bytes 884744 | tf_op jit(solution)/shard_map/ppermute | solution.py:58
  68.9 13.4 %collective-permute-start.18 = (bf16[4,32,1152]{2,1,0:T(8,128)(2,1)}, bf16[4,32,1152]{2,1,0:T(8,128)(2,1)}, u32[]{:S(2)}, u32[]{:S(2)}) collective-permute-start(bf16[4,32,1152]{2,1,0:T(8,128)(2,1)} %bitcast.38), channel_id=1, source_target_pairs={{0,3},{1,0},{2,1},{3,2},{4,7},{5,4},{6,5},{7,6},{8,11},{9,8},{10,9... | collective-permute-start | bytes 884744 | tf_op jit(solution)/shard_map/ppermute | solution.py:59
  70.4 11.9 %collective-permute-start.19 = (bf16[4,32,1152]{2,1,0:T(8,128)(2,1)}, bf16[4,32,1152]{2,1,0:T(8,128)(2,1)}, u32[]{:S(2)}, u32[]{:S(2)}) collective-permute-start(bf16[4,32,1152]{2,1,0:T(8,128)(2,1)} %bitcast.39), channel_id=1, source_target_pairs={{0,2},{1,3},{2,0},{3,1},{4,6},{5,7},{6,4},{7,5},{8,10},{9,11},{10,... | collective-permute-start | bytes 884744 | tf_op jit(solution)/shard_map/ppermute | solution.py:59
  71.6 28.6 %all-to-all-start.1 = ((bf16[8,64,1152]{2,1,0:T(8,128)(2,1)}), bf16[8,64,1152]{2,1,0:T(8,128)(2,1)S(1)}, u32[]{:S(2)}, u32[]{:S(2)}) async-start(bf16[8,64,1152]{2,1,0:T(8,128)(2,1)} %bitcast.27), calls=%async_computation.1 | async-start | bytes 2359296 | tf_op jit(solution)/shard_map/all_to_all | solution.py:133
  75.6 12.7 %collective-permute-start.20 = (bf16[4,32,1152]{2,1,0:T(8,128)(2,1)}, bf16[4,32,1152]{2,1,0:T(8,128)(2,1)S(1)}, u32[]{:S(2)}, u32[]{:S(2)}) collective-permute-start(bf16[4,32,1152]{2,1,0:T(8,128)(2,1)} %bitcast.40), channel_id=1, source_target_pairs={{0,1},{1,2},{2,3},{3,0},{4,5},{5,6},{6,7},{7,4},{8,9},{9,10},{10,1... | collective-permute-start | bytes 884744 | tf_op jit(solution)/shard_map/ppermute | solution.py:59
  78.8 15.0 %collective-permute-start.15 = (bf16[32,1152]{1,0:T(8,128)(2,1)S(1)}, bf16[32,1152]{1,0:T(8,128)(2,1)S(1)}, u32[]{:S(2)}, u32[]{:S(2)}) collective-permute-start(bf16[32,1152]{1,0:T(8,128)(2,1)S(1)} %get-tuple-element.22), channel_id=1, source_target_pairs={{0,3},{1,0},{2,1},{3,2},{4,7},{5,4},{6,5},{7,6},{8,11},{9,8},{10,9... | collective-permute-start | bytes 221192 | tf_op jit(solution)/shard_map/ppermute | solution.py:63
  80.6 14.5 %collective-permute-start.16 = (bf16[32,1152]{1,0:T(8,128)(2,1)S(1)}, bf16[32,1152]{1,0:T(8,128)(2,1)S(1)}, u32[]{:S(2)}, u32[]{:S(2)}) collective-permute-start(bf16[32,1152]{1,0:T(8,128)(2,1)S(1)} %get-tuple-element.24), channel_id=1, source_target_pairs={{0,2},{1,3},{2,0},{3,1},{4,6},{5,7},{6,4},{7,5},{8,10},{9,11},{10,... | collective-permute-start | bytes 221192 | tf_op jit(solution)/shard_map/ppermute | solution.py:63
  82.3 12.8 %collective-permute-start.17 = (bf16[32,1152]{1,0:T(8,128)(2,1)S(1)}, bf16[32,1152]{1,0:T(8,128)(2,1)S(1)}, u32[]{:S(2)}, u32[]{:S(2)}) collective-permute-start(bf16[32,1152]{1,0:T(8,128)(2,1)S(1)} %get-tuple-element.23), channel_id=1, source_target_pairs={{0,1},{1,2},{2,3},{3,0},{4,5},{5,6},{6,7},{7,4},{8,9},{9,10},{10,1... | collective-permute-start | bytes 221192 | tf_op jit(solution)/shard_map/ppermute | solution.py:63
  89.5 5.7 %collective-permute-start.21 = (bf16[32,1152]{1,0:T(8,128)(2,1)S(1)}, bf16[32,1152]{1,0:T(8,128)(2,1)S(1)}, u32[]{:S(2)}, u32[]{:S(2)}) collective-permute-start(bf16[32,1152]{1,0:T(8,128)(2,1)S(1)} %get-tuple-element.25), channel_id=1, source_target_pairs={{0,12},{1,13},{2,14},{3,15},{4,0},{5,1},{6,2},{7,3},{8,4},{9,5},{1... | collective-permute-start | bytes 221192 | tf_op jit(solution)/shard_map/ppermute | solution.py:64
  92.2 5.9 %collective-permute-start.22 = (bf16[32,1152]{1,0:T(8,128)(2,1)S(1)}, bf16[32,1152]{1,0:T(8,128)(2,1)S(1)}, u32[]{:S(2)}, u32[]{:S(2)}) collective-permute-start(bf16[32,1152]{1,0:T(8,128)(2,1)S(1)} %get-tuple-element.27), channel_id=1, source_target_pairs={{0,8},{1,9},{2,10},{3,11},{4,12},{5,13},{6,14},{7,15},{8,0},{9,1},... | collective-permute-start | bytes 221192 | tf_op jit(solution)/shard_map/ppermute | solution.py:64
  93.8 5.6 %collective-permute-start.23 = (bf16[32,1152]{1,0:T(8,128)(2,1)S(1)}, bf16[32,1152]{1,0:T(8,128)(2,1)S(1)}, u32[]{:S(2)}, u32[]{:S(2)}) collective-permute-start(bf16[32,1152]{1,0:T(8,128)(2,1)S(1)} %get-tuple-element.26), channel_id=1, source_target_pairs={{0,4},{1,5},{2,6},{3,7},{4,8},{5,9},{6,10},{7,11},{8,12},{9,13},{1... | collective-permute-start | bytes 221192 | tf_op jit(solution)/shard_map/ppermute | solution.py:64

commit v4 on v3

--- a/solution.py
+++ b/solution.py
@@ -83,9 +83,10 @@
     member = lax.axis_index("mem")
     my_z = member // ny
     my_y = member % ny
-    tag = jnp.broadcast_to(caption_bucket.astype(captions.dtype)[:, None], (cap_rows, 128))
-    own = jnp.concatenate([captions, tag], axis=1)
-    inner_a, inner_b = gather_first(own[:half], own[half:], nz, ny)
+    tags = caption_bucket.astype(captions.dtype).reshape(2, half).T
+    tag_a = jnp.concatenate([tags, jnp.zeros((half, 126), captions.dtype)], axis=1)
+    own_a = jnp.concatenate([captions[:half], tag_a], axis=1)
+    inner_a, inner_b = gather_first(own_a, captions[half:], nz, ny)
     got_a, got_b = gather_second(inner_a, inner_b, nz, ny)
     bucket_hot = clip_bucket[:, None] == jnp.arange(n_buckets, dtype=jnp.int32)[None, :]
     owner = jnp.sum(jnp.where(bucket_hot, bucket_owner[None, :], 0), axis=1)
@@ -108,6 +109,8 @@
     recv_meta = recv_ext[:, width + 1:width + 4].astype(jnp.int32)
     recv_bucket = recv_meta[:, 0] - 1
     recv_positive = jnp.where(recv_bucket >= 0, recv_meta[:, 1] * 128 + recv_meta[:, 2], -1)
+    bucket_a = got_a[..., width].reshape(-1).astype(jnp.int32)
+    bucket_b = jnp.swapaxes(got_a[..., width + 1], 0, 1).reshape(-1).astype(jnp.int32)
     got_a = got_a.reshape(members * half, -1)
     got_b = got_b.reshape(members * half, -1)
     ar = jnp.arange(half, dtype=jnp.int32)
@@ -120,9 +123,8 @@
     ids_b = (base + src_b[:, :, None] * cap_rows + half + ar[None, None, :]).reshape(-1)
     weights = []
     rows = []
-    for got, ids in ((got_a, ids_a), (got_b, ids_b)):
+    for got, ids, bucket_y in ((got_a, ids_a, bucket_a), (got_b, ids_b, bucket_b)):
         rows_y = got[:, :width]
-        bucket_y = got[:, width].astype(jnp.int32)
         logits = mult * inner_rows(recv_rows, rows_y) + shift
         weights.append(pair_weights(
             logits, recv_positive[:, None] == ids[None, :], recv_bucket[:, None] == bucket_y[None, :]

time: 102 us -> 96.9 us (0.950)
  starting transfers between devices: 39 us -> 36.6 us
  matrix products: 11.5 us -> 10.2 us
  local copies, waits for them, and re-layouts: 5.79 us -> 4.59 us
    ppermute x3, waiting for transfers between devices: 11.4 us -> 5.49 us  [gather_second(): parts_a.append(lax.ppermute(inner_a, 'mem', shift_pairs(nz, ny, d, False)))]
    ppermute x3, waiting for transfers between devices: 7.41 us -> 11.8 us  [gather_second(): parts_b.append(lax.ppermute(inner_b, 'mem', shift_pairs(nz, ny, d, True)))]
    ppermute x3, waiting for transfers between devices: 6.87 us -> 3.99 us  [reduce_pair(): lax.ppermute(blocks_b[d].astype(low), 'mem', shift_pairs(nz, ny, -d, True))]
    ppermute x3, waiting for transfers between devices: 1.88 us -> 4.49 us  [reduce_pair(): lax.ppermute(blocks_a[d].astype(low), 'mem', shift_pairs(nz, ny, -d, False))]
    ppermute x3, starting transfers between devices: 3.69 us -> 1.54 us  [gather_second(): parts_a.append(lax.ppermute(inner_a, 'mem', shift_pairs(nz, ny, d, False)))]
    ppermute x3, starting transfers between devices: 2.72 us -> 0.64 us  [reduce_pair(): lax.ppermute(blocks_b[d].astype(low), 'mem', shift_pairs(nz, ny, -d, True))]
    ppermute x3, starting transfers between devices: 1.47 us -> 3.37 us  [gather_second(): parts_b.append(lax.ppermute(inner_b, 'mem', shift_pairs(nz, ny, d, True)))]
    unnamed x6 -> x4, local copies, waits for them, and re-layouts: 1.71 us -> 0.01 us
  transfers between devices with their start and end apart: 26 -> 26, of which waited for: 9 -> 9; matrix products, arithmetic and copies ran while one was open for 18% -> 19% of each run, Pallas kernels for 0% -> 0%
where the time goes in v4:
time: 96.9 us; the launch traced here: 96.2 us
  starting transfers between devices  36.6 us (38%)
  waiting for transfers between devices  31.3 us (32%)
  other arithmetic  11.2 us (12%)
  matrix products  10.2 us (11%)
  local copies, waits for them, and re-layouts  4.59 us (5%)
  between operations  2.17 us (2%)
    ppermute x3, waiting for transfers between devices, gather_second(): parts_b.append(lax.ppermute(inner_b, 'mem', shift_pairs(nz, ny, d, True)))  11.8 us
    ppermute x3, starting transfers between devices, gather_first(): parts_b.append(lax.ppermute(xb, 'mem', shift_pairs(nz, ny, d, False)))  6.51 us
    ppermute x3, starting transfers between devices, gather_first(): parts_a.append(lax.ppermute(xa, 'mem', shift_pairs(nz, ny, d, True)))  5.98 us
    ppermute x3, waiting for transfers between devices, gather_second(): parts_a.append(lax.ppermute(inner_a, 'mem', shift_pairs(nz, ny, d, False)))  5.49 us
    ppermute x3, waiting for transfers between devices, reduce_pair(): lax.ppermute(total_b[d].astype(low), 'mem', shift_pairs(nz, ny, -d, False))  5.46 us
    ppermute x3, starting transfers between devices, reduce_pair(): lax.ppermute(total_b[d].astype(low), 'mem', shift_pairs(nz, ny, -d, False))  4.67 us
    ppermute x3, waiting for transfers between devices, reduce_pair(): lax.ppermute(blocks_a[d].astype(low), 'mem', shift_pairs(nz, ny, -d, False))  4.49 us
    all_to_all x1, starting transfers between devices, inner_body(): lax.all_to_all(send_rows, 'grp', split_axis=0, concat_axis=0, tiled=True)  4.3 us
  transfers between devices with their start and end apart: 26, of which 9 were waited for; matrix products, arithmetic and copies ran while one was open for 19% of the time, Pallas kernels for 0%

profile of v4, /device:TPU:0, one launch (start us, length us, event | category | flops | bytes accessed | tf_op | source)
XLA Modules:
  0.0 96.2 jit_solution(6984952968872760072)
XLA Ops:
  0.6 1.0 %slice_bitcast_fusion.8 = (bf16[1,32,1152]{2,1,0:T(8,128)(2,1)S(1)}, bf16[32,1152]{1,0:T(8,128)(2,1)S(1)}, bf16[32,1152]{1,0:T(8,128)(2,1)S(1)}) fusion(bf16[64,1152]{1,0:T(8,128)(2,1)} %param.9), kind=kLoop, calls=%fused_computation.92 | loop fusion | bytes 368640 | tf_op jit(solution)/shard_map/stack | solution.py:41
  1.6 0.7 convert_element_type.141
  2.4 0.1 copy.25
  2.5 0.1 concatenate.11
  2.6 1.7 %collective-permute-start = (bf16[32,1280]{1,0:T(8,128)(2,1)S(1)}, bf16[32,1280]{1,0:T(8,128)(2,1)S(1)}, u32[]{:S(2)}, u32[]{:S(2)}) collective-permute-start(bf16[32,1280]{1,0:T(8,128)(2,1)S(1)} %concatenate.11), channel_id=1, source_target_pairs={{0,1},{1,2},{2,3},{3,0},{4,5},{5,6},{6,7},{7,4},{8,9},{9,10},{10,1... | collective-permute-start | bytes 245768 | tf_op jit(solution)/shard_map/ppermute | solution.py:39
  4.3 2.9 %collective-permute-start.1 = (bf16[32,1280]{1,0:T(8,128)(2,1)S(1)}, bf16[32,1280]{1,0:T(8,128)(2,1)S(1)}, u32[]{:S(2)}, u32[]{:S(2)}) collective-permute-start(bf16[32,1280]{1,0:T(8,128)(2,1)S(1)} %concatenate.11), channel_id=1, source_target_pairs={{0,2},{1,3},{2,0},{3,1},{4,6},{5,7},{6,4},{7,5},{8,10},{9,11},{10,... | collective-permute-start | bytes 245768 | tf_op jit(solution)/shard_map/ppermute | solution.py:39
  7.2 1.9 %collective-permute-start.6 = (bf16[32,1152]{1,0:T(8,128)(2,1)S(1)}, bf16[32,1152]{1,0:T(8,128)(2,1)S(1)}, u32[]{:S(2)}, u32[]{:S(2)}) collective-permute-start(bf16[32,1152]{1,0:T(8,128)(2,1)S(1)} %get-tuple-element.31), channel_id=1, source_target_pairs={{0,4},{1,5},{2,6},{3,7},{4,8},{5,9},{6,10},{7,11},{8,12},{9,13},{1... | collective-permute-start | bytes 221192 | tf_op jit(solution)/shard_map/ppermute | solution.py:40
  9.1 3.6 %collective-permute-start.7 = (bf16[32,1152]{1,0:T(8,128)(2,1)S(1)}, bf16[32,1152]{1,0:T(8,128)(2,1)S(1)}, u32[]{:S(2)}, u32[]{:S(2)}) collective-permute-start(bf16[32,1152]{1,0:T(8,128)(2,1)S(1)} %get-tuple-element.31), channel_id=1, source_target_pairs={{0,8},{1,9},{2,10},{3,11},{4,12},{5,13},{6,14},{7,15},{8,0},{9,1},... | collective-permute-start | bytes 221192 | tf_op jit(solution)/shard_map/ppermute | solution.py:40
  12.7 1.0 %collective-permute-start.8 = (bf16[32,1152]{1,0:T(8,128)(2,1)S(1)}, bf16[32,1152]{1,0:T(8,128)(2,1)S(1)}, u32[]{:S(2)}, u32[]{:S(2)}) collective-permute-start(bf16[32,1152]{1,0:T(8,128)(2,1)S(1)} %get-tuple-element.31), channel_id=1, source_target_pairs={{0,12},{1,13},{2,14},{3,15},{4,0},{5,1},{6,2},{7,3},{8,4},{9,5},{1... | collective-permute-start | bytes 221192 | tf_op jit(solution)/shard_map/ppermute | solution.py:40
  13.7 0.7 add_convert_fusion
  14.4 0.8 select_reduce_fusion
  15.2 0.6 reduce-window.6
  15.8 0.2 slice_reduce_fusion
  16.0 0.1 fusion.34
  16.1 0.7 fusion.36
  16.8 0.1 stack.98
  16.9 0.1 stack.99
  17.0 0.1 stack.97
  17.2 0.3 concatenate.10
  17.5 1.8 %convolution_convert_fusion = bf16[512,1280]{1,0:T(8,128)(2,1)} fusion(bf16[256,1280]{1,0:T(8,128)(2,1)S(1)} %concatenate.10, s32[256]{0:T(256)S(1)} %multiply_add_fusion.1), kind=kOutput, calls=%fused_computation.1 | convolution fusion | flops 336330752 | bytes 1967104 | tf_op jit(solution)/shard_map/dot_general | solution.py:103
  19.3 4.3 %all-to-all-start = ((bf16[8,64,1280]{2,1,0:T(8,128)(2,1)}), bf16[8,64,1280]{2,1,0:T(8,128)(2,1)S(1)}, u32[]{:S(2)}, u32[]{:S(2)}) async-start(bf16[8,64,1280]{2,1,0:T(8,128)(2,1)} %bitcast.3), calls=%async_computation | async-start | bytes 2621440 | tf_op jit(solution)/shard_map/all_to_all | solution.py:107
  23.7 1.4 %collective-permute-start.2 = (bf16[32,1280]{1,0:T(8,128)(2,1)S(1)}, bf16[32,1280]{1,0:T(8,128)(2,1)S(1)}, u32[]{:S(2)}, u32[]{:S(2)}) collective-permute-start(bf16[32,1280]{1,0:T(8,128)(2,1)S(1)} %concatenate.11), channel_id=1, source_target_pairs={{0,3},{1,0},{2,1},{3,2},{4,7},{5,4},{6,5},{7,6},{8,11},{9,8},{10,9... | collective-permute-start | bytes 245768 | tf_op jit(solution)/shard_map/ppermute | solution.py:39
  25.1 0.8 fusion.41
  25.9 0.7 collective-permute-start.9
  26.6 0.8 collective-permute-start.10
  27.4 1.9 %collective-permute-start.11 = (bf16[4,32,1152]{2,1,0:T(8,128)(2,1)}, bf16[4,32,1152]{2,1,0:T(8,128)(2,1)}, u32[]{:S(2)}, u32[]{:S(2)}) collective-permute-start(bf16[4,32,1152]{2,1,0:T(8,128)(2,1)} %get-tuple-element.29), channel_id=1, source_target_pairs={{0,3},{1,0},{2,1},{3,2},{4,7},{5,4},{6,5},{7,6},{8,11},{9,8},{10,9... | collective-permute-start | bytes 884744 | tf_op jit(solution)/shard_map/ppermute | solution.py:49
  29.4 1.1 %collective-permute-start.3 = (bf16[4,32,1280]{2,1,0:T(8,128)(2,1)S(1)}, bf16[4,32,1280]{2,1,0:T(8,128)(2,1)S(1)}, u32[]{:S(2)}, u32[]{:S(2)}) collective-permute-start(bf16[4,32,1280]{2,1,0:T(8,128)(2,1)S(1)} %get-tuple-element.21), channel_id=1, source_target_pairs={{0,4},{1,5},{2,6},{3,7},{4,8},{5,9},{6,10},{7,11},{8,12},{9,13},{1... | collective-permute-start | bytes 983048 | tf_op jit(solution)/shard_map/ppermute | solution.py:48
  30.5 0.4 collective-permute-start.4
  30.9 11.8 %collective-permute-done.9 = bf16[4,32,1152]{2,1,0:T(8,128)(2,1)S(1)} collective-permute-done((bf16[4,32,1152]{2,1,0:T(8,128)(2,1)}, bf16[4,32,1152]{2,1,0:T(8,128)(2,1)S(1)}, u32[]{:S(2)}, u32[]{:S(2)}) %collective-permute-start.9) | collective-permute-done | bytes 294944 | tf_op jit(solution)/shard_map/ppermute | solution.py:49
  44.3 2.2 %pad_maximum_fusion.1 = bf16[4,4,32,1152]{3,2,1,0:T(8,128)(2,1)} fusion(bf16[1,4,32,1152]{3,2,1,0:T(8,128)(2,1)} %bitcast.25, bf16[1,4,32,1152]{3,2,1,0:T(8,128)(2,1)S(1)} %bitcast.102, bf16[1,4,32,1152]{3,2,1,0:T(8,128)(2,1)S(1)} %bitcast.101, bf16[1,4,32,1152]{3,2,1,0:T(8,128)(2,1)S(1)} %get-tuple-element.28), kind=kLoop, calls=%fused_computation.23 | loop fusion | flops 1769472 | bytes 2359296 | tf_op jit(solution)/shard_map/stack | solution.py:50
  46.5 0.5 collective-permute-done.3
  47.0 5.0 %collective-permute-done.5 = bf16[4,32,1280]{2,1,0:T(8,128)(2,1)} collective-permute-done((bf16[4,32,1280]{2,1,0:T(8,128)(2,1)S(1)}, bf16[4,32,1280]{2,1,0:T(8,128)(2,1)}, u32[]{:S(2)}, u32[]{:S(2)}) %collective-permute-start.5) | collective-permute-done | bytes 327712 | tf_op jit(solution)/shard_map/ppermute | solution.py:48
  51.9 1.2 %pad_maximum_fusion = bf16[4,4,32,1280]{3,2,1,0:T(8,128)(2,1)S(1)} fusion(bf16[1,4,32,1280]{3,2,1,0:T(8,128)(2,1)} %bitcast.13, bf16[1,4,32,1280]{3,2,1,0:T(8,128)(2,1)} %bitcast.12, bf16[1,4,32,1280]{3,2,1,0:T(8,128)(2,1)S(1)} %bitcast.99, bf16[1,4,32,1280]{3,2,1,0:T(8,128)(2,1)S(1)} %get-tuple-element.20), kind=kLoop, calls=%fused_computation.18 | loop fusion | flops 1966080 | bytes 2621440 | tf_op jit(solution)/shard_map/stack | solution.py:50
  53.2 0.7 convert_reduce_fusion
  54.1 0.1 slice_convert_fusion
  54.2 0.4 fusion.26
  54.6 1.2 %fusion.17 = bf16[512,512]{1,0:T(8,128)(2,1)S(1)} fusion(bf16[512,1280]{1,0:T(8,128)(2,1)S(1)} %bitcast.92, f32[]{:T(128)} %bitcast.85, f32[]{:T(128)} %bitcast.83, s32[512]{0:T(512)S(1)} %add.241, s32[512]{0:T(512)S(1)} %reshape.276, s32[512]{0:T(512)S(1)} %get-tuple-element.9, s32[512]{0:T(512)S(1)} %get-tuple-element.8, bf16[512,1280]{1,0:T(8,128)(2,1)S(1)} %bitcast.88), kind=kOutput, calls=%fused_computation.22 | convolution fusion | flops 607387648 | bytes 2891784 | tf_op jit(solution)/shard_map/dot_general | solution.py:13
  55.8 0.9 fusion.52
  56.7 0.8 fusion.18
  57.5 0.1 slice.138
  57.7 0.9 fusion.49
  58.6 1.5 %collective-permute-start.12 = (bf16[4,32,1152]{2,1,0:T(8,128)(2,1)}, bf16[4,32,1152]{2,1,0:T(8,128)(2,1)S(1)}, u32[]{:S(2)}, u32[]{:S(2)}) collective-permute-start(bf16[4,32,1152]{2,1,0:T(8,128)(2,1)} %bitcast.30), channel_id=1, source_target_pairs={{0,12},{1,13},{2,14},{3,15},{4,0},{5,1},{6,2},{7,3},{8,4},{9,5},{1... | collective-permute-start | bytes 884744 | tf_op jit(solution)/shard_map/ppermute | solution.py:58
  60.1 1.5 %collective-permute-start.13 = (bf16[4,32,1152]{2,1,0:T(8,128)(2,1)}, bf16[4,32,1152]{2,1,0:T(8,128)(2,1)S(1)}, u32[]{:S(2)}, u32[]{:S(2)}) collective-permute-start(bf16[4,32,1152]{2,1,0:T(8,128)(2,1)} %bitcast.31), channel_id=1, source_target_pairs={{0,8},{1,9},{2,10},{3,11},{4,12},{5,13},{6,14},{7,15},{8,0},{9,1},... | collective-permute-start | bytes 884744 | tf_op jit(solution)/shard_map/ppermute | solution.py:58
  61.6 1.2 %fusion.15 = bf16[512,512]{1,0:T(8,128)(2,1)S(1)} fusion(bf16[512,1152]{1,0:T(8,128)(2,1)S(1)} %bitcast.94, s32[512]{0:T(512)S(1)} %add.253, s32[512]{0:T(512)S(1)} %reshape.277, f32[]{:T(128)} %bitcast.86, f32[]{:T(128)} %bitcast.84, s32[512]{0:T(512)S(1)} %get-tuple-element.9, s32[512]{0:T(512)S(1)} %get-tuple-element.8, bf16[512,1280]{1,0:T(8,128)(2,1)S(1)} %bitcast.91), kind=kOutput, calls=%fused_computation.20 | convolution fusion | flops 607387648 | bytes 2891784 | tf_op jit(solution)/shard_map/dot_general | solution.py:13
  62.9 1.9 %convolution_add_fusion = bf16[512,1152]{1,0:T(8,128)(2,1)} fusion(f32[512,1152]{1,0:T(8,128)S(1)} %fusion.18, bf16[512,512]{1,0:T(8,128)(2,1)S(1)} %fusion.15, bf16[512,1152]{1,0:T(8,128)(2,1)S(1)} %bitcast.95), kind=kOutput, calls=%fused_computation | convolution fusion | flops 605159424 | bytes 5242880 | tf_op jit(solution)/shard_map/dot_general | solution.py:134
  64.7 0.9 fusion.51
  65.6 0.9 fusion.50
  66.6 4.0 %all-to-all-start.1 = ((bf16[8,64,1152]{2,1,0:T(8,128)(2,1)}), bf16[8,64,1152]{2,1,0:T(8,128)(2,1)S(1)}, u32[]{:S(2)}, u32[]{:S(2)}) async-start(bf16[8,64,1152]{2,1,0:T(8,128)(2,1)} %bitcast.27), calls=%async_computation.1 | async-start | bytes 2359296 | tf_op jit(solution)/shard_map/all_to_all | solution.py:135
  70.6 1.5 %collective-permute-done.12 = bf16[4,32,1152]{2,1,0:T(8,128)(2,1)S(1)} collective-permute-done((bf16[4,32,1152]{2,1,0:T(8,128)(2,1)}, bf16[4,32,1152]{2,1,0:T(8,128)(2,1)S(1)}, u32[]{:S(2)}, u32[]{:S(2)}) %collective-permute-start.12) | collective-permute-done | bytes 294944 | tf_op jit(solution)/shard_map/ppermute | solution.py:58
  72.1 0.6 collective-permute-start.20
  72.7 3.0 %collective-permute-done.14 = bf16[4,32,1152]{2,1,0:T(8,128)(2,1)} collective-permute-done((bf16[4,32,1152]{2,1,0:T(8,128)(2,1)}, bf16[4,32,1152]{2,1,0:T(8,128)(2,1)}, u32[]{:S(2)}, u32[]{:S(2)}) %collective-permute-start.14) | collective-permute-done | bytes 294944 | tf_op jit(solution)/shard_map/ppermute | solution.py:58
  75.8 1.1 %fusion.47 = (bf16[4,32,1152]{2,1,0:T(8,128)(2,1)S(1)}, f32[4,32,1152]{2,1,0:T(8,128)S(1)}) fusion(bf16[4,32,1152]{2,1,0:T(8,128)(2,1)} %collective-permute-done.14, bf16[4,32,1152]{2,1,0:T(8,128)(2,1)S(1)} %collective-permute-done.13, f32[4,32,1152]{2,1,0:T(8,128)S(1)} %bitcast.98, bf16[4,32,1152]{2,1,0:T(8,128)(2,1)S(1)} %collective-permute-done.12), kind=kLoop, calls=%fused_computation.99 | loop fusion | flops 1032192 | bytes 2359296 | tf_op jit(solution)/shard_map/convert.12
  77.0 1.2 %collective-permute-start.16 = (bf16[32,1152]{1,0:T(8,128)(2,1)S(1)}, bf16[32,1152]{1,0:T(8,128)(2,1)S(1)}, u32[]{:S(2)}, u32[]{:S(2)}) collective-permute-start(bf16[32,1152]{1,0:T(8,128)(2,1)S(1)} %get-tuple-element.24), channel_id=1, source_target_pairs={{0,2},{1,3},{2,0},{3,1},{4,6},{5,7},{6,4},{7,5},{8,10},{9,11},{10,... | collective-permute-start | bytes 221192 | tf_op jit(solution)/shard_map/ppermute | solution.py:63
  78.1 1.3 %collective-permute-start.17 = (bf16[32,1152]{1,0:T(8,128)(2,1)S(1)}, bf16[32,1152]{1,0:T(8,128)(2,1)S(1)}, u32[]{:S(2)}, u32[]{:S(2)}) collective-permute-start(bf16[32,1152]{1,0:T(8,128)(2,1)S(1)} %get-tuple-element.23), channel_id=1, source_target_pairs={{0,1},{1,2},{2,3},{3,0},{4,5},{5,6},{6,7},{7,4},{8,9},{9,10},{10,1... | collective-permute-start | bytes 221192 | tf_op jit(solution)/shard_map/ppermute | solution.py:63
  79.5 4.0 %collective-permute-done.20 = bf16[4,32,1152]{2,1,0:T(8,128)(2,1)S(1)} collective-permute-done((bf16[4,32,1152]{2,1,0:T(8,128)(2,1)}, bf16[4,32,1152]{2,1,0:T(8,128)(2,1)S(1)}, u32[]{:S(2)}, u32[]{:S(2)}) %collective-permute-start.20) | collective-permute-done | bytes 294944 | tf_op jit(solution)/shard_map/ppermute | solution.py:59
  83.5 0.1 fusion.48
  83.6 3.5 %collective-permute-start.21 = (bf16[32,1152]{1,0:T(8,128)(2,1)S(1)}, bf16[32,1152]{1,0:T(8,128)(2,1)S(1)}, u32[]{:S(2)}, u32[]{:S(2)}) collective-permute-start(bf16[32,1152]{1,0:T(8,128)(2,1)S(1)} %get-tuple-element.25), channel_id=1, source_target_pairs={{0,12},{1,13},{2,14},{3,15},{4,0},{5,1},{6,2},{7,3},{8,4},{9,5},{1... | collective-permute-start | bytes 221192 | tf_op jit(solution)/shard_map/ppermute | solution.py:64
  87.2 0.6 collective-permute-start.22
  87.8 0.5 collective-permute-start.23
  88.3 1.5 %collective-permute-done.21 = bf16[32,1152]{1,0:T(8,128)(2,1)S(1)} collective-permute-done((bf16[32,1152]{1,0:T(8,128)(2,1)S(1)}, bf16[32,1152]{1,0:T(8,128)(2,1)S(1)}, u32[]{:S(2)}, u32[]{:S(2)}) %collective-permute-start.21) | collective-permute-done | bytes 73760 | tf_op jit(solution)/shard_map/ppermute | solution.py:64
  89.9 3.2 %collective-permute-done.22 = bf16[32,1152]{1,0:T(8,128)(2,1)S(1)} collective-permute-done((bf16[32,1152]{1,0:T(8,128)(2,1)S(1)}, bf16[32,1152]{1,0:T(8,128)(2,1)S(1)}, u32[]{:S(2)}, u32[]{:S(2)}) %collective-permute-start.22) | collective-permute-done | bytes 73760 | tf_op jit(solution)/shard_map/ppermute | solution.py:64
  93.1 0.7 collective-permute-done.23
  93.9 0.7 pad_maximum_fusion.4
  94.6 1.6 %fusion.21 = f32[256,1152]{1,0:T(8,128)} fusion(bf16[512,1152]{1,0:T(8,128)(2,1)S(1)} %bitcast.96, s32[256]{0:T(256)S(1)} %multiply_add_fusion.1), kind=kOutput, calls=%fused_computation.30 | convolution fusion | flops 302120960 | bytes 2360320 | tf_op jit(solution)/shard_map/dot_general | solution.py:136
  (50 shorter events, 1.1 us)
Async XLA Ops:
  0.6 16.5 %copy-start.1 = (bf16[256,1152]{1,0:T(8,128)(2,1)S(1)}, bf16[256,1152]{1,0:T(8,128)(2,1)}, u32[]{:S(2)}) copy-start(bf16[256,1152]{1,0:T(8,128)(2,1)} %param.8) | copy-start | bytes 1769476
  2.6 24.8 %collective-permute-start = (bf16[32,1280]{1,0:T(8,128)(2,1)S(1)}, bf16[32,1280]{1,0:T(8,128)(2,1)S(1)}, u32[]{:S(2)}, u32[]{:S(2)}) collective-permute-start(bf16[32,1280]{1,0:T(8,128)(2,1)S(1)} %concatenate.11), channel_id=1, source_target_pairs={{0,1},{1,2},{2,3},{3,0},{4,5},{5,6},{6,7},{7,4},{8,9},{9,10},{10,1... | collective-permute-start | bytes 245768 | tf_op jit(solution)/shard_map/ppermute | solution.py:39
  4.3 25.0 %collective-permute-start.1 = (bf16[32,1280]{1,0:T(8,128)(2,1)S(1)}, bf16[32,1280]{1,0:T(8,128)(2,1)S(1)}, u32[]{:S(2)}, u32[]{:S(2)}) collective-permute-start(bf16[32,1280]{1,0:T(8,128)(2,1)S(1)} %concatenate.11), channel_id=1, source_target_pairs={{0,2},{1,3},{2,0},{3,1},{4,6},{5,7},{6,4},{7,5},{8,10},{9,11},{10,... | collective-permute-start | bytes 245768 | tf_op jit(solution)/shard_map/ppermute | solution.py:39
  7.2 16.5 %collective-permute-start.6 = (bf16[32,1152]{1,0:T(8,128)(2,1)S(1)}, bf16[32,1152]{1,0:T(8,128)(2,1)S(1)}, u32[]{:S(2)}, u32[]{:S(2)}) collective-permute-start(bf16[32,1152]{1,0:T(8,128)(2,1)S(1)} %get-tuple-element.31), channel_id=1, source_target_pairs={{0,4},{1,5},{2,6},{3,7},{4,8},{5,9},{6,10},{7,11},{8,12},{9,13},{1... | collective-permute-start | bytes 221192 | tf_op jit(solution)/shard_map/ppermute | solution.py:40
  9.1 16.0 %collective-permute-start.7 = (bf16[32,1152]{1,0:T(8,128)(2,1)S(1)}, bf16[32,1152]{1,0:T(8,128)(2,1)S(1)}, u32[]{:S(2)}, u32[]{:S(2)}) collective-permute-start(bf16[32,1152]{1,0:T(8,128)(2,1)S(1)} %get-tuple-element.31), channel_id=1, source_target_pairs={{0,8},{1,9},{2,10},{3,11},{4,12},{5,13},{6,14},{7,15},{8,0},{9,1},... | collective-permute-start | bytes 221192 | tf_op jit(solution)/shard_map/ppermute | solution.py:40
  12.7 12.4 %collective-permute-start.8 = (bf16[32,1152]{1,0:T(8,128)(2,1)S(1)}, bf16[32,1152]{1,0:T(8,128)(2,1)S(1)}, u32[]{:S(2)}, u32[]{:S(2)}) collective-permute-start(bf16[32,1152]{1,0:T(8,128)(2,1)S(1)} %get-tuple-element.31), channel_id=1, source_target_pairs={{0,12},{1,13},{2,14},{3,15},{4,0},{5,1},{6,2},{7,3},{8,4},{9,5},{1... | collective-permute-start | bytes 221192 | tf_op jit(solution)/shard_map/ppermute | solution.py:40
  19.3 34.8 %all-to-all-start = ((bf16[8,64,1280]{2,1,0:T(8,128)(2,1)}), bf16[8,64,1280]{2,1,0:T(8,128)(2,1)S(1)}, u32[]{:S(2)}, u32[]{:S(2)}) async-start(bf16[8,64,1280]{2,1,0:T(8,128)(2,1)} %bitcast.3), calls=%async_computation | async-start | bytes 2621440 | tf_op jit(solution)/shard_map/all_to_all | solution.py:107
  23.7 5.6 %collective-permute-start.2 = (bf16[32,1280]{1,0:T(8,128)(2,1)S(1)}, bf16[32,1280]{1,0:T(8,128)(2,1)S(1)}, u32[]{:S(2)}, u32[]{:S(2)}) collective-permute-start(bf16[32,1280]{1,0:T(8,128)(2,1)S(1)} %concatenate.11), channel_id=1, source_target_pairs={{0,3},{1,0},{2,1},{3,2},{4,7},{5,4},{6,5},{7,6},{8,11},{9,8},{10,9... | collective-permute-start | bytes 245768 | tf_op jit(solution)/shard_map/ppermute | solution.py:39
  25.9 16.9 %collective-permute-start.9 = (bf16[4,32,1152]{2,1,0:T(8,128)(2,1)}, bf16[4,32,1152]{2,1,0:T(8,128)(2,1)S(1)}, u32[]{:S(2)}, u32[]{:S(2)}) collective-permute-start(bf16[4,32,1152]{2,1,0:T(8,128)(2,1)} %get-tuple-element.29), channel_id=1, source_target_pairs={{0,1},{1,2},{2,3},{3,0},{4,5},{5,6},{6,7},{7,4},{8,9},{9,10},{10,1... | collective-permute-start | bytes 884744 | tf_op jit(solution)/shard_map/ppermute | solution.py:49
  26.6 17.7 %collective-permute-start.10 = (bf16[4,32,1152]{2,1,0:T(8,128)(2,1)}, bf16[4,32,1152]{2,1,0:T(8,128)(2,1)S(1)}, u32[]{:S(2)}, u32[]{:S(2)}) collective-permute-start(bf16[4,32,1152]{2,1,0:T(8,128)(2,1)} %get-tuple-element.29), channel_id=1, source_target_pairs={{0,2},{1,3},{2,0},{3,1},{4,6},{5,7},{6,4},{7,5},{8,10},{9,11},{10,... | collective-permute-start | bytes 884744 | tf_op jit(solution)/shard_map/ppermute | solution.py:49
  27.4 16.9 %collective-permute-start.11 = (bf16[4,32,1152]{2,1,0:T(8,128)(2,1)}, bf16[4,32,1152]{2,1,0:T(8,128)(2,1)}, u32[]{:S(2)}, u32[]{:S(2)}) collective-permute-start(bf16[4,32,1152]{2,1,0:T(8,128)(2,1)} %get-tuple-element.29), channel_id=1, source_target_pairs={{0,3},{1,0},{2,1},{3,2},{4,7},{5,4},{6,5},{7,6},{8,11},{9,8},{10,9... | collective-permute-start | bytes 884744 | tf_op jit(solution)/shard_map/ppermute | solution.py:49
  29.4 17.6 %collective-permute-start.3 = (bf16[4,32,1280]{2,1,0:T(8,128)(2,1)S(1)}, bf16[4,32,1280]{2,1,0:T(8,128)(2,1)S(1)}, u32[]{:S(2)}, u32[]{:S(2)}) collective-permute-start(bf16[4,32,1280]{2,1,0:T(8,128)(2,1)S(1)} %get-tuple-element.21), channel_id=1, source_target_pairs={{0,4},{1,5},{2,6},{3,7},{4,8},{5,9},{6,10},{7,11},{8,12},{9,13},{1... | collective-permute-start | bytes 983048 | tf_op jit(solution)/shard_map/ppermute | solution.py:48
  30.5 16.5 %collective-permute-start.4 = (bf16[4,32,1280]{2,1,0:T(8,128)(2,1)S(1)}, bf16[4,32,1280]{2,1,0:T(8,128)(2,1)}, u32[]{:S(2)}, u32[]{:S(2)}) collective-permute-start(bf16[4,32,1280]{2,1,0:T(8,128)(2,1)S(1)} %get-tuple-element.21), channel_id=1, source_target_pairs={{0,8},{1,9},{2,10},{3,11},{4,12},{5,13},{6,14},{7,15},{8,0},{9,1},... | collective-permute-start | bytes 983048 | tf_op jit(solution)/shard_map/ppermute | solution.py:48
  42.7 9.2 %collective-permute-start.5 = (bf16[4,32,1280]{2,1,0:T(8,128)(2,1)S(1)}, bf16[4,32,1280]{2,1,0:T(8,128)(2,1)}, u32[]{:S(2)}, u32[]{:S(2)}) collective-permute-start(bf16[4,32,1280]{2,1,0:T(8,128)(2,1)S(1)} %get-tuple-element.21), channel_id=1, source_target_pairs={{0,12},{1,13},{2,14},{3,15},{4,0},{5,1},{6,2},{7,3},{8,4},{9,5},{1... | collective-permute-start | bytes 983048 | tf_op jit(solution)/shard_map/ppermute | solution.py:48
  57.6 4.0 %copy-start = (bf16[4,4,32,1152]{3,2,1,0:T(8,128)(2,1)S(1)}, bf16[4,4,32,1152]{3,2,1,0:T(8,128)(2,1)}, u32[]{:S(2)}) copy-start(bf16[4,4,32,1152]{3,2,1,0:T(8,128)(2,1)} %pad_maximum_fusion.1) | copy-start | bytes 3538948
  58.6 13.5 %collective-permute-start.12 = (bf16[4,32,1152]{2,1,0:T(8,128)(2,1)}, bf16[4,32,1152]{2,1,0:T(8,128)(2,1)S(1)}, u32[]{:S(2)}, u32[]{:S(2)}) collective-permute-start(bf16[4,32,1152]{2,1,0:T(8,128)(2,1)} %bitcast.30), channel_id=1, source_target_pairs={{0,12},{1,13},{2,14},{3,15},{4,0},{5,1},{6,2},{7,3},{8,4},{9,5},{1... | collective-permute-start | bytes 884744 | tf_op jit(solution)/shard_map/ppermute | solution.py:58
  60.1 12.6 %collective-permute-start.13 = (bf16[4,32,1152]{2,1,0:T(8,128)(2,1)}, bf16[4,32,1152]{2,1,0:T(8,128)(2,1)S(1)}, u32[]{:S(2)}, u32[]{:S(2)}) collective-permute-start(bf16[4,32,1152]{2,1,0:T(8,128)(2,1)} %bitcast.31), channel_id=1, source_target_pairs={{0,8},{1,9},{2,10},{3,11},{4,12},{5,13},{6,14},{7,15},{8,0},{9,1},... | collective-permute-start | bytes 884744 | tf_op jit(solution)/shard_map/ppermute | solution.py:58
  61.6 14.2 %collective-permute-start.14 = (bf16[4,32,1152]{2,1,0:T(8,128)(2,1)}, bf16[4,32,1152]{2,1,0:T(8,128)(2,1)}, u32[]{:S(2)}, u32[]{:S(2)}) collective-permute-start(bf16[4,32,1152]{2,1,0:T(8,128)(2,1)} %bitcast.32), channel_id=1, source_target_pairs={{0,4},{1,5},{2,6},{3,7},{4,8},{5,9},{6,10},{7,11},{8,12},{9,13},{1... | collective-permute-start | bytes 884744 | tf_op jit(solution)/shard_map/ppermute | solution.py:58
  66.5 11.6 %collective-permute-start.18 = (bf16[4,32,1152]{2,1,0:T(8,128)(2,1)}, bf16[4,32,1152]{2,1,0:T(8,128)(2,1)S(1)}, u32[]{:S(2)}, u32[]{:S(2)}) collective-permute-start(bf16[4,32,1152]{2,1,0:T(8,128)(2,1)} %bitcast.38), channel_id=1, source_target_pairs={{0,3},{1,0},{2,1},{3,2},{4,7},{5,4},{6,5},{7,6},{8,11},{9,8},{10,9... | collective-permute-start | bytes 884744 | tf_op jit(solution)/shard_map/ppermute | solution.py:59
  66.5 12.9 %collective-permute-start.19 = (bf16[4,32,1152]{2,1,0:T(8,128)(2,1)}, bf16[4,32,1152]{2,1,0:T(8,128)(2,1)S(1)}, u32[]{:S(2)}, u32[]{:S(2)}) collective-permute-start(bf16[4,32,1152]{2,1,0:T(8,128)(2,1)} %bitcast.39), channel_id=1, source_target_pairs={{0,2},{1,3},{2,0},{3,1},{4,6},{5,7},{6,4},{7,5},{8,10},{9,11},{10,... | collective-permute-start | bytes 884744 | tf_op jit(solution)/shard_map/ppermute | solution.py:59
  66.6 28.0 %all-to-all-start.1 = ((bf16[8,64,1152]{2,1,0:T(8,128)(2,1)}), bf16[8,64,1152]{2,1,0:T(8,128)(2,1)S(1)}, u32[]{:S(2)}, u32[]{:S(2)}) async-start(bf16[8,64,1152]{2,1,0:T(8,128)(2,1)} %bitcast.27), calls=%async_computation.1 | async-start | bytes 2359296 | tf_op jit(solution)/shard_map/all_to_all | solution.py:135
  72.1 11.4 %collective-permute-start.20 = (bf16[4,32,1152]{2,1,0:T(8,128)(2,1)}, bf16[4,32,1152]{2,1,0:T(8,128)(2,1)S(1)}, u32[]{:S(2)}, u32[]{:S(2)}) collective-permute-start(bf16[4,32,1152]{2,1,0:T(8,128)(2,1)} %bitcast.103), channel_id=1, source_target_pairs={{0,1},{1,2},{2,3},{3,0},{4,5},{5,6},{6,7},{7,4},{8,9},{9,10},{10,1... | collective-permute-start | bytes 884744 | tf_op jit(solution)/shard_map/ppermute | solution.py:59
  76.9 10.9 %collective-permute-start.15 = (bf16[32,1152]{1,0:T(8,128)(2,1)S(1)}, bf16[32,1152]{1,0:T(8,128)(2,1)S(1)}, u32[]{:S(2)}, u32[]{:S(2)}) collective-permute-start(bf16[32,1152]{1,0:T(8,128)(2,1)S(1)} %get-tuple-element.22), channel_id=1, source_target_pairs={{0,3},{1,0},{2,1},{3,2},{4,7},{5,4},{6,5},{7,6},{8,11},{9,8},{10,9... | collective-permute-start | bytes 221192 | tf_op jit(solution)/shard_map/ppermute | solution.py:63
  77.0 11.3 %collective-permute-start.16 = (bf16[32,1152]{1,0:T(8,128)(2,1)S(1)}, bf16[32,1152]{1,0:T(8,128)(2,1)S(1)}, u32[]{:S(2)}, u32[]{:S(2)}) collective-permute-start(bf16[32,1152]{1,0:T(8,128)(2,1)S(1)} %get-tuple-element.24), channel_id=1, source_target_pairs={{0,2},{1,3},{2,0},{3,1},{4,6},{5,7},{6,4},{7,5},{8,10},{9,11},{10,... | collective-permute-start | bytes 221192 | tf_op jit(solution)/shard_map/ppermute | solution.py:63
  78.1 10.2 %collective-permute-start.17 = (bf16[32,1152]{1,0:T(8,128)(2,1)S(1)}, bf16[32,1152]{1,0:T(8,128)(2,1)S(1)}, u32[]{:S(2)}, u32[]{:S(2)}) collective-permute-start(bf16[32,1152]{1,0:T(8,128)(2,1)S(1)} %get-tuple-element.23), channel_id=1, source_target_pairs={{0,1},{1,2},{2,3},{3,0},{4,5},{5,6},{6,7},{7,4},{8,9},{9,10},{10,1... | collective-permute-start | bytes 221192 | tf_op jit(solution)/shard_map/ppermute | solution.py:63
  83.6 6.2 %collective-permute-start.21 = (bf16[32,1152]{1,0:T(8,128)(2,1)S(1)}, bf16[32,1152]{1,0:T(8,128)(2,1)S(1)}, u32[]{:S(2)}, u32[]{:S(2)}) collective-permute-start(bf16[32,1152]{1,0:T(8,128)(2,1)S(1)} %get-tuple-element.25), channel_id=1, source_target_pairs={{0,12},{1,13},{2,14},{3,15},{4,0},{5,1},{6,2},{7,3},{8,4},{9,5},{1... | collective-permute-start | bytes 221192 | tf_op jit(solution)/shard_map/ppermute | solution.py:64
  87.2 5.9 %collective-permute-start.22 = (bf16[32,1152]{1,0:T(8,128)(2,1)S(1)}, bf16[32,1152]{1,0:T(8,128)(2,1)S(1)}, u32[]{:S(2)}, u32[]{:S(2)}) collective-permute-start(bf16[32,1152]{1,0:T(8,128)(2,1)S(1)} %get-tuple-element.27), channel_id=1, source_target_pairs={{0,8},{1,9},{2,10},{3,11},{4,12},{5,13},{6,14},{7,15},{8,0},{9,1},... | collective-permute-start | bytes 221192 | tf_op jit(solution)/shard_map/ppermute | solution.py:64
  87.8 6.1 %collective-permute-start.23 = (bf16[32,1152]{1,0:T(8,128)(2,1)S(1)}, bf16[32,1152]{1,0:T(8,128)(2,1)S(1)}, u32[]{:S(2)}, u32[]{:S(2)}) collective-permute-start(bf16[32,1152]{1,0:T(8,128)(2,1)S(1)} %get-tuple-element.26), channel_id=1, source_target_pairs={{0,4},{1,5},{2,6},{3,7},{4,8},{5,9},{6,10},{7,11},{8,12},{9,13},{1... | collective-permute-start | bytes 221192 | tf_op jit(solution)/shard_map/ppermute | solution.py:64

commit v5 on v4

--- a/solution.py
+++ b/solution.py
@@ -90,9 +90,11 @@
     got_a, got_b = gather_second(inner_a, inner_b, nz, ny)
     bucket_hot = clip_bucket[:, None] == jnp.arange(n_buckets, dtype=jnp.int32)[None, :]
     owner = jnp.sum(jnp.where(bucket_hot, bucket_owner[None, :], 0), axis=1)
-    onehot = (owner[:, None] == jnp.arange(groups, dtype=jnp.int32)[None, :]).astype(jnp.int32)
-    before = jnp.cumsum(onehot, axis=0) - onehot
-    rank = jnp.sum(before * onehot, axis=1)
+    onehot = (owner[:, None] == jnp.arange(groups, dtype=jnp.int32)[None, :]).astype(clips.dtype)
+    local = jnp.arange(clip_rows, dtype=jnp.int32)
+    earlier = (local[:, None] > local[None, :]).astype(clips.dtype)
+    before = jnp.dot(earlier, onehot, preferred_element_type=jnp.float32)
+    rank = jnp.sum(before * onehot.astype(jnp.float32), axis=1).astype(jnp.int32)
     position = owner * capacity + rank
     meta = jnp.stack(
         [clip_bucket + 1, clip_positive // 128, clip_positive % 128], axis=1
@@ -101,7 +103,7 @@
                              jnp.zeros((clip_rows, 124), clips.dtype)], axis=1)
     placer = (position[:, None] == jnp.arange(slots, dtype=jnp.int32)[None, :]).astype(clips.dtype)
     send_rows = lax.dot_general(
-        placer, jnp.concatenate([clips, extra], axis=1), (((0,), (0,)), ((), ())),
+        placer, jnp.pad(clips, ((0, 0), (0, 128))) + jnp.pad(extra, ((0, 0), (width, 0))), (((0,), (0,)), ((), ())),
         preferred_element_type=jnp.float32,
     ).astype(clips.dtype)
     recv_ext = lax.all_to_all(send_rows, "grp", split_axis=0, concat_axis=0, tiled=True)

time: 96.9 us -> 97.2 us (level)
  starting transfers between devices: 36.6 us -> 40.3 us
  waiting for transfers between devices: 31.3 us -> 28.7 us
    ppermute x3, waiting for transfers between devices: 4.49 us -> 1.77 us  [reduce_pair(): lax.ppermute(blocks_a[d].astype(low), 'mem', shift_pairs(nz, ny, -d, False))]
    ppermute x3, starting transfers between devices: 0.64 us -> 2.1 us  [reduce_pair(): lax.ppermute(blocks_b[d].astype(low), 'mem', shift_pairs(nz, ny, -d, True))]
    ppermute x3, starting transfers between devices: 2.59 us -> 3.86 us  [reduce_pair(): lax.ppermute(total_a[d].astype(low), 'mem', shift_pairs(nz, ny, -d, True))]
    ppermute x3, starting transfers between devices: 1.54 us -> 2.54 us  [gather_second(): parts_a.append(lax.ppermute(inner_a, 'mem', shift_pairs(nz, ny, d, False)))]
    another operation x6 -> x4, other arithmetic: 3.21 us -> 2.59 us
    dot_general x1 -> x2, matrix products: 1.8 us -> 1.98 us  [the longest x1 1.79 us: inner_body(): lax.dot_general(placer, jnp.pad(clips, ((0, 0), (0, 128))) + jnp.pad(extr...]
  transfers between devices with their start and end apart: 26 -> 26, of which waited for: 9 -> 7; matrix products, arithmetic and copies ran while one was open for 19% -> 18% of each run, Pallas kernels for 0% -> 0%
where the time goes in v5:
time: 97.2 us; the launch traced here: 96.4 us
  starting transfers between devices  40.3 us (41%)
  waiting for transfers between devices  28.7 us (30%)
  other arithmetic  10.5 us (11%)
  matrix products  10.4 us (11%)
  local copies, waits for them, and re-layouts  4.23 us (4%)
  between operations  2.17 us (2%)
    ppermute x3, waiting for transfers between devices, gather_second(): parts_b.append(lax.ppermute(inner_b, 'mem', shift_pairs(nz, ny, d, True)))  11.3 us
    ppermute x3, starting transfers between devices, gather_first(): parts_b.append(lax.ppermute(xb, 'mem', shift_pairs(nz, ny, d, False)))  6.51 us
    ppermute x3, waiting for transfers between devices, gather_second(): parts_a.append(lax.ppermute(inner_a, 'mem', shift_pairs(nz, ny, d, False)))  6.44 us
    ppermute x3, starting transfers between devices, gather_first(): parts_a.append(lax.ppermute(xa, 'mem', shift_pairs(nz, ny, d, True)))  5.98 us
    ppermute x3, waiting for transfers between devices, reduce_pair(): lax.ppermute(total_b[d].astype(low), 'mem', shift_pairs(nz, ny, -d, False))  5.24 us
    ppermute x3, starting transfers between devices, reduce_pair(): lax.ppermute(total_b[d].astype(low), 'mem', shift_pairs(nz, ny, -d, False))  4.57 us
    all_to_all x1, starting transfers between devices, inner_body(): lax.all_to_all(send_rows, 'grp', split_axis=0, concat_axis=0, tiled=True)  4.3 us
    another operation x4, other arithmetic, gather_second(): return (jnp.stack(parts_a), jnp.stack(parts_b))  4.21 us
  transfers between devices with their start and end apart: 26, of which 7 were waited for; matrix products, arithmetic and copies ran while one was open for 18% of the time, Pallas kernels for 0%

profile of v5, /device:TPU:0, one launch (start us, length us, event | category | flops | bytes accessed | tf_op | source)
XLA Modules:
  0.0 96.4 jit_solution(1960467632578692365)
XLA Ops:
  0.6 1.0 %slice_bitcast_fusion.8 = (bf16[1,32,1152]{2,1,0:T(8,128)(2,1)S(1)}, bf16[32,1152]{1,0:T(8,128)(2,1)S(1)}, bf16[32,1152]{1,0:T(8,128)(2,1)S(1)}) fusion(bf16[64,1152]{1,0:T(8,128)(2,1)} %param.9), kind=kLoop, calls=%fused_computation.95 | loop fusion | bytes 368640 | tf_op jit(solution)/shard_map/stack | solution.py:41
  1.6 0.7 convert_element_type.153
  2.3 0.1 reshape.258
  2.4 0.1 copy.25
  2.5 0.1 concatenate.11
  2.6 1.7 %collective-permute-start = (bf16[32,1280]{1,0:T(8,128)(2,1)S(1)}, bf16[32,1280]{1,0:T(8,128)(2,1)S(1)}, u32[]{:S(2)}, u32[]{:S(2)}) collective-permute-start(bf16[32,1280]{1,0:T(8,128)(2,1)S(1)} %concatenate.11), channel_id=1, source_target_pairs={{0,1},{1,2},{2,3},{3,0},{4,5},{5,6},{6,7},{7,4},{8,9},{9,10},{10,1... | collective-permute-start | bytes 245768 | tf_op jit(solution)/shard_map/ppermute | solution.py:39
  4.3 2.9 %collective-permute-start.1 = (bf16[32,1280]{1,0:T(8,128)(2,1)S(1)}, bf16[32,1280]{1,0:T(8,128)(2,1)S(1)}, u32[]{:S(2)}, u32[]{:S(2)}) collective-permute-start(bf16[32,1280]{1,0:T(8,128)(2,1)S(1)} %concatenate.11), channel_id=1, source_target_pairs={{0,2},{1,3},{2,0},{3,1},{4,6},{5,7},{6,4},{7,5},{8,10},{9,11},{10,... | collective-permute-start | bytes 245768 | tf_op jit(solution)/shard_map/ppermute | solution.py:39
  7.2 1.9 %collective-permute-start.6 = (bf16[32,1152]{1,0:T(8,128)(2,1)S(1)}, bf16[32,1152]{1,0:T(8,128)(2,1)S(1)}, u32[]{:S(2)}, u32[]{:S(2)}) collective-permute-start(bf16[32,1152]{1,0:T(8,128)(2,1)S(1)} %get-tuple-element.31), channel_id=1, source_target_pairs={{0,4},{1,5},{2,6},{3,7},{4,8},{5,9},{6,10},{7,11},{8,12},{9,13},{1... | collective-permute-start | bytes 221192 | tf_op jit(solution)/shard_map/ppermute | solution.py:40
  9.1 3.6 %collective-permute-start.7 = (bf16[32,1152]{1,0:T(8,128)(2,1)S(1)}, bf16[32,1152]{1,0:T(8,128)(2,1)S(1)}, u32[]{:S(2)}, u32[]{:S(2)}) collective-permute-start(bf16[32,1152]{1,0:T(8,128)(2,1)S(1)} %get-tuple-element.31), channel_id=1, source_target_pairs={{0,8},{1,9},{2,10},{3,11},{4,12},{5,13},{6,14},{7,15},{8,0},{9,1},... | collective-permute-start | bytes 221192 | tf_op jit(solution)/shard_map/ppermute | solution.py:40
  12.7 1.0 %collective-permute-start.8 = (bf16[32,1152]{1,0:T(8,128)(2,1)S(1)}, bf16[32,1152]{1,0:T(8,128)(2,1)S(1)}, u32[]{:S(2)}, u32[]{:S(2)}) collective-permute-start(bf16[32,1152]{1,0:T(8,128)(2,1)S(1)} %get-tuple-element.31), channel_id=1, source_target_pairs={{0,12},{1,13},{2,14},{3,15},{4,0},{5,1},{6,2},{7,3},{8,4},{9,5},{1... | collective-permute-start | bytes 221192 | tf_op jit(solution)/shard_map/ppermute | solution.py:40
  13.7 0.7 add_convert_fusion
  14.4 0.8 select_reduce_fusion
  15.2 0.2 fusion.18
  15.4 0.7 fusion.39
  16.1 0.1 stack.98
  16.2 0.1 stack.99
  16.3 0.1 stack.97
  16.4 0.2 concatenate.10
  16.6 1.8 %convolution_convert_fusion = bf16[512,1280]{1,0:T(8,128)(2,1)} fusion(bf16[256,128]{1,0:T(8,128)(2,1)S(1)} %concatenate.10, bf16[256,1152]{1,0:T(8,128)(2,1)S(1)} %copy-done.1, s32[256]{0:T(256)S(1)} %convert_add_fusion.2), kind=kOutput, calls=%fused_computation.1 | convolution fusion | flops 337641472 | bytes 1967104 | tf_op jit(solution)/shard_map/dot_general | solution.py:105
  18.4 4.3 %all-to-all-start = ((bf16[8,64,1280]{2,1,0:T(8,128)(2,1)}), bf16[8,64,1280]{2,1,0:T(8,128)(2,1)S(1)}, u32[]{:S(2)}, u32[]{:S(2)}) async-start(bf16[8,64,1280]{2,1,0:T(8,128)(2,1)} %bitcast), calls=%async_computation | async-start | bytes 2621440 | tf_op jit(solution)/shard_map/all_to_all | solution.py:109
  22.8 1.4 %collective-permute-start.2 = (bf16[32,1280]{1,0:T(8,128)(2,1)S(1)}, bf16[32,1280]{1,0:T(8,128)(2,1)S(1)}, u32[]{:S(2)}, u32[]{:S(2)}) collective-permute-start(bf16[32,1280]{1,0:T(8,128)(2,1)S(1)} %concatenate.11), channel_id=1, source_target_pairs={{0,3},{1,0},{2,1},{3,2},{4,7},{5,4},{6,5},{7,6},{8,11},{9,8},{10,9... | collective-permute-start | bytes 245768 | tf_op jit(solution)/shard_map/ppermute | solution.py:39
  24.2 0.8 fusion.45
  24.9 0.7 collective-permute-start.9
  25.7 0.8 collective-permute-start.10
  26.5 1.9 %collective-permute-start.11 = (bf16[4,32,1152]{2,1,0:T(8,128)(2,1)}, bf16[4,32,1152]{2,1,0:T(8,128)(2,1)}, u32[]{:S(2)}, u32[]{:S(2)}) collective-permute-start(bf16[4,32,1152]{2,1,0:T(8,128)(2,1)} %get-tuple-element.29), channel_id=1, source_target_pairs={{0,3},{1,0},{2,1},{3,2},{4,7},{5,4},{6,5},{7,6},{8,11},{9,8},{10,9... | collective-permute-start | bytes 884744 | tf_op jit(solution)/shard_map/ppermute | solution.py:49
  28.5 2.0 %collective-permute-start.3 = (bf16[4,32,1280]{2,1,0:T(8,128)(2,1)S(1)}, bf16[4,32,1280]{2,1,0:T(8,128)(2,1)}, u32[]{:S(2)}, u32[]{:S(2)}) collective-permute-start(bf16[4,32,1280]{2,1,0:T(8,128)(2,1)S(1)} %get-tuple-element.21), channel_id=1, source_target_pairs={{0,4},{1,5},{2,6},{3,7},{4,8},{5,9},{6,10},{7,11},{8,12},{9,13},{1... | collective-permute-start | bytes 983048 | tf_op jit(solution)/shard_map/ppermute | solution.py:48
  30.6 11.3 %collective-permute-done.9 = bf16[4,32,1152]{2,1,0:T(8,128)(2,1)S(1)} collective-permute-done((bf16[4,32,1152]{2,1,0:T(8,128)(2,1)}, bf16[4,32,1152]{2,1,0:T(8,128)(2,1)S(1)}, u32[]{:S(2)}, u32[]{:S(2)}) %collective-permute-start.9) | collective-permute-done | bytes 294944 | tf_op jit(solution)/shard_map/ppermute | solution.py:49
  41.8 0.5 collective-permute-start.4
  43.8 2.2 %pad_maximum_fusion.1 = bf16[4,4,32,1152]{3,2,1,0:T(8,128)(2,1)} fusion(bf16[1,4,32,1152]{3,2,1,0:T(8,128)(2,1)} %bitcast.22, bf16[1,4,32,1152]{3,2,1,0:T(8,128)(2,1)S(1)} %bitcast.92, bf16[1,4,32,1152]{3,2,1,0:T(8,128)(2,1)S(1)} %bitcast.91, bf16[1,4,32,1152]{3,2,1,0:T(8,128)(2,1)S(1)} %get-tuple-element.28), kind=kLoop, calls=%fused_computation.23 | loop fusion | flops 1769472 | bytes 2359296 | tf_op jit(solution)/shard_map/stack | solution.py:50
  46.0 6.4 %collective-permute-done.4 = bf16[4,32,1280]{2,1,0:T(8,128)(2,1)} collective-permute-done((bf16[4,32,1280]{2,1,0:T(8,128)(2,1)S(1)}, bf16[4,32,1280]{2,1,0:T(8,128)(2,1)}, u32[]{:S(2)}, u32[]{:S(2)}) %collective-permute-start.4) | collective-permute-done | bytes 327712 | tf_op jit(solution)/shard_map/ppermute | solution.py:48
  52.4 1.2 %pad_maximum_fusion = bf16[4,4,32,1280]{3,2,1,0:T(8,128)(2,1)S(1)} fusion(bf16[1,4,32,1280]{3,2,1,0:T(8,128)(2,1)S(1)} %bitcast.89, bf16[1,4,32,1280]{3,2,1,0:T(8,128)(2,1)} %bitcast.9, bf16[1,4,32,1280]{3,2,1,0:T(8,128)(2,1)} %bitcast.8, bf16[1,4,32,1280]{3,2,1,0:T(8,128)(2,1)S(1)} %get-tuple-element.20), kind=kLoop, calls=%fused_computation.18 | loop fusion | flops 1966080 | bytes 2621440 | tf_op jit(solution)/shard_map/stack | solution.py:50
  53.7 0.7 convert_reduce_fusion
  54.4 0.1 reshape.261
  54.5 0.1 reshape.262
  54.6 0.1 slice_convert_fusion
  54.7 0.4 fusion.30
  55.1 1.2 %fusion.17 = bf16[512,512]{1,0:T(8,128)(2,1)S(1)} fusion(bf16[512,1280]{1,0:T(8,128)(2,1)S(1)} %bitcast.82, f32[]{:T(128)} %bitcast.75, f32[]{:T(128)} %bitcast.73, s32[512]{0:T(512)S(1)} %add.249, s32[512]{0:T(512)S(1)} %reshape.261, s32[512]{0:T(512)S(1)} %get-tuple-element.9, s32[512]{0:T(512)S(1)} %get-tuple-element.8, bf16[512,1280]{1,0:T(8,128)(2,1)S(1)} %bitcast.78), kind=kOutput, calls=%fused_computation.22 | convolution fusion | flops 607387648 | bytes 2891784 | tf_op jit(solution)/shard_map/dot_general | solution.py:13
  56.3 0.9 fusion.56
  57.2 0.8 fusion.19
  58.0 0.1 slice.129
  58.1 1.0 fusion.53
  59.1 0.4 collective-permute-start.12
  59.5 2.6 %collective-permute-start.13 = (bf16[4,32,1152]{2,1,0:T(8,128)(2,1)}, bf16[4,32,1152]{2,1,0:T(8,128)(2,1)S(1)}, u32[]{:S(2)}, u32[]{:S(2)}) collective-permute-start(bf16[4,32,1152]{2,1,0:T(8,128)(2,1)} %bitcast.28), channel_id=1, source_target_pairs={{0,8},{1,9},{2,10},{3,11},{4,12},{5,13},{6,14},{7,15},{8,0},{9,1},... | collective-permute-start | bytes 884744 | tf_op jit(solution)/shard_map/ppermute | solution.py:58
  62.2 1.2 %fusion.15 = bf16[512,512]{1,0:T(8,128)(2,1)S(1)} fusion(bf16[512,1152]{1,0:T(8,128)(2,1)S(1)} %bitcast.84, s32[512]{0:T(512)S(1)} %add.261, s32[512]{0:T(512)S(1)} %reshape.262, f32[]{:T(128)} %bitcast.76, f32[]{:T(128)} %bitcast.74, s32[512]{0:T(512)S(1)} %get-tuple-element.9, s32[512]{0:T(512)S(1)} %get-tuple-element.8, bf16[512,1280]{1,0:T(8,128)(2,1)S(1)} %bitcast.81), kind=kOutput, calls=%fused_computation.20 | convolution fusion | flops 607387648 | bytes 2891784 | tf_op jit(solution)/shard_map/dot_general | solution.py:13
  63.5 1.9 %convolution_add_fusion = bf16[512,1152]{1,0:T(8,128)(2,1)} fusion(f32[512,1152]{1,0:T(8,128)S(1)} %fusion.19, bf16[512,512]{1,0:T(8,128)(2,1)S(1)} %fusion.15, bf16[512,1152]{1,0:T(8,128)(2,1)S(1)} %bitcast.85), kind=kOutput, calls=%fused_computation | convolution fusion | flops 605159424 | bytes 5242880 | tf_op jit(solution)/shard_map/dot_general | solution.py:136
  65.3 0.9 fusion.55
  66.2 0.9 fusion.54
  67.2 4.0 %all-to-all-start.1 = ((bf16[8,64,1152]{2,1,0:T(8,128)(2,1)}), bf16[8,64,1152]{2,1,0:T(8,128)(2,1)S(1)}, u32[]{:S(2)}, u32[]{:S(2)}) async-start(bf16[8,64,1152]{2,1,0:T(8,128)(2,1)} %bitcast.24), calls=%async_computation.1 | async-start | bytes 2359296 | tf_op jit(solution)/shard_map/all_to_all | solution.py:137
  71.2 2.1 %collective-permute-start.20 = (bf16[4,32,1152]{2,1,0:T(8,128)(2,1)}, bf16[4,32,1152]{2,1,0:T(8,128)(2,1)S(1)}, u32[]{:S(2)}, u32[]{:S(2)}) collective-permute-start(bf16[4,32,1152]{2,1,0:T(8,128)(2,1)} %bitcast.93), channel_id=1, source_target_pairs={{0,1},{1,2},{2,3},{3,0},{4,5},{5,6},{6,7},{7,4},{8,9},{9,10},{10,1... | collective-permute-start | bytes 884744 | tf_op jit(solution)/shard_map/ppermute | solution.py:59
  73.3 1.8 %collective-permute-done.14 = bf16[4,32,1152]{2,1,0:T(8,128)(2,1)} collective-permute-done((bf16[4,32,1152]{2,1,0:T(8,128)(2,1)}, bf16[4,32,1152]{2,1,0:T(8,128)(2,1)}, u32[]{:S(2)}, u32[]{:S(2)}) %collective-permute-start.14) | collective-permute-done | bytes 294944 | tf_op jit(solution)/shard_map/ppermute | solution.py:58
  75.1 1.1 %fusion.51 = (bf16[4,32,1152]{2,1,0:T(8,128)(2,1)S(1)}, f32[4,32,1152]{2,1,0:T(8,128)S(1)}) fusion(bf16[4,32,1152]{2,1,0:T(8,128)(2,1)} %collective-permute-done.14, bf16[4,32,1152]{2,1,0:T(8,128)(2,1)S(1)} %collective-permute-done.13, f32[4,32,1152]{2,1,0:T(8,128)S(1)} %bitcast.88, bf16[4,32,1152]{2,1,0:T(8,128)(2,1)S(1)} %collective-permute-done.12), kind=kLoop, calls=%fused_computation.102 | loop fusion | flops 1032192 | bytes 2359296 | tf_op jit(solution)/shard_map/convert.12
  76.2 1.0 %collective-permute-start.15 = (bf16[32,1152]{1,0:T(8,128)(2,1)S(1)}, bf16[32,1152]{1,0:T(8,128)(2,1)S(1)}, u32[]{:S(2)}, u32[]{:S(2)}) collective-permute-start(bf16[32,1152]{1,0:T(8,128)(2,1)S(1)} %get-tuple-element.22), channel_id=1, source_target_pairs={{0,3},{1,0},{2,1},{3,2},{4,7},{5,4},{6,5},{7,6},{8,11},{9,8},{10,9... | collective-permute-start | bytes 221192 | tf_op jit(solution)/shard_map/ppermute | solution.py:63
  77.2 1.5 %collective-permute-start.16 = (bf16[32,1152]{1,0:T(8,128)(2,1)S(1)}, bf16[32,1152]{1,0:T(8,128)(2,1)S(1)}, u32[]{:S(2)}, u32[]{:S(2)}) collective-permute-start(bf16[32,1152]{1,0:T(8,128)(2,1)S(1)} %get-tuple-element.24), channel_id=1, source_target_pairs={{0,2},{1,3},{2,0},{3,1},{4,6},{5,7},{6,4},{7,5},{8,10},{9,11},{10,... | collective-permute-start | bytes 221192 | tf_op jit(solution)/shard_map/ppermute | solution.py:63
  78.8 1.3 %collective-permute-start.17 = (bf16[32,1152]{1,0:T(8,128)(2,1)S(1)}, bf16[32,1152]{1,0:T(8,128)(2,1)S(1)}, u32[]{:S(2)}, u32[]{:S(2)}) collective-permute-start(bf16[32,1152]{1,0:T(8,128)(2,1)S(1)} %get-tuple-element.23), channel_id=1, source_target_pairs={{0,1},{1,2},{2,3},{3,0},{4,5},{5,6},{6,7},{7,4},{8,9},{9,10},{10,1... | collective-permute-start | bytes 221192 | tf_op jit(solution)/shard_map/ppermute | solution.py:63
  80.1 4.0 %collective-permute-done.20 = bf16[4,32,1152]{2,1,0:T(8,128)(2,1)S(1)} collective-permute-done((bf16[4,32,1152]{2,1,0:T(8,128)(2,1)}, bf16[4,32,1152]{2,1,0:T(8,128)(2,1)S(1)}, u32[]{:S(2)}, u32[]{:S(2)}) %collective-permute-start.20) | collective-permute-done | bytes 294944 | tf_op jit(solution)/shard_map/ppermute | solution.py:59
  84.1 0.1 fusion.52
  84.2 3.3 %collective-permute-start.21 = (bf16[32,1152]{1,0:T(8,128)(2,1)S(1)}, bf16[32,1152]{1,0:T(8,128)(2,1)S(1)}, u32[]{:S(2)}, u32[]{:S(2)}) collective-permute-start(bf16[32,1152]{1,0:T(8,128)(2,1)S(1)} %get-tuple-element.25), channel_id=1, source_target_pairs={{0,12},{1,13},{2,14},{3,15},{4,0},{5,1},{6,2},{7,3},{8,4},{9,5},{1... | collective-permute-start | bytes 221192 | tf_op jit(solution)/shard_map/ppermute | solution.py:64
  87.5 0.2 collective-permute-start.22
  87.7 1.1 %collective-permute-start.23 = (bf16[32,1152]{1,0:T(8,128)(2,1)S(1)}, bf16[32,1152]{1,0:T(8,128)(2,1)S(1)}, u32[]{:S(2)}, u32[]{:S(2)}) collective-permute-start(bf16[32,1152]{1,0:T(8,128)(2,1)S(1)} %get-tuple-element.26), channel_id=1, source_target_pairs={{0,4},{1,5},{2,6},{3,7},{4,8},{5,9},{6,10},{7,11},{8,12},{9,13},{1... | collective-permute-start | bytes 221192 | tf_op jit(solution)/shard_map/ppermute | solution.py:64
  88.9 1.6 %collective-permute-done.21 = bf16[32,1152]{1,0:T(8,128)(2,1)S(1)} collective-permute-done((bf16[32,1152]{1,0:T(8,128)(2,1)S(1)}, bf16[32,1152]{1,0:T(8,128)(2,1)S(1)}, u32[]{:S(2)}, u32[]{:S(2)}) %collective-permute-start.21) | collective-permute-done | bytes 73760 | tf_op jit(solution)/shard_map/ppermute | solution.py:64
  90.4 3.0 %collective-permute-done.22 = bf16[32,1152]{1,0:T(8,128)(2,1)S(1)} collective-permute-done((bf16[32,1152]{1,0:T(8,128)(2,1)S(1)}, bf16[32,1152]{1,0:T(8,128)(2,1)S(1)}, u32[]{:S(2)}, u32[]{:S(2)}) %collective-permute-start.22) | collective-permute-done | bytes 73760 | tf_op jit(solution)/shard_map/ppermute | solution.py:64
  93.4 0.7 collective-permute-done.23
  94.1 0.7 pad_maximum_fusion.4
  94.9 1.6 %fusion.25 = f32[256,1152]{1,0:T(8,128)} fusion(bf16[512,1152]{1,0:T(8,128)(2,1)S(1)} %bitcast.86, s32[256]{0:T(256)S(1)} %convert_add_fusion.2), kind=kOutput, calls=%fused_computation.35 | convolution fusion | flops 302120960 | bytes 2360320 | tf_op jit(solution)/shard_map/dot_general | solution.py:138
  (45 shorter events, 0.8 us)
Async XLA Ops:
  0.6 16.0 %copy-start.1 = (bf16[256,1152]{1,0:T(8,128)(2,1)S(1)}, bf16[256,1152]{1,0:T(8,128)(2,1)}, u32[]{:S(2)}) copy-start(bf16[256,1152]{1,0:T(8,128)(2,1)} %param.8) | copy-start | bytes 1769476
  2.6 23.9 %collective-permute-start = (bf16[32,1280]{1,0:T(8,128)(2,1)S(1)}, bf16[32,1280]{1,0:T(8,128)(2,1)S(1)}, u32[]{:S(2)}, u32[]{:S(2)}) collective-permute-start(bf16[32,1280]{1,0:T(8,128)(2,1)S(1)} %concatenate.11), channel_id=1, source_target_pairs={{0,1},{1,2},{2,3},{3,0},{4,5},{5,6},{6,7},{7,4},{8,9},{9,10},{10,1... | collective-permute-start | bytes 245768 | tf_op jit(solution)/shard_map/ppermute | solution.py:39
  4.3 24.1 %collective-permute-start.1 = (bf16[32,1280]{1,0:T(8,128)(2,1)S(1)}, bf16[32,1280]{1,0:T(8,128)(2,1)S(1)}, u32[]{:S(2)}, u32[]{:S(2)}) collective-permute-start(bf16[32,1280]{1,0:T(8,128)(2,1)S(1)} %concatenate.11), channel_id=1, source_target_pairs={{0,2},{1,3},{2,0},{3,1},{4,6},{5,7},{6,4},{7,5},{8,10},{9,11},{10,... | collective-permute-start | bytes 245768 | tf_op jit(solution)/shard_map/ppermute | solution.py:39
  7.2 15.6 %collective-permute-start.6 = (bf16[32,1152]{1,0:T(8,128)(2,1)S(1)}, bf16[32,1152]{1,0:T(8,128)(2,1)S(1)}, u32[]{:S(2)}, u32[]{:S(2)}) collective-permute-start(bf16[32,1152]{1,0:T(8,128)(2,1)S(1)} %get-tuple-element.31), channel_id=1, source_target_pairs={{0,4},{1,5},{2,6},{3,7},{4,8},{5,9},{6,10},{7,11},{8,12},{9,13},{1... | collective-permute-start | bytes 221192 | tf_op jit(solution)/shard_map/ppermute | solution.py:40
  9.1 15.1 %collective-permute-start.7 = (bf16[32,1152]{1,0:T(8,128)(2,1)S(1)}, bf16[32,1152]{1,0:T(8,128)(2,1)S(1)}, u32[]{:S(2)}, u32[]{:S(2)}) collective-permute-start(bf16[32,1152]{1,0:T(8,128)(2,1)S(1)} %get-tuple-element.31), channel_id=1, source_target_pairs={{0,8},{1,9},{2,10},{3,11},{4,12},{5,13},{6,14},{7,15},{8,0},{9,1},... | collective-permute-start | bytes 221192 | tf_op jit(solution)/shard_map/ppermute | solution.py:40
  12.7 11.5 %collective-permute-start.8 = (bf16[32,1152]{1,0:T(8,128)(2,1)S(1)}, bf16[32,1152]{1,0:T(8,128)(2,1)S(1)}, u32[]{:S(2)}, u32[]{:S(2)}) collective-permute-start(bf16[32,1152]{1,0:T(8,128)(2,1)S(1)} %get-tuple-element.31), channel_id=1, source_target_pairs={{0,12},{1,13},{2,14},{3,15},{4,0},{5,1},{6,2},{7,3},{8,4},{9,5},{1... | collective-permute-start | bytes 221192 | tf_op jit(solution)/shard_map/ppermute | solution.py:40
  18.4 36.2 %all-to-all-start = ((bf16[8,64,1280]{2,1,0:T(8,128)(2,1)}), bf16[8,64,1280]{2,1,0:T(8,128)(2,1)S(1)}, u32[]{:S(2)}, u32[]{:S(2)}) async-start(bf16[8,64,1280]{2,1,0:T(8,128)(2,1)} %bitcast), calls=%async_computation | async-start | bytes 2621440 | tf_op jit(solution)/shard_map/all_to_all | solution.py:109
  22.8 5.6 %collective-permute-start.2 = (bf16[32,1280]{1,0:T(8,128)(2,1)S(1)}, bf16[32,1280]{1,0:T(8,128)(2,1)S(1)}, u32[]{:S(2)}, u32[]{:S(2)}) collective-permute-start(bf16[32,1280]{1,0:T(8,128)(2,1)S(1)} %concatenate.11), channel_id=1, source_target_pairs={{0,3},{1,0},{2,1},{3,2},{4,7},{5,4},{6,5},{7,6},{8,11},{9,8},{10,9... | collective-permute-start | bytes 245768 | tf_op jit(solution)/shard_map/ppermute | solution.py:39
  24.9 16.9 %collective-permute-start.9 = (bf16[4,32,1152]{2,1,0:T(8,128)(2,1)}, bf16[4,32,1152]{2,1,0:T(8,128)(2,1)S(1)}, u32[]{:S(2)}, u32[]{:S(2)}) collective-permute-start(bf16[4,32,1152]{2,1,0:T(8,128)(2,1)} %get-tuple-element.29), channel_id=1, source_target_pairs={{0,1},{1,2},{2,3},{3,0},{4,5},{5,6},{6,7},{7,4},{8,9},{9,10},{10,1... | collective-permute-start | bytes 884744 | tf_op jit(solution)/shard_map/ppermute | solution.py:49
  25.7 18.1 %collective-permute-start.10 = (bf16[4,32,1152]{2,1,0:T(8,128)(2,1)}, bf16[4,32,1152]{2,1,0:T(8,128)(2,1)S(1)}, u32[]{:S(2)}, u32[]{:S(2)}) collective-permute-start(bf16[4,32,1152]{2,1,0:T(8,128)(2,1)} %get-tuple-element.29), channel_id=1, source_target_pairs={{0,2},{1,3},{2,0},{3,1},{4,6},{5,7},{6,4},{7,5},{8,10},{9,11},{10,... | collective-permute-start | bytes 884744 | tf_op jit(solution)/shard_map/ppermute | solution.py:49
  26.5 17.3 %collective-permute-start.11 = (bf16[4,32,1152]{2,1,0:T(8,128)(2,1)}, bf16[4,32,1152]{2,1,0:T(8,128)(2,1)}, u32[]{:S(2)}, u32[]{:S(2)}) collective-permute-start(bf16[4,32,1152]{2,1,0:T(8,128)(2,1)} %get-tuple-element.29), channel_id=1, source_target_pairs={{0,3},{1,0},{2,1},{3,2},{4,7},{5,4},{6,5},{7,6},{8,11},{9,8},{10,9... | collective-permute-start | bytes 884744 | tf_op jit(solution)/shard_map/ppermute | solution.py:49
  28.5 17.5 %collective-permute-start.5 = (bf16[4,32,1280]{2,1,0:T(8,128)(2,1)S(1)}, bf16[4,32,1280]{2,1,0:T(8,128)(2,1)S(1)}, u32[]{:S(2)}, u32[]{:S(2)}) collective-permute-start(bf16[4,32,1280]{2,1,0:T(8,128)(2,1)S(1)} %get-tuple-element.21), channel_id=1, source_target_pairs={{0,12},{1,13},{2,14},{3,15},{4,0},{5,1},{6,2},{7,3},{8,4},{9,5},{1... | collective-permute-start | bytes 983048 | tf_op jit(solution)/shard_map/ppermute | solution.py:48
  28.5 17.4 %collective-permute-start.3 = (bf16[4,32,1280]{2,1,0:T(8,128)(2,1)S(1)}, bf16[4,32,1280]{2,1,0:T(8,128)(2,1)}, u32[]{:S(2)}, u32[]{:S(2)}) collective-permute-start(bf16[4,32,1280]{2,1,0:T(8,128)(2,1)S(1)} %get-tuple-element.21), channel_id=1, source_target_pairs={{0,4},{1,5},{2,6},{3,7},{4,8},{5,9},{6,10},{7,11},{8,12},{9,13},{1... | collective-permute-start | bytes 983048 | tf_op jit(solution)/shard_map/ppermute | solution.py:48
  41.8 10.6 %collective-permute-start.4 = (bf16[4,32,1280]{2,1,0:T(8,128)(2,1)S(1)}, bf16[4,32,1280]{2,1,0:T(8,128)(2,1)}, u32[]{:S(2)}, u32[]{:S(2)}) collective-permute-start(bf16[4,32,1280]{2,1,0:T(8,128)(2,1)S(1)} %get-tuple-element.21), channel_id=1, source_target_pairs={{0,8},{1,9},{2,10},{3,11},{4,12},{5,13},{6,14},{7,15},{8,0},{9,1},... | collective-permute-start | bytes 983048 | tf_op jit(solution)/shard_map/ppermute | solution.py:48
  58.1 4.1 %copy-start = (bf16[4,4,32,1152]{3,2,1,0:T(8,128)(2,1)S(1)}, bf16[4,4,32,1152]{3,2,1,0:T(8,128)(2,1)}, u32[]{:S(2)}) copy-start(bf16[4,4,32,1152]{3,2,1,0:T(8,128)(2,1)} %pad_maximum_fusion.1) | copy-start | bytes 3538948
  59.1 12.1 %collective-permute-start.12 = (bf16[4,32,1152]{2,1,0:T(8,128)(2,1)}, bf16[4,32,1152]{2,1,0:T(8,128)(2,1)S(1)}, u32[]{:S(2)}, u32[]{:S(2)}) collective-permute-start(bf16[4,32,1152]{2,1,0:T(8,128)(2,1)} %bitcast.27), channel_id=1, source_target_pairs={{0,12},{1,13},{2,14},{3,15},{4,0},{5,1},{6,2},{7,3},{8,4},{9,5},{1... | collective-permute-start | bytes 884744 | tf_op jit(solution)/shard_map/ppermute | solution.py:58
  59.5 13.8 %collective-permute-start.13 = (bf16[4,32,1152]{2,1,0:T(8,128)(2,1)}, bf16[4,32,1152]{2,1,0:T(8,128)(2,1)S(1)}, u32[]{:S(2)}, u32[]{:S(2)}) collective-permute-start(bf16[4,32,1152]{2,1,0:T(8,128)(2,1)} %bitcast.28), channel_id=1, source_target_pairs={{0,8},{1,9},{2,10},{3,11},{4,12},{5,13},{6,14},{7,15},{8,0},{9,1},... | collective-permute-start | bytes 884744 | tf_op jit(solution)/shard_map/ppermute | solution.py:58
  62.2 12.9 %collective-permute-start.14 = (bf16[4,32,1152]{2,1,0:T(8,128)(2,1)}, bf16[4,32,1152]{2,1,0:T(8,128)(2,1)}, u32[]{:S(2)}, u32[]{:S(2)}) collective-permute-start(bf16[4,32,1152]{2,1,0:T(8,128)(2,1)} %bitcast.29), channel_id=1, source_target_pairs={{0,4},{1,5},{2,6},{3,7},{4,8},{5,9},{6,10},{7,11},{8,12},{9,13},{1... | collective-permute-start | bytes 884744 | tf_op jit(solution)/shard_map/ppermute | solution.py:58
  67.1 11.6 %collective-permute-start.18 = (bf16[4,32,1152]{2,1,0:T(8,128)(2,1)}, bf16[4,32,1152]{2,1,0:T(8,128)(2,1)S(1)}, u32[]{:S(2)}, u32[]{:S(2)}) collective-permute-start(bf16[4,32,1152]{2,1,0:T(8,128)(2,1)} %bitcast.35), channel_id=1, source_target_pairs={{0,3},{1,0},{2,1},{3,2},{4,7},{5,4},{6,5},{7,6},{8,11},{9,8},{10,9... | collective-permute-start | bytes 884744 | tf_op jit(solution)/shard_map/ppermute | solution.py:59
  67.1 12.9 %collective-permute-start.19 = (bf16[4,32,1152]{2,1,0:T(8,128)(2,1)}, bf16[4,32,1152]{2,1,0:T(8,128)(2,1)S(1)}, u32[]{:S(2)}, u32[]{:S(2)}) collective-permute-start(bf16[4,32,1152]{2,1,0:T(8,128)(2,1)} %bitcast.36), channel_id=1, source_target_pairs={{0,2},{1,3},{2,0},{3,1},{4,6},{5,7},{6,4},{7,5},{8,10},{9,11},{10,... | collective-permute-start | bytes 884744 | tf_op jit(solution)/shard_map/ppermute | solution.py:59
  67.2 27.7 %all-to-all-start.1 = ((bf16[8,64,1152]{2,1,0:T(8,128)(2,1)}), bf16[8,64,1152]{2,1,0:T(8,128)(2,1)S(1)}, u32[]{:S(2)}, u32[]{:S(2)}) async-start(bf16[8,64,1152]{2,1,0:T(8,128)(2,1)} %bitcast.24), calls=%async_computation.1 | async-start | bytes 2359296 | tf_op jit(solution)/shard_map/all_to_all | solution.py:137
  71.2 12.8 %collective-permute-start.20 = (bf16[4,32,1152]{2,1,0:T(8,128)(2,1)}, bf16[4,32,1152]{2,1,0:T(8,128)(2,1)S(1)}, u32[]{:S(2)}, u32[]{:S(2)}) collective-permute-start(bf16[4,32,1152]{2,1,0:T(8,128)(2,1)} %bitcast.93), channel_id=1, source_target_pairs={{0,1},{1,2},{2,3},{3,0},{4,5},{5,6},{6,7},{7,4},{8,9},{9,10},{10,1... | collective-permute-start | bytes 884744 | tf_op jit(solution)/shard_map/ppermute | solution.py:59
  76.2 11.5 %collective-permute-start.15 = (bf16[32,1152]{1,0:T(8,128)(2,1)S(1)}, bf16[32,1152]{1,0:T(8,128)(2,1)S(1)}, u32[]{:S(2)}, u32[]{:S(2)}) collective-permute-start(bf16[32,1152]{1,0:T(8,128)(2,1)S(1)} %get-tuple-element.22), channel_id=1, source_target_pairs={{0,3},{1,0},{2,1},{3,2},{4,7},{5,4},{6,5},{7,6},{8,11},{9,8},{10,9... | collective-permute-start | bytes 221192 | tf_op jit(solution)/shard_map/ppermute | solution.py:63
  77.2 11.6 %collective-permute-start.16 = (bf16[32,1152]{1,0:T(8,128)(2,1)S(1)}, bf16[32,1152]{1,0:T(8,128)(2,1)S(1)}, u32[]{:S(2)}, u32[]{:S(2)}) collective-permute-start(bf16[32,1152]{1,0:T(8,128)(2,1)S(1)} %get-tuple-element.24), channel_id=1, source_target_pairs={{0,2},{1,3},{2,0},{3,1},{4,6},{5,7},{6,4},{7,5},{8,10},{9,11},{10,... | collective-permute-start | bytes 221192 | tf_op jit(solution)/shard_map/ppermute | solution.py:63
  78.8 10.1 %collective-permute-start.17 = (bf16[32,1152]{1,0:T(8,128)(2,1)S(1)}, bf16[32,1152]{1,0:T(8,128)(2,1)S(1)}, u32[]{:S(2)}, u32[]{:S(2)}) collective-permute-start(bf16[32,1152]{1,0:T(8,128)(2,1)S(1)} %get-tuple-element.23), channel_id=1, source_target_pairs={{0,1},{1,2},{2,3},{3,0},{4,5},{5,6},{6,7},{7,4},{8,9},{9,10},{10,1... | collective-permute-start | bytes 221192 | tf_op jit(solution)/shard_map/ppermute | solution.py:63
  84.2 6.2 %collective-permute-start.21 = (bf16[32,1152]{1,0:T(8,128)(2,1)S(1)}, bf16[32,1152]{1,0:T(8,128)(2,1)S(1)}, u32[]{:S(2)}, u32[]{:S(2)}) collective-permute-start(bf16[32,1152]{1,0:T(8,128)(2,1)S(1)} %get-tuple-element.25), channel_id=1, source_target_pairs={{0,12},{1,13},{2,14},{3,15},{4,0},{5,1},{6,2},{7,3},{8,4},{9,5},{1... | collective-permute-start | bytes 221192 | tf_op jit(solution)/shard_map/ppermute | solution.py:64
  87.5 5.9 %collective-permute-start.22 = (bf16[32,1152]{1,0:T(8,128)(2,1)S(1)}, bf16[32,1152]{1,0:T(8,128)(2,1)S(1)}, u32[]{:S(2)}, u32[]{:S(2)}) collective-permute-start(bf16[32,1152]{1,0:T(8,128)(2,1)S(1)} %get-tuple-element.27), channel_id=1, source_target_pairs={{0,8},{1,9},{2,10},{3,11},{4,12},{5,13},{6,14},{7,15},{8,0},{9,1},... | collective-permute-start | bytes 221192 | tf_op jit(solution)/shard_map/ppermute | solution.py:64
  87.7 6.4 %collective-permute-start.23 = (bf16[32,1152]{1,0:T(8,128)(2,1)S(1)}, bf16[32,1152]{1,0:T(8,128)(2,1)S(1)}, u32[]{:S(2)}, u32[]{:S(2)}) collective-permute-start(bf16[32,1152]{1,0:T(8,128)(2,1)S(1)} %get-tuple-element.26), channel_id=1, source_target_pairs={{0,4},{1,5},{2,6},{3,7},{4,8},{5,9},{6,10},{7,11},{8,12},{9,13},{1... | collective-permute-start | bytes 221192 | tf_op jit(solution)/shard_map/ppermute | solution.py:64
